TPU v7x, 768 devices: a whole 4x8x12 slice. The times are simulated.
768 devices in a mesh: section: 12 (over z), tensor: 64 (over x, y, core).
Axes of the slice: x: 4, y: 8, z: 12, core: 2. Of those that a mesh axis runs over, the one named last changes fastest.
Arguments:
- hidden: bfloat16 [192, 8192], P('section'), may hold values from -600 to 600
- norm_gain: bfloat16 [8192], replicated, may hold values from 0.5 to 1.5
- targets: int32 [192], replicated, may hold values from 0 to 98303
- out_weight: bfloat16 [8192, 98304], P(None, ('section', 'tensor')), may hold values from -1 to 1
Outputs:
- token_loss: float32 [192], replicated
- grad_normed: bfloat16 [192, 8192], P('section', 'tensor')
- grad_weight: bfloat16 [8192, 98304], P(None, ('section', 'tensor'))
- normed_rows: bfloat16 [192, 8192], P('section', 'tensor')
All inputs are finite; a program needn't handle non-finite values.
Results may differ from a plain program's by a relative error of at most 0.0073.
Values may be sent and summed in bfloat16 or wider, within the bound.
No kernel may reach another device: no remote copies, remote signals or barrier semaphores. Data moves between devices by JAX's collectives and lax.ppermute only.
A program may use at most 32 MiB of HBM per device.

v0:
```python
import jax
import jax.numpy as jnp
from jax import lax
from jax.sharding import PartitionSpec as P


def local(hidden, norm_gain, targets, out_weight):
    row_values = hidden.astype(jnp.float32)
    inv_rms = lax.rsqrt(jnp.mean(row_values * row_values, axis=-1, keepdims=True) + 1e-05)
    normed_part = (row_values * inv_rms * norm_gain.astype(jnp.float32)[None, :]).astype(
        jnp.bfloat16
    )
    feature_width = normed_part.shape[1] // lax.axis_size("tensor")
    normed_rows = lax.dynamic_slice_in_dim(
        normed_part, lax.axis_index("tensor") * feature_width, feature_width, 1
    )
    normed = lax.all_gather(normed_part, "section", axis=0, tiled=True)
    logits = jnp.dot(normed, out_weight, preferred_element_type=jnp.float32)
    shard_width = out_weight.shape[1]
    offset = (
        lax.axis_index("section") * lax.axis_size("tensor") + lax.axis_index("tensor")
    ) * shard_width
    columns = offset + lax.iota(jnp.int32, shard_width)
    target_hits = (targets[:, None] == columns[None, :]).astype(jnp.float32)
    own_target = jnp.sum(logits * target_hits, axis=1)
    local_peak = jnp.max(logits, axis=1)
    row_peak = lax.pmax(local_peak, ("section", "tensor"))
    weights = jnp.exp(logits - row_peak[:, None])
    row_total, target_logit = lax.psum(
        (jnp.sum(weights, axis=1), own_target), ("section", "tensor")
    )
    token_loss = row_peak + jnp.log(row_total) - target_logit
    shares = weights / row_total[:, None]
    probs = shares.astype(jnp.bfloat16)
    grad_logits = (shares - target_hits).astype(jnp.bfloat16)
    grad_weight = lax.dot_general(
        normed, probs, (((0,), (0,)), ((), ())), preferred_element_type=jnp.float32
    ).astype(jnp.bfloat16)
    grad_term = lax.dot_general(
        grad_logits, out_weight, (((1,), (1,)), ((), ())), preferred_element_type=jnp.float32
    )
    partial_value = lax.psum_scatter(grad_term, "tensor", scatter_dimension=1, tiled=True)
    grad_normed = lax.psum_scatter(partial_value, "section", scatter_dimension=0, tiled=True)
    return (token_loss, grad_normed.astype(jnp.bfloat16), grad_weight, normed_rows)


def solution(mesh):
    placed = (P("section", None), P(), P(), P(None, ("section", "tensor")))
    return jax.shard_map(
        local,
        mesh=mesh,
        in_specs=placed,
        out_specs=(
            P(),
            P("section", "tensor"),
            P(None, ("section", "tensor")),
            P("section", "tensor"),
        ),
        check_vma=False,
    )
```

profile of v0, /device:TPU:6, one launch (start us, length us, event | category | flops | bytes accessed | tf_op | source)
XLA Modules:
  0.0 524.8 jit_solution(16388162568244123822)
XLA Ops:
  7.2 0.0 copy-start
  7.2 0.0 all-gather.2.cloned.1.call-start
  7.2 1.3 fusion
  8.5 0.7 convert_element_type.25
  9.2 1.8 fusion.2
  11.0 0.0 all-gather.2.cloned.1.call-update
  11.0 0.0 reduce-scatter.3.cloned.1.call-start
  11.1 0.0 copy-start.1
  11.1 71.5 %all-gather.2.cloned.1.call-done = bf16[192,8192]{1,0:T(8,128)(2,1)} async-done(((bf16[16,8192]{1,0:T(8,128)(2,1)}), bf16[192,8192]{1,0:T(8,128)(2,1)}) %all-gather.2.cloned.1.call-update) | async-done | bytes 3145744 | tf_op jit(solution)/shard_map/all_gather | solution.py:17
  82.6 0.0 copy-done
  82.6 3.0 fusion.15
  85.6 103.3 %pmax.7 = f32[192]{0:T(256)S(1)} all-reduce(f32[192]{0:T(256)S(1)} %get-tuple-element.8), channel_id=1, replica_groups=mesh['section'=12,'tensor'=64] {'section','tensor'}, use_global_device_ids=true, to_apply=%region_2.0 | all-reduce | flops 192 | bytes 1536 | tf_op jit(solution)/shard_map/pmax | solution.py:27
  188.9 0.0 copy-done.1
  188.9 0.2 fusion.7
  189.1 105.7 %all-reduce = (f32[192]{0:T(256)S(1)}, f32[192]{0:T(256)S(1)}) all-reduce(f32[192]{0:T(256)S(1)} %get-tuple-element.5, f32[192]{0:T(256)S(1)} %get-tuple-element.4), channel_id=1, replica_groups=mesh['section'=12,'tensor'=64] {'section','tensor'}, use_global_device_ids=true, to_apply=%region_6.0 | all-reduce | flops 384 | bytes 3072 | tf_op jit(solution)/shard_map/psum | solution.py:29
  294.8 3.7 fusion.8
  298.6 0.0 reduce-scatter.3.cloned.1.call-update
  298.6 0.0 reduce-scatter.5.cloned.1.call-start
  298.7 1.3 constant_dynamic-slice_fusion
  299.9 4.6 convolution_convert_fusion
  304.5 153.0 %reduce-scatter.3.cloned.1.call-done = f32[192,128]{1,0:T(8,128)} async-done(((f32[192,8192]{1,0:T(8,128)}), f32[192,128]{1,0:T(8,128)}) %reduce-scatter.3.cloned.1.call-update) | async-done | bytes 98320 | tf_op jit(solution)/shard_map/reduce_scatter | solution.py:42
  457.5 0.0 reduce-scatter.5.cloned.1.call-update
  457.5 0.6 add_subtract_fusion
  458.1 58.9 %reduce-scatter.5.cloned.1.call-done = f32[16,128]{1,0:T(8,128)} async-done(((f32[192,128]{1,0:T(8,128)}), f32[16,128]{1,0:T(8,128)}) %reduce-scatter.5.cloned.1.call-update) | async-done | bytes 8208 | tf_op jit(solution)/shard_map/reduce_scatter | solution.py:43
  517.0 1.3 convert_element_type.29
  (2 shorter events, 0.0 us)
Async XLA Ops:
  7.2 75.4 %copy-start = (bf16[8192,128]{1,0:T(8,128)(2,1)S(1)}, bf16[8192,128]{1,0:T(8,128)(2,1)}, u32[]{:S(2)}) copy-start(bf16[8192,128]{1,0:T(8,128)(2,1)} %param.7) | copy-start | bytes 6291460
  7.2 75.4 %all-gather.2.cloned.1.call-start = ((), (), s32[]{:S(2)}) async-start(), calls=%async_computation.2 | async-start | bytes 3407872 | tf_op jit(solution)/shard_map/all_gather | solution.py:17
  11.0 446.5 %reduce-scatter.3.cloned.1.call-start = ((), (), s32[]{:S(2)}) async-start(), calls=%async_computation.3 | async-start | bytes 6389760 | tf_op jit(solution)/shard_map/reduce_scatter | solution.py:42
  11.1 177.8 %copy-start.1 = (s32[192]{0:T(256)S(1)}, s32[192]{0:T(256)}, u32[]{:S(2)}) copy-start(s32[192]{0:T(256)} %param.6) | copy-start | bytes 2308
  298.6 218.4 %reduce-scatter.5.cloned.1.call-start = ((), (), s32[]{:S(2)}) async-start(), calls=%async_computation.4 | async-start | bytes 106496 | tf_op jit(solution)/shard_map/reduce_scatter | solution.py:43
Sparse Core Ops, SparseCore 0:
  11.2 71.3 all-gather.1
  298.7 158.7 reduce-scatter.2
  460.9 56.0 reduce-scatter.4
where the time goes:
time: 525 us
  waiting for transfers between devices  283 us (54%)
  blocking collectives  209 us (40%)
  between operations  13.8 us (3%)
  matrix products  11.3 us (2%)
  other arithmetic  5.89 us (1%)
    reduce_scatter x1, waiting for transfers between devices, local(): lax.psum_scatter(grad_term, 'tensor', scatter_dimension=1, tiled=True)  153 us
    psum x1, blocking collectives, local(): lax.psum((jnp.sum(weights, axis=1), own_target), ('section', 'tensor'))  106 us
    pmax x1, blocking collectives, local(): row_peak = lax.pmax(local_peak, ('section', 'tensor'))  103 us
    all_gather x1, waiting for transfers between devices, local(): normed = lax.all_gather(normed_part, 'section', axis=0, tiled=True)  71.5 us
    reduce_scatter x1, waiting for transfers between devices, local(): lax.psum_scatter(partial_value, 'section', scatter_dimension=0, tiled=True)  58.9 us
  transfers between devices with their start and end apart: 3, of which 3 were waited for; matrix products, arithmetic and copies ran while one was open for 1% of the time, Pallas kernels for 0%

commit v1 on v0

v1 whole, which is shorter than its diff:
```python
import jax
import jax.numpy as jnp
from jax import lax
from jax.sharding import PartitionSpec as P

ALL = ("section", "tensor")


def local(hidden, norm_gain, targets, out_weight):
    n_ten = lax.axis_size("tensor")
    row_values = hidden.astype(jnp.float32)
    inv_rms = lax.rsqrt(jnp.mean(row_values * row_values, axis=-1, keepdims=True) + 1e-05)
    normed_part = (row_values * inv_rms * norm_gain.astype(jnp.float32)[None, :]).astype(
        jnp.bfloat16
    )
    feature_width = normed_part.shape[1] // n_ten
    normed_rows = lax.dynamic_slice_in_dim(
        normed_part, lax.axis_index("tensor") * feature_width, feature_width, 1
    )
    normed = lax.all_gather(normed_part, "section", axis=0, tiled=True)
    logits = jnp.dot(normed, out_weight, preferred_element_type=jnp.float32)
    shard_width = out_weight.shape[1]
    offset = (lax.axis_index("section") * n_ten + lax.axis_index("tensor")) * shard_width
    columns = offset + lax.iota(jnp.int32, shard_width)
    target_hits = (targets[:, None] == columns[None, :]).astype(jnp.float32)
    own_target = jnp.sum(logits * target_hits, axis=1)
    local_peak = jnp.max(logits, axis=1)
    local_total = jnp.sum(jnp.exp(logits - local_peak[:, None]), axis=1)
    stats = jnp.stack([local_peak, local_total, own_target])
    with jax.named_scope("softmax_stats_gather"):
        every = lax.all_gather(stats, ALL, axis=0)
    row_peak = jnp.max(every[:, 0], axis=0)
    row_total = jnp.sum(every[:, 1] * jnp.exp(every[:, 0] - row_peak[None, :]), axis=0)
    target_logit = jnp.sum(every[:, 2], axis=0)
    token_loss = row_peak + jnp.log(row_total) - target_logit
    weights = jnp.exp(logits - row_peak[:, None])
    shares = weights / row_total[:, None]
    probs = shares.astype(jnp.bfloat16)
    grad_logits = (shares - target_hits).astype(jnp.bfloat16)
    grad_weight = lax.dot_general(
        normed, probs, (((0,), (0,)), ((), ())), preferred_element_type=jnp.float32
    ).astype(jnp.bfloat16)
    grad_term = lax.dot_general(
        grad_logits, out_weight, (((1,), (1,)), ((), ())), preferred_element_type=jnp.float32
    )
    with jax.named_scope("grad_rows_reduce_scatter"):
        partial_value = lax.psum_scatter(grad_term, "tensor", scatter_dimension=1, tiled=True)
        grad_normed = lax.psum_scatter(partial_value, "section", scatter_dimension=0, tiled=True)
    return (token_loss, grad_normed.astype(jnp.bfloat16), grad_weight, normed_rows)


def solution(mesh):
    placed = (P("section", None), P(), P(), P(None, ("section", "tensor")))
    return jax.shard_map(
        local,
        mesh=mesh,
        in_specs=placed,
        out_specs=(
            P(),
            P("section", "tensor"),
            P(None, ("section", "tensor")),
            P("section", "tensor"),
        ),
        check_vma=False,
    )
```

time: 525 us -> 496 us (0.945)
  blocking collectives: 209 us -> 0 us
  waiting for transfers between devices: 283 us -> 449 us
  other arithmetic: 5.89 us -> 14 us
    all_gather x0 -> x1, waiting for transfers between devices: none -> 164 us  [local(): every = lax.all_gather(stats, ALL, axis=0)]
    psum x1 -> x0, blocking collectives: 106 us -> none  [local(): lax.psum((jnp.sum(weights, axis=1), own_target), ('section', 'tensor'))]
    pmax x1 -> x0, blocking collectives: 103 us -> none  [local(): row_peak = lax.pmax(local_peak, ('section', 'tensor'))]
    slice x0 -> x1, other arithmetic: none -> 6.18 us  [local(): every[:, 1] * jnp.exp(every[:, 0] - row_peak[None, :])]
  transfers between devices with their start and end apart: 3 -> 4, of which waited for: 3 -> 4; matrix products, arithmetic and copies ran while one was open for 1% -> 1% of each run, Pallas kernels for 0% -> 0%
where the time goes in v1:
time: 496 us; the launch traced here: 495 us
  waiting for transfers between devices  449 us (91%)
  other arithmetic  14 us (3%)
  between operations  13.8 us (3%)
  matrix products  12.2 us (2%)
  local copies, waits for them, and re-layouts  5.72 us (1%)
    all_gather x1, waiting for transfers between devices, local(): every = lax.all_gather(stats, ALL, axis=0)  164 us
    reduce_scatter x1, waiting for transfers between devices, local(): lax.psum_scatter(grad_term, 'tensor', scatter_dimension=1, tiled=True)  155 us
    all_gather x1, waiting for transfers between devices, local(): normed = lax.all_gather(normed_part, 'section', axis=0, tiled=True)  71.5 us
    reduce_scatter x1, waiting for transfers between devices, local(): lax.psum_scatter(partial_value, 'section', scatter_dimension=0, tiled=True)  58.6 us
  transfers between devices with their start and end apart: 4, of which 4 were waited for; matrix products, arithmetic and copies ran while one was open for 1% of the time, Pallas kernels for 0%

profile of v1, /device:TPU:6, one launch (start us, length us, event | category | flops | bytes accessed | tf_op | source)
XLA Modules:
  0.0 495.2 jit_solution(9710092144481755567)
XLA Ops:
  7.2 0.0 copy-start
  7.2 0.0 all-gather.5.cloned.1.call-start
  7.2 1.3 fusion.3
  8.5 0.7 convert_element_type.25
  9.2 1.8 fusion.5
  11.0 0.0 all-gather.5.cloned.1.call-update
  11.0 0.0 all-gather.7.cloned.1.call-start
  11.1 0.0 copy-start.3
  11.1 71.5 %all-gather.5.cloned.1.call-done = bf16[192,8192]{1,0:T(8,128)(2,1)} async-done(((bf16[16,8192]{1,0:T(8,128)(2,1)}), bf16[192,8192]{1,0:T(8,128)(2,1)}) %all-gather.5.cloned.1.call-update) | async-done | bytes 3145744 | tf_op jit(solution)/shard_map/all_gather | solution.py:20
  82.6 0.0 copy-done
  82.6 3.0 fusion.15
  85.6 0.0 copy-start.1
  85.6 0.6 copy-done.1
  86.2 0.2 exponential_reduce_fusion
  86.5 0.6 maximum_bitcast_fusion
  87.1 0.0 all-gather.7.cloned.1.call-update
  87.1 0.0 reduce-scatter.3.cloned.1.call-start
  87.2 164.4 %all-gather.7.cloned.1.call-done = f32[768,3,192]{2,1,0:T(4,128)} async-done(((f32[1,3,192]{2,1,0:T(4,128)}), f32[768,3,192]{2,1,0:T(4,128)}) %all-gather.7.cloned.1.call-update) | async-done | bytes 1769488 | tf_op jit(solution)/shard_map/softmax_stats_gather/all_gather | solution.py:31
  251.5 6.2 %fusion.14 = (f32[768,1,192]{2,1,0:T(1,128)}, f32[768,1,192]{2,1,0:T(1,128)S(1)}, f32[192]{0:T(256)S(1)}, f32[192]{0:T(256)S(1)}) fusion(f32[768,3,192]{2,1,0:T(4,128)} %all-gather.7.cloned.1.call-done), kind=kLoop, calls=%fused_computation.28 | loop fusion | flops 294528 | bytes 2950656 | tf_op jit(solution)/shard_map/slice | solution.py:33
  257.7 2.1 copy.16
  259.9 1.6 copy.15
  261.5 1.3 fusion.2
  262.8 4.6 fusion.9
  267.4 0.0 reduce-scatter.3.cloned.1.call-update
  267.5 0.0 reduce-scatter.5.cloned.1.call-start
  267.5 1.3 constant_dynamic-slice_fusion
  268.8 4.6 convolution_convert_fusion
  273.4 154.8 %reduce-scatter.3.cloned.1.call-done = f32[192,128]{1,0:T(8,128)} async-done(((f32[192,8192]{1,0:T(8,128)}), f32[192,128]{1,0:T(8,128)}) %reduce-scatter.3.cloned.1.call-update) | async-done | bytes 98320 | tf_op jit(solution)/shard_map/grad_rows_reduce_scatter/reduce_scatter | solution.py:47
  428.2 0.0 reduce-scatter.5.cloned.1.call-update
  428.2 0.6 add_subtract_fusion
  428.8 58.6 %reduce-scatter.5.cloned.1.call-done = f32[16,128]{1,0:T(8,128)} async-done(((f32[192,128]{1,0:T(8,128)}), f32[16,128]{1,0:T(8,128)}) %reduce-scatter.5.cloned.1.call-update) | async-done | bytes 8208 | tf_op jit(solution)/shard_map/grad_rows_reduce_scatter/reduce_scatter | solution.py:48
  487.4 1.3 convert_element_type.29
  (5 shorter events, 0.0 us)
Async XLA Ops:
  7.2 75.4 %copy-start = (bf16[8192,128]{1,0:T(8,128)(2,1)S(1)}, bf16[8192,128]{1,0:T(8,128)(2,1)}, u32[]{:S(2)}) copy-start(bf16[8192,128]{1,0:T(8,128)(2,1)} %param.7) | copy-start | bytes 6291460
  7.2 75.4 %all-gather.5.cloned.1.call-start = ((), (), s32[]{:S(2)}) async-start(), calls=%async_computation.2 | async-start | bytes 3407872 | tf_op jit(solution)/shard_map/all_gather | solution.py:20
  11.0 240.5 %all-gather.7.cloned.1.call-start = ((), (), s32[]{:S(2)}) async-start(), calls=%async_computation.5 | async-start | bytes 3149824 | tf_op jit(solution)/shard_map/softmax_stats_gather/all_gather | solution.py:31
  11.1 75.1 %copy-start.3 = (s32[192]{0:T(256)S(1)}, s32[192]{0:T(256)}, u32[]{:S(2)}) copy-start(s32[192]{0:T(256)} %param.6) | copy-start | bytes 2308
  85.6 0.6 copy-start.1
  87.1 341.1 %reduce-scatter.3.cloned.1.call-start = ((), (), s32[]{:S(2)}) async-start(), calls=%async_computation.3 | async-start | bytes 6389760 | tf_op jit(solution)/shard_map/grad_rows_reduce_scatter/reduce_scatter | solution.py:47
  267.4 1.4 copy-start.2
  267.5 219.9 %reduce-scatter.5.cloned.1.call-start = ((), (), s32[]{:S(2)}) async-start(), calls=%async_computation.4 | async-start | bytes 106496 | tf_op jit(solution)/shard_map/grad_rows_reduce_scatter/reduce_scatter | solution.py:48
Sparse Core Ops, SparseCore 0:
  11.2 71.3 all-gather.4
  88.7 162.7 all-gather.6
  267.6 160.5 reduce-scatter.2
  431.4 55.8 reduce-scatter.4

commit v2 on v1

--- a/solution.py
+++ b/solution.py
@@ -4,6 +4,32 @@
 from jax.sharding import PartitionSpec as P
 
 ALL = ("section", "tensor")
+
+
+def shifted_pairs(size, stride, count, shift):
+    pairs = []
+    for index in range(size):
+        coord = (index // stride) % count
+        pairs.append((index, index + ((coord + shift) % count - coord) * stride))
+    return pairs
+
+
+def gather_along(value, name, stride, count):
+    size = lax.axis_size(name)
+    coord = (lax.axis_index(name) // stride) % count
+    received = [value]
+    for shift in range(1, count):
+        received.append(lax.ppermute(value, name, shifted_pairs(size, stride, count, shift)))
+    stacked = jnp.stack(received)
+    order = (coord - jnp.arange(count, dtype=jnp.int32)) % count
+    return jnp.take(stacked, order, axis=0)
+
+
+def merge_stats(every):
+    peak = jnp.max(every[:, 0], axis=0)
+    total = jnp.sum(every[:, 1] * jnp.exp(every[:, 0] - peak[None, :]), axis=0)
+    target = jnp.sum(every[:, 2], axis=0)
+    return jnp.stack([peak, total, target])
 
 
 def local(hidden, norm_gain, targets, out_weight):
@@ -27,11 +53,11 @@
     local_peak = jnp.max(logits, axis=1)
     local_total = jnp.sum(jnp.exp(logits - local_peak[:, None]), axis=1)
     stats = jnp.stack([local_peak, local_total, own_target])
-    with jax.named_scope("softmax_stats_gather"):
-        every = lax.all_gather(stats, ALL, axis=0)
-    row_peak = jnp.max(every[:, 0], axis=0)
-    row_total = jnp.sum(every[:, 1] * jnp.exp(every[:, 0] - row_peak[None, :]), axis=0)
-    target_logit = jnp.sum(every[:, 2], axis=0)
+    with jax.named_scope("softmax_stats_exchange"):
+        for stride, count in ((1, 2), (2, 8), (16, 4)):
+            stats = merge_stats(gather_along(stats, "tensor", stride, count))
+        stats = merge_stats(gather_along(stats, "section", 1, lax.axis_size("section")))
+    row_peak, row_total, target_logit = stats[0], stats[1], stats[2]
     token_loss = row_peak + jnp.log(row_total) - target_logit
     weights = jnp.exp(logits - row_peak[:, None])
     shares = weights / row_total[:, None]
@@ -45,7 +71,15 @@
     )
     with jax.named_scope("grad_rows_reduce_scatter"):
         partial_value = lax.psum_scatter(grad_term, "tensor", scatter_dimension=1, tiled=True)
-        grad_normed = lax.psum_scatter(partial_value, "section", scatter_dimension=0, tiled=True)
+    with jax.named_scope("grad_rows_section_exchange"):
+        n_sec = lax.axis_size("section")
+        sec = lax.axis_index("section")
+        blocks = partial_value.reshape(n_sec, partial_value.shape[0] // n_sec, partial_value.shape[1])
+        grad_normed = lax.dynamic_index_in_dim(blocks, sec, 0, keepdims=False)
+        for shift in range(1, n_sec):
+            sent = lax.dynamic_index_in_dim(blocks, (sec + shift) % n_sec, 0, keepdims=False)
+            pairs = [(i, (i + shift) % n_sec) for i in range(n_sec)]
+            grad_normed = grad_normed + lax.ppermute(sent, "section", pairs)
     return (token_loss, grad_normed.astype(jnp.bfloat16), grad_weight, normed_rows)
 
 

time: 496 us -> 457 us (0.921)
  waiting for transfers between devices: 449 us -> 288 us
  starting transfers between devices: 0.16 us -> 130 us
  other arithmetic: 14 us -> 6.7 us
    all_gather x1 -> x0, waiting for transfers between devices: 164 us -> none  [local(): every = lax.all_gather(stats, ALL, axis=0)]
    ppermute x0 -> x33, starting transfers between devices: none -> 130 us  [the longest x22 77.4 us: gather_along(): lax.ppermute(value, name, shifted_pairs(size, stride, count, shift))]
    ppermute x0 -> x33, waiting for transfers between devices: none -> 59.6 us  [the longest x22 56 us: gather_along(): lax.ppermute(value, name, shifted_pairs(size, stride, count, shift))]
    reduce_scatter x1 -> x0, waiting for transfers between devices: 58.6 us -> none  [local(): lax.psum_scatter(partial_value, 'section', scatter_dimension=0, tiled=True)]
    slice x1 -> x0, other arithmetic: 6.18 us -> none  [local(): every[:, 1] * jnp.exp(every[:, 0] - row_peak[None, :])]
  transfers between devices with their start and end apart: 4 -> 35, of which waited for: 4 -> 15; matrix products, arithmetic and copies ran while one was open for 1% -> 1% of each run, Pallas kernels for 0% -> 0%
where the time goes in v2:
time: 457 us; the launch traced here: 455 us
  waiting for transfers between devices  288 us (63%)
  starting transfers between devices  130 us (28%)
  between operations  14.9 us (3%)
  matrix products  11.3 us (2%)
  other arithmetic  6.7 us (1%)
  local copies, waits for them, and re-layouts  4.6 us (1%)
    reduce_scatter x1, waiting for transfers between devices, local(): lax.psum_scatter(grad_term, 'tensor', scatter_dimension=1, tiled=True)  157 us
    ppermute x22, starting transfers between devices, gather_along(): lax.ppermute(value, name, shifted_pairs(size, stride, count, shift))  77.4 us
    all_gather x1, waiting for transfers between devices, local(): normed = lax.all_gather(normed_part, 'section', axis=0, tiled=True)  71.2 us
    ppermute x22, waiting for transfers between devices, gather_along(): lax.ppermute(value, name, shifted_pairs(size, stride, count, shift))  56 us
    ppermute x11, starting transfers between devices, local(): grad_normed = grad_normed + lax.ppermute(sent, 'section', pairs)  52.6 us
  transfers between devices with their start and end apart: 35, of which 15 were waited for; matrix products, arithmetic and copies ran while one was open for 1% of the time, Pallas kernels for 0%

profile of v2, /device:TPU:6, one launch (start us, length us, event | category | flops | bytes accessed | tf_op | source)
XLA Modules:
  0.0 455.4 jit_solution(7251327297460288295)
XLA Ops:
  11.4 71.2 %all-gather.2.cloned.1.call-done = bf16[192,8192]{1,0:T(8,128)(2,1)} async-done(((bf16[16,8192]{1,0:T(8,128)(2,1)}), bf16[192,8192]{1,0:T(8,128)(2,1)}) %all-gather.2.cloned.1.call-update) | async-done | bytes 3145744 | tf_op jit(solution)/shard_map/all_gather | solution.py:46
  89.6 5.6 %collective-permute-start.6 = (f32[3,192]{1,0:T(4,128)S(1)}, f32[3,192]{1,0:T(4,128)S(1)}, u32[]{:S(2)}, u32[]{:S(2)}) collective-permute-start(f32[3,192]{1,0:T(4,128)S(1)} %pad_maximum_fusion.3), channel_id=1, source_target_pairs={{0,12},{1,13},{2,14},{3,15},{4,0},{5,1},{6,2},{7,3},{8,4},{9,5},{1... | collective-permute-start | bytes 6920 | tf_op jit(solution)/shard_map/softmax_stats_exchange/ppermute | solution.py:22
  95.2 4.2 collective-permute-start.5
  99.4 4.7 %collective-permute-start.4 = (f32[3,192]{1,0:T(4,128)S(1)}, f32[3,192]{1,0:T(4,128)S(1)}, u32[]{:S(2)}, u32[]{:S(2)}) collective-permute-start(f32[3,192]{1,0:T(4,128)S(1)} %pad_maximum_fusion.3), channel_id=1, source_target_pairs={{0,8},{1,9},{2,10},{3,11},{4,12},{5,13},{6,14},{7,15},{8,0},{9,1},... | collective-permute-start | bytes 6920 | tf_op jit(solution)/shard_map/softmax_stats_exchange/ppermute | solution.py:22
  107.1 4.6 %collective-permute-start.1 = (f32[3,192]{1,0:T(4,128)S(1)}, f32[3,192]{1,0:T(4,128)S(1)}, u32[]{:S(2)}, u32[]{:S(2)}) collective-permute-start(f32[3,192]{1,0:T(4,128)S(1)} %pad_maximum_fusion.3), channel_id=1, source_target_pairs={{0,2},{1,3},{2,4},{3,5},{4,6},{5,7},{6,8},{7,9},{8,10},{9,11},{10,... | collective-permute-start | bytes 6920 | tf_op jit(solution)/shard_map/softmax_stats_exchange/ppermute | solution.py:22
  113.8 4.3 collective-permute-start.2
  131.0 4.0 collective-permute-start.8
  136.9 4.7 %collective-permute-done.10 = f32[3,192]{1,0:T(4,128)S(1)} collective-permute-done((f32[3,192]{1,0:T(4,128)S(1)}, f32[3,192]{1,0:T(4,128)S(1)}, u32[]{:S(2)}, u32[]{:S(2)}) %collective-permute-start.10) | collective-permute-done | bytes 2336 | tf_op jit(solution)/shard_map/softmax_stats_exchange/ppermute | solution.py:22
  142.4 3.9 collective-permute-start.20
  146.3 4.3 collective-permute-start.19
  150.6 4.4 collective-permute-start.18
  155.0 5.9 %collective-permute-start.17 = (f32[3,192]{1,0:T(4,128)S(1)}, f32[3,192]{1,0:T(4,128)S(1)}, u32[]{:S(2)}, u32[]{:S(2)}) collective-permute-start(f32[3,192]{1,0:T(4,128)S(1)} %pad_maximum_fusion.5), channel_id=1, source_target_pairs={{0,448},{64,512},{128,576},{192,640},{256,704},{320,0},{384,64},{4... | collective-permute-start | bytes 6920 | tf_op jit(solution)/shard_map/softmax_stats_exchange/ppermute | solution.py:22
  163.5 4.2 collective-permute-done.11
  169.6 5.7 %collective-permute-done.12 = f32[3,192]{1,0:T(4,128)S(1)} collective-permute-done((f32[3,192]{1,0:T(4,128)S(1)}, f32[3,192]{1,0:T(4,128)S(1)}, u32[]{:S(2)}, u32[]{:S(2)}) %collective-permute-start.12) | collective-permute-done | bytes 2336 | tf_op jit(solution)/shard_map/softmax_stats_exchange/ppermute | solution.py:22
  177.2 6.6 %collective-permute-done.13 = f32[3,192]{1,0:T(4,128)S(1)} collective-permute-done((f32[3,192]{1,0:T(4,128)S(1)}, f32[3,192]{1,0:T(4,128)S(1)}, u32[]{:S(2)}, u32[]{:S(2)}) %collective-permute-start.13) | collective-permute-done | bytes 2336 | tf_op jit(solution)/shard_map/softmax_stats_exchange/ppermute | solution.py:22
  183.8 4.8 %collective-permute-start.14 = (f32[3,192]{1,0:T(4,128)S(1)}, f32[3,192]{1,0:T(4,128)S(1)}, u32[]{:S(2)}, u32[]{:S(2)}) collective-permute-start(f32[3,192]{1,0:T(4,128)S(1)} %pad_maximum_fusion.5), channel_id=1, source_target_pairs={{0,256},{64,320},{128,384},{192,448},{256,512},{320,576},{384,640}... | collective-permute-start | bytes 6920 | tf_op jit(solution)/shard_map/softmax_stats_exchange/ppermute | solution.py:22
  188.6 4.6 %collective-permute-done.14 = f32[3,192]{1,0:T(4,128)S(1)} collective-permute-done((f32[3,192]{1,0:T(4,128)S(1)}, f32[3,192]{1,0:T(4,128)S(1)}, u32[]{:S(2)}, u32[]{:S(2)}) %collective-permute-start.14) | collective-permute-done | bytes 2336 | tf_op jit(solution)/shard_map/softmax_stats_exchange/ppermute | solution.py:22
  196.7 8.0 %collective-permute-done.15 = f32[3,192]{1,0:T(4,128)S(1)} collective-permute-done((f32[3,192]{1,0:T(4,128)S(1)}, f32[3,192]{1,0:T(4,128)S(1)}, u32[]{:S(2)}, u32[]{:S(2)}) %collective-permute-start.15) | collective-permute-done | bytes 2336 | tf_op jit(solution)/shard_map/softmax_stats_exchange/ppermute | solution.py:22
  207.6 8.9 %collective-permute-done.16 = f32[3,192]{1,0:T(4,128)S(1)} collective-permute-done((f32[3,192]{1,0:T(4,128)S(1)}, f32[3,192]{1,0:T(4,128)S(1)}, u32[]{:S(2)}, u32[]{:S(2)}) %collective-permute-start.16) | collective-permute-done | bytes 2336 | tf_op jit(solution)/shard_map/softmax_stats_exchange/ppermute | solution.py:22
  222.7 3.7 fusion.6
  226.7 156.9 %reduce-scatter.2.cloned.1.call-done = f32[192,128]{1,0:T(8,128)} async-done(((f32[192,8192]{1,0:T(8,128)}), f32[192,128]{1,0:T(8,128)}) %reduce-scatter.2.cloned.1.call-update) | async-done | bytes 98320 | tf_op jit(solution)/shard_map/grad_rows_reduce_scatter/reduce_scatter | solution.py:73
  384.4 3.5 collective-permute-start.22
  389.3 4.9 %collective-permute-start.32 = (f32[16,128]{1,0:T(8,128)S(1)}, f32[16,128]{1,0:T(8,128)S(1)}, u32[]{:S(2)}, u32[]{:S(2)}) collective-permute-start(f32[16,128]{1,0:T(8,128)S(1)} %get-tuple-element.15), channel_id=1, source_target_pairs={{0,704},{64,0},{128,64},{192,128},{256,192},{320,256},{384,320},{4... | collective-permute-start | bytes 24584 | tf_op jit(solution)/shard_map/grad_rows_section_exchange/ppermute | solution.py:82
  394.2 4.7 %collective-permute-start.31 = (f32[16,128]{1,0:T(8,128)S(1)}, f32[16,128]{1,0:T(8,128)S(1)}, u32[]{:S(2)}, u32[]{:S(2)}) collective-permute-start(f32[16,128]{1,0:T(8,128)S(1)} %get-tuple-element.16), channel_id=1, source_target_pairs={{0,640},{64,704},{128,0},{192,64},{256,128},{320,192},{384,256},{4... | collective-permute-start | bytes 24584 | tf_op jit(solution)/shard_map/grad_rows_section_exchange/ppermute | solution.py:82
  398.9 5.8 %collective-permute-start.30 = (f32[16,128]{1,0:T(8,128)S(1)}, f32[16,128]{1,0:T(8,128)S(1)}, u32[]{:S(2)}, u32[]{:S(2)}) collective-permute-start(f32[16,128]{1,0:T(8,128)S(1)} %get-tuple-element.17), channel_id=1, source_target_pairs={{0,576},{64,640},{128,704},{192,0},{256,64},{320,128},{384,192},{4... | collective-permute-start | bytes 24584 | tf_op jit(solution)/shard_map/grad_rows_section_exchange/ppermute | solution.py:82
  407.6 5.9 %collective-permute-start.28 = (f32[16,128]{1,0:T(8,128)S(1)}, f32[16,128]{1,0:T(8,128)S(1)}, u32[]{:S(2)}, u32[]{:S(2)}) collective-permute-start(f32[16,128]{1,0:T(8,128)S(1)} %get-tuple-element.19), channel_id=1, source_target_pairs={{0,448},{64,512},{128,576},{192,640},{256,704},{320,0},{384,64},{4... | collective-permute-start | bytes 24584 | tf_op jit(solution)/shard_map/grad_rows_section_exchange/ppermute | solution.py:82
  413.5 4.6 %convolution_convert_fusion = bf16[8192,128]{1,0:T(8,128)(2,1)} fusion(bf16[192,8192]{1,0:T(8,128)(2,1)} %all-gather.2.cloned.1.call-done, f32[192,128]{1,0:T(8,128)S(1)} %get-tuple-element.38, f32[192]{0:T(256)S(1)} %fusion.14, f32[192]{0:T(256)S(1)} %get-tuple-element.6), kind=kOutput, calls=%fused_computation.4 | convolution fusion | flops 403775488 | bytes 5342720 | tf_op jit(solution)/shard_map/dot_general | solution.py:66
  418.1 6.8 %collective-permute-start.27 = (f32[16,128]{1,0:T(8,128)S(1)}, f32[16,128]{1,0:T(8,128)S(1)}, u32[]{:S(2)}, u32[]{:S(2)}) collective-permute-start(f32[16,128]{1,0:T(8,128)S(1)} %get-tuple-element.20), channel_id=1, source_target_pairs={{0,384},{64,448},{128,512},{192,576},{256,640},{320,704},{384,0},{... | collective-permute-start | bytes 24584 | tf_op jit(solution)/shard_map/grad_rows_section_exchange/ppermute | solution.py:82
  424.9 4.0 collective-permute-start.26
  428.9 3.6 collective-permute-start.25
  432.5 7.1 %collective-permute-start.24 = (f32[16,128]{1,0:T(8,128)S(1)}, f32[16,128]{1,0:T(8,128)S(1)}, u32[]{:S(2)}, u32[]{:S(2)}) collective-permute-start(f32[16,128]{1,0:T(8,128)S(1)} %get-tuple-element.23), channel_id=1, source_target_pairs={{0,192},{64,256},{128,320},{192,384},{256,448},{320,512},{384,576}... | collective-permute-start | bytes 24584 | tf_op jit(solution)/shard_map/grad_rows_section_exchange/ppermute | solution.py:82
  443.7 3.6 collective-permute-done.23
  (111 shorter events, 60.8 us)
Async XLA Ops:
  7.2 75.4 %all-gather.2.cloned.1.call-start = ((), (), s32[]{:S(2)}) async-start(), calls=%async_computation.1 | async-start | bytes 3407872 | tf_op jit(solution)/shard_map/all_gather | solution.py:46
  11.0 372.5 %reduce-scatter.2.cloned.1.call-start = ((), (), s32[]{:S(2)}) async-start(), calls=%async_computation.2 | async-start | bytes 6389760 | tf_op jit(solution)/shard_map/grad_rows_reduce_scatter/reduce_scatter | solution.py:73
  89.6 33.8 %collective-permute-start.6 = (f32[3,192]{1,0:T(4,128)S(1)}, f32[3,192]{1,0:T(4,128)S(1)}, u32[]{:S(2)}, u32[]{:S(2)}) collective-permute-start(f32[3,192]{1,0:T(4,128)S(1)} %pad_maximum_fusion.3), channel_id=1, source_target_pairs={{0,12},{1,13},{2,14},{3,15},{4,0},{5,1},{6,2},{7,3},{8,4},{9,5},{1... | collective-permute-start | bytes 6920 | tf_op jit(solution)/shard_map/softmax_stats_exchange/ppermute | solution.py:22
  95.2 28.1 %collective-permute-start.5 = (f32[3,192]{1,0:T(4,128)S(1)}, f32[3,192]{1,0:T(4,128)S(1)}, u32[]{:S(2)}, u32[]{:S(2)}) collective-permute-start(f32[3,192]{1,0:T(4,128)S(1)} %pad_maximum_fusion.3), channel_id=1, source_target_pairs={{0,10},{1,11},{2,12},{3,13},{4,14},{5,15},{6,0},{7,1},{8,2},{9,3},... | collective-permute-start | bytes 6920 | tf_op jit(solution)/shard_map/softmax_stats_exchange/ppermute | solution.py:22
  99.4 23.9 %collective-permute-start.4 = (f32[3,192]{1,0:T(4,128)S(1)}, f32[3,192]{1,0:T(4,128)S(1)}, u32[]{:S(2)}, u32[]{:S(2)}) collective-permute-start(f32[3,192]{1,0:T(4,128)S(1)} %pad_maximum_fusion.3), channel_id=1, source_target_pairs={{0,8},{1,9},{2,10},{3,11},{4,12},{5,13},{6,14},{7,15},{8,0},{9,1},... | collective-permute-start | bytes 6920 | tf_op jit(solution)/shard_map/softmax_stats_exchange/ppermute | solution.py:22
  104.1 19.2 %collective-permute-start.3 = (f32[3,192]{1,0:T(4,128)S(1)}, f32[3,192]{1,0:T(4,128)S(1)}, u32[]{:S(2)}, u32[]{:S(2)}) collective-permute-start(f32[3,192]{1,0:T(4,128)S(1)} %pad_maximum_fusion.3), channel_id=1, source_target_pairs={{0,6},{1,7},{2,8},{3,9},{4,10},{5,11},{6,12},{7,13},{8,14},{9,15},... | collective-permute-start | bytes 6920 | tf_op jit(solution)/shard_map/softmax_stats_exchange/ppermute | solution.py:22
  107.1 6.7 %collective-permute-start.1 = (f32[3,192]{1,0:T(4,128)S(1)}, f32[3,192]{1,0:T(4,128)S(1)}, u32[]{:S(2)}, u32[]{:S(2)}) collective-permute-start(f32[3,192]{1,0:T(4,128)S(1)} %pad_maximum_fusion.3), channel_id=1, source_target_pairs={{0,2},{1,3},{2,4},{3,5},{4,6},{5,7},{6,8},{7,9},{8,10},{9,11},{10,... | collective-permute-start | bytes 6920 | tf_op jit(solution)/shard_map/softmax_stats_exchange/ppermute | solution.py:22
  113.8 7.6 %collective-permute-start.2 = (f32[3,192]{1,0:T(4,128)S(1)}, f32[3,192]{1,0:T(4,128)S(1)}, u32[]{:S(2)}, u32[]{:S(2)}) collective-permute-start(f32[3,192]{1,0:T(4,128)S(1)} %pad_maximum_fusion.3), channel_id=1, source_target_pairs={{0,4},{1,5},{2,6},{3,7},{4,8},{5,9},{6,10},{7,11},{8,12},{9,13},{1... | collective-permute-start | bytes 6920 | tf_op jit(solution)/shard_map/softmax_stats_exchange/ppermute | solution.py:22
  127.6 9.3 %collective-permute-start.9 = (f32[3,192]{1,0:T(4,128)S(1)}, f32[3,192]{1,0:T(4,128)S(1)}, u32[]{:S(2)}, u32[]{:S(2)}) collective-permute-start(f32[3,192]{1,0:T(4,128)S(1)} %get-tuple-element.34), channel_id=1, source_target_pairs={{0,32},{1,33},{2,34},{3,35},{4,36},{5,37},{6,38},{7,39},{8,40},{9,... | collective-permute-start | bytes 6920 | tf_op jit(solution)/shard_map/softmax_stats_exchange/ppermute | solution.py:22
  131.0 5.9 %collective-permute-start.8 = (f32[3,192]{1,0:T(4,128)S(1)}, f32[3,192]{1,0:T(4,128)S(1)}, u32[]{:S(2)}, u32[]{:S(2)}) collective-permute-start(f32[3,192]{1,0:T(4,128)S(1)} %get-tuple-element.34), channel_id=1, source_target_pairs={{0,16},{1,17},{2,18},{3,19},{4,20},{5,21},{6,22},{7,23},{8,24},{9,... | collective-permute-start | bytes 6920 | tf_op jit(solution)/shard_map/softmax_stats_exchange/ppermute | solution.py:22
  135.0 6.7 %collective-permute-start.10 = (f32[3,192]{1,0:T(4,128)S(1)}, f32[3,192]{1,0:T(4,128)S(1)}, u32[]{:S(2)}, u32[]{:S(2)}) collective-permute-start(f32[3,192]{1,0:T(4,128)S(1)} %get-tuple-element.34), channel_id=1, source_target_pairs={{0,48},{1,49},{2,50},{3,51},{4,52},{5,53},{6,54},{7,55},{8,56},{9,... | collective-permute-start | bytes 6920 | tf_op jit(solution)/shard_map/softmax_stats_exchange/ppermute | solution.py:22
  142.4 76.1 %collective-permute-start.20 = (f32[3,192]{1,0:T(4,128)S(1)}, f32[3,192]{1,0:T(4,128)S(1)}, u32[]{:S(2)}, u32[]{:S(2)}) collective-permute-start(f32[3,192]{1,0:T(4,128)S(1)} %pad_maximum_fusion.5), channel_id=1, source_target_pairs={{0,640},{64,704},{128,0},{192,64},{256,128},{320,192},{384,256},{4... | collective-permute-start | bytes 6920 | tf_op jit(solution)/shard_map/softmax_stats_exchange/ppermute | solution.py:22
  146.3 72.1 %collective-permute-start.19 = (f32[3,192]{1,0:T(4,128)S(1)}, f32[3,192]{1,0:T(4,128)S(1)}, u32[]{:S(2)}, u32[]{:S(2)}) collective-permute-start(f32[3,192]{1,0:T(4,128)S(1)} %pad_maximum_fusion.5), channel_id=1, source_target_pairs={{0,576},{64,640},{128,704},{192,0},{256,64},{320,128},{384,192},{4... | collective-permute-start | bytes 6920 | tf_op jit(solution)/shard_map/softmax_stats_exchange/ppermute | solution.py:22
  150.6 67.8 %collective-permute-start.18 = (f32[3,192]{1,0:T(4,128)S(1)}, f32[3,192]{1,0:T(4,128)S(1)}, u32[]{:S(2)}, u32[]{:S(2)}) collective-permute-start(f32[3,192]{1,0:T(4,128)S(1)} %pad_maximum_fusion.5), channel_id=1, source_target_pairs={{0,512},{64,576},{128,640},{192,704},{256,0},{320,64},{384,128},{4... | collective-permute-start | bytes 6920 | tf_op jit(solution)/shard_map/softmax_stats_exchange/ppermute | solution.py:22
  155.0 63.4 %collective-permute-start.17 = (f32[3,192]{1,0:T(4,128)S(1)}, f32[3,192]{1,0:T(4,128)S(1)}, u32[]{:S(2)}, u32[]{:S(2)}) collective-permute-start(f32[3,192]{1,0:T(4,128)S(1)} %pad_maximum_fusion.5), channel_id=1, source_target_pairs={{0,448},{64,512},{128,576},{192,640},{256,704},{320,0},{384,64},{4... | collective-permute-start | bytes 6920 | tf_op jit(solution)/shard_map/softmax_stats_exchange/ppermute | solution.py:22
  161.0 6.7 %collective-permute-start.11 = (f32[3,192]{1,0:T(4,128)S(1)}, f32[3,192]{1,0:T(4,128)S(1)}, u32[]{:S(2)}, u32[]{:S(2)}) collective-permute-start(f32[3,192]{1,0:T(4,128)S(1)} %pad_maximum_fusion.5), channel_id=1, source_target_pairs={{0,64},{64,128},{128,192},{192,256},{256,320},{320,384},{384,448},... | collective-permute-start | bytes 6920 | tf_op jit(solution)/shard_map/softmax_stats_exchange/ppermute | solution.py:22
  167.7 7.6 %collective-permute-start.12 = (f32[3,192]{1,0:T(4,128)S(1)}, f32[3,192]{1,0:T(4,128)S(1)}, u32[]{:S(2)}, u32[]{:S(2)}) collective-permute-start(f32[3,192]{1,0:T(4,128)S(1)} %pad_maximum_fusion.5), channel_id=1, source_target_pairs={{0,128},{64,192},{128,256},{192,320},{256,384},{320,448},{384,512}... | collective-permute-start | bytes 6920 | tf_op jit(solution)/shard_map/softmax_stats_exchange/ppermute | solution.py:22
  175.3 8.5 %collective-permute-start.13 = (f32[3,192]{1,0:T(4,128)S(1)}, f32[3,192]{1,0:T(4,128)S(1)}, u32[]{:S(2)}, u32[]{:S(2)}) collective-permute-start(f32[3,192]{1,0:T(4,128)S(1)} %pad_maximum_fusion.5), channel_id=1, source_target_pairs={{0,192},{64,256},{128,320},{192,384},{256,448},{320,512},{384,576}... | collective-permute-start | bytes 6920 | tf_op jit(solution)/shard_map/softmax_stats_exchange/ppermute | solution.py:22
  183.8 9.4 %collective-permute-start.14 = (f32[3,192]{1,0:T(4,128)S(1)}, f32[3,192]{1,0:T(4,128)S(1)}, u32[]{:S(2)}, u32[]{:S(2)}) collective-permute-start(f32[3,192]{1,0:T(4,128)S(1)} %pad_maximum_fusion.5), channel_id=1, source_target_pairs={{0,256},{64,320},{128,384},{192,448},{256,512},{320,576},{384,640}... | collective-permute-start | bytes 6920 | tf_op jit(solution)/shard_map/softmax_stats_exchange/ppermute | solution.py:22
  193.2 11.5 %collective-permute-start.15 = (f32[3,192]{1,0:T(4,128)S(1)}, f32[3,192]{1,0:T(4,128)S(1)}, u32[]{:S(2)}, u32[]{:S(2)}) collective-permute-start(f32[3,192]{1,0:T(4,128)S(1)} %pad_maximum_fusion.5), channel_id=1, source_target_pairs={{0,320},{64,384},{128,448},{192,512},{256,576},{320,640},{384,704}... | collective-permute-start | bytes 6920 | tf_op jit(solution)/shard_map/softmax_stats_exchange/ppermute | solution.py:22
  204.7 11.8 %collective-permute-start.16 = (f32[3,192]{1,0:T(4,128)S(1)}, f32[3,192]{1,0:T(4,128)S(1)}, u32[]{:S(2)}, u32[]{:S(2)}) collective-permute-start(f32[3,192]{1,0:T(4,128)S(1)} %pad_maximum_fusion.5), channel_id=1, source_target_pairs={{0,384},{64,448},{128,512},{192,576},{256,640},{320,704},{384,0},{... | collective-permute-start | bytes 6920 | tf_op jit(solution)/shard_map/softmax_stats_exchange/ppermute | solution.py:22
  384.4 23.2 %collective-permute-start.22 = (f32[16,128]{1,0:T(8,128)S(1)}, f32[16,128]{1,0:T(8,128)S(1)}, u32[]{:S(2)}, u32[]{:S(2)}) collective-permute-start(f32[16,128]{1,0:T(8,128)S(1)} %get-tuple-element.14), channel_id=1, source_target_pairs={{0,64},{64,128},{128,192},{192,256},{256,320},{320,384},{384,448},... | collective-permute-start | bytes 24584 | tf_op jit(solution)/shard_map/grad_rows_section_exchange/ppermute | solution.py:82
  389.3 28.9 %collective-permute-start.32 = (f32[16,128]{1,0:T(8,128)S(1)}, f32[16,128]{1,0:T(8,128)S(1)}, u32[]{:S(2)}, u32[]{:S(2)}) collective-permute-start(f32[16,128]{1,0:T(8,128)S(1)} %get-tuple-element.15), channel_id=1, source_target_pairs={{0,704},{64,0},{128,64},{192,128},{256,192},{320,256},{384,320},{4... | collective-permute-start | bytes 24584 | tf_op jit(solution)/shard_map/grad_rows_section_exchange/ppermute | solution.py:82
  394.2 30.7 %collective-permute-start.31 = (f32[16,128]{1,0:T(8,128)S(1)}, f32[16,128]{1,0:T(8,128)S(1)}, u32[]{:S(2)}, u32[]{:S(2)}) collective-permute-start(f32[16,128]{1,0:T(8,128)S(1)} %get-tuple-element.16), channel_id=1, source_target_pairs={{0,640},{64,704},{128,0},{192,64},{256,128},{320,192},{384,256},{4... | collective-permute-start | bytes 24584 | tf_op jit(solution)/shard_map/grad_rows_section_exchange/ppermute | solution.py:82
  398.9 30.0 %collective-permute-start.30 = (f32[16,128]{1,0:T(8,128)S(1)}, f32[16,128]{1,0:T(8,128)S(1)}, u32[]{:S(2)}, u32[]{:S(2)}) collective-permute-start(f32[16,128]{1,0:T(8,128)S(1)} %get-tuple-element.17), channel_id=1, source_target_pairs={{0,576},{64,640},{128,704},{192,0},{256,64},{320,128},{384,192},{4... | collective-permute-start | bytes 24584 | tf_op jit(solution)/shard_map/grad_rows_section_exchange/ppermute | solution.py:82
  404.7 27.8 %collective-permute-start.29 = (f32[16,128]{1,0:T(8,128)S(1)}, f32[16,128]{1,0:T(8,128)S(1)}, u32[]{:S(2)}, u32[]{:S(2)}) collective-permute-start(f32[16,128]{1,0:T(8,128)S(1)} %get-tuple-element.18), channel_id=1, source_target_pairs={{0,512},{64,576},{128,640},{192,704},{256,0},{320,64},{384,128},{4... | collective-permute-start | bytes 24584 | tf_op jit(solution)/shard_map/grad_rows_section_exchange/ppermute | solution.py:82
  407.6 32.0 %collective-permute-start.28 = (f32[16,128]{1,0:T(8,128)S(1)}, f32[16,128]{1,0:T(8,128)S(1)}, u32[]{:S(2)}, u32[]{:S(2)}) collective-permute-start(f32[16,128]{1,0:T(8,128)S(1)} %get-tuple-element.19), channel_id=1, source_target_pairs={{0,448},{64,512},{128,576},{192,640},{256,704},{320,0},{384,64},{4... | collective-permute-start | bytes 24584 | tf_op jit(solution)/shard_map/grad_rows_section_exchange/ppermute | solution.py:82
  418.1 25.5 %collective-permute-start.27 = (f32[16,128]{1,0:T(8,128)S(1)}, f32[16,128]{1,0:T(8,128)S(1)}, u32[]{:S(2)}, u32[]{:S(2)}) collective-permute-start(f32[16,128]{1,0:T(8,128)S(1)} %get-tuple-element.20), channel_id=1, source_target_pairs={{0,384},{64,448},{128,512},{192,576},{256,640},{320,704},{384,0},{... | collective-permute-start | bytes 24584 | tf_op jit(solution)/shard_map/grad_rows_section_exchange/ppermute | solution.py:82
  424.9 18.7 %collective-permute-start.26 = (f32[16,128]{1,0:T(8,128)S(1)}, f32[16,128]{1,0:T(8,128)S(1)}, u32[]{:S(2)}, u32[]{:S(2)}) collective-permute-start(f32[16,128]{1,0:T(8,128)S(1)} %get-tuple-element.21), channel_id=1, source_target_pairs={{0,320},{64,384},{128,448},{192,512},{256,576},{320,640},{384,704}... | collective-permute-start | bytes 24584 | tf_op jit(solution)/shard_map/grad_rows_section_exchange/ppermute | solution.py:82
  428.9 14.7 %collective-permute-start.25 = (f32[16,128]{1,0:T(8,128)S(1)}, f32[16,128]{1,0:T(8,128)S(1)}, u32[]{:S(2)}, u32[]{:S(2)}) collective-permute-start(f32[16,128]{1,0:T(8,128)S(1)} %get-tuple-element.22), channel_id=1, source_target_pairs={{0,256},{64,320},{128,384},{192,448},{256,512},{320,576},{384,640}... | collective-permute-start | bytes 24584 | tf_op jit(solution)/shard_map/grad_rows_section_exchange/ppermute | solution.py:82
  432.5 11.1 %collective-permute-start.24 = (f32[16,128]{1,0:T(8,128)S(1)}, f32[16,128]{1,0:T(8,128)S(1)}, u32[]{:S(2)}, u32[]{:S(2)}) collective-permute-start(f32[16,128]{1,0:T(8,128)S(1)} %get-tuple-element.23), channel_id=1, source_target_pairs={{0,192},{64,256},{128,320},{192,384},{256,448},{320,512},{384,576}... | collective-permute-start | bytes 24584 | tf_op jit(solution)/shard_map/grad_rows_section_exchange/ppermute | solution.py:82
  439.6 7.7 %collective-permute-start.23 = (f32[16,128]{1,0:T(8,128)S(1)}, f32[16,128]{1,0:T(8,128)S(1)}, u32[]{:S(2)}, u32[]{:S(2)}) collective-permute-start(f32[16,128]{1,0:T(8,128)S(1)} %get-tuple-element.24), channel_id=1, source_target_pairs={{0,128},{64,192},{128,256},{192,320},{256,384},{320,448},{384,512}... | collective-permute-start | bytes 24584 | tf_op jit(solution)/shard_map/grad_rows_section_exchange/ppermute | solution.py:82
  (5 other events, 163.7 us)
Sparse Core Ops, SparseCore 0:
  11.2 71.3 all-gather.1
  226.6 156.9 reduce-scatter.1

commit v3 on v1

--- a/solution.py
+++ b/solution.py
@@ -3,16 +3,98 @@
 from jax import lax
 from jax.sharding import PartitionSpec as P
 
-ALL = ("section", "tensor")
+TENSOR_MASK_ORDER = (1, 2, 16, 4, 32, 8)
+
+
+def split_pow2(count):
+    low = 1
+    while count % (low * 2) == 0:
+        low *= 2
+    return low, count // low
+
+
+def tensor_masks(count):
+    masks = [m for m in TENSOR_MASK_ORDER if m < count]
+    masks += [1 << j for j in range(count.bit_length() - 1) if (1 << j) not in masks]
+    return masks
+
+
+def section_masks(count):
+    low, _ = split_pow2(count)
+    return [1 << j for j in range(low.bit_length() - 1)]
+
+
+def xor_pairs(count, mask):
+    return [(i, i ^ mask) for i in range(count)]
+
+
+def merge_pair(first, second):
+    peak = jnp.maximum(first[0], second[0])
+    total = first[1] * jnp.exp(first[0] - peak) + second[1] * jnp.exp(second[0] - peak)
+    return jnp.stack([peak, total, first[2] + second[2]])
+
+
+def merge_stats(every):
+    peak = jnp.max(every[:, 0], axis=0)
+    total = jnp.sum(every[:, 1] * jnp.exp(every[:, 0] - peak[None, :]), axis=0)
+    target = jnp.sum(every[:, 2], axis=0)
+    return jnp.stack([peak, total, target])
+
+
+def exchange_stats(stats):
+    steps = [("tensor", m) for m in tensor_masks(lax.axis_size("tensor"))]
+    steps += [("section", m) for m in section_masks(lax.axis_size("section"))]
+    for name, mask in steps:
+        other = lax.ppermute(stats, name, xor_pairs(lax.axis_size(name), mask))
+        upper = (lax.axis_index(name) & mask) != 0
+        stats = merge_pair(jnp.where(upper, other, stats), jnp.where(upper, stats, other))
+    n_sec = lax.axis_size("section")
+    low, groups = split_pow2(n_sec)
+    if groups > 1:
+        group = lax.axis_index("section") // low
+        received = [stats]
+        for shift in range(1, groups):
+            pairs = [(i, (i + shift * low) % n_sec) for i in range(n_sec)]
+            received.append(lax.ppermute(stats, "section", pairs))
+        order = (group - jnp.arange(groups, dtype=jnp.int32)) % groups
+        stats = merge_stats(jnp.take(jnp.stack(received), order, axis=0))
+    return stats
+
+
+def reduce_scatter_blocks(blocks):
+    n_sec, n_ten = blocks.shape[0], blocks.shape[1]
+    low, groups = split_pow2(n_sec)
+    t_bits = n_ten.bit_length() - 1
+    s_bits = low.bit_length() - 1
+    labels = ["group"] + [("section", 1 << j) for j in reversed(range(s_bits))]
+    labels += [("tensor", 1 << j) for j in reversed(range(t_bits))]
+    value = blocks.reshape((groups,) + (2,) * (s_bits + t_bits) + blocks.shape[2:])
+    steps = [("tensor", m) for m in tensor_masks(n_ten)] + [("section", m) for m in section_masks(n_sec)]
+    for name, mask in steps:
+        axis = labels.index((name, mask))
+        mine = (lax.axis_index(name) & mask) // mask
+        keep = lax.dynamic_index_in_dim(value, mine, axis, keepdims=False)
+        sent = lax.dynamic_index_in_dim(value, 1 - mine, axis, keepdims=False)
+        value = keep + lax.ppermute(sent, name, xor_pairs(lax.axis_size(name), mask))
+        labels.pop(axis)
+    group = lax.axis_index("section") // low
+    total = lax.dynamic_index_in_dim(value, group, 0, keepdims=False)
+    for shift in range(1, groups):
+        sent = lax.dynamic_index_in_dim(value, (group + shift) % groups, 0, keepdims=False)
+        pairs = [(i, (i + shift * low) % n_sec) for i in range(n_sec)]
+        total = total + lax.ppermute(sent, "section", pairs)
+    return total
 
 
 def local(hidden, norm_gain, targets, out_weight):
+    n_sec = lax.axis_size("section")
     n_ten = lax.axis_size("tensor")
     row_values = hidden.astype(jnp.float32)
     inv_rms = lax.rsqrt(jnp.mean(row_values * row_values, axis=-1, keepdims=True) + 1e-05)
     normed_part = (row_values * inv_rms * norm_gain.astype(jnp.float32)[None, :]).astype(
         jnp.bfloat16
     )
+    rows_per_sec = normed_part.shape[0]
     feature_width = normed_part.shape[1] // n_ten
     normed_rows = lax.dynamic_slice_in_dim(
         normed_part, lax.axis_index("tensor") * feature_width, feature_width, 1
@@ -26,12 +108,9 @@
     own_target = jnp.sum(logits * target_hits, axis=1)
     local_peak = jnp.max(logits, axis=1)
     local_total = jnp.sum(jnp.exp(logits - local_peak[:, None]), axis=1)
-    stats = jnp.stack([local_peak, local_total, own_target])
-    with jax.named_scope("softmax_stats_gather"):
-        every = lax.all_gather(stats, ALL, axis=0)
-    row_peak = jnp.max(every[:, 0], axis=0)
-    row_total = jnp.sum(every[:, 1] * jnp.exp(every[:, 0] - row_peak[None, :]), axis=0)
-    target_logit = jnp.sum(every[:, 2], axis=0)
+    with jax.named_scope("softmax_stats_exchange"):
+        stats = exchange_stats(jnp.stack([local_peak, local_total, own_target]))
+    row_peak, row_total, target_logit = stats[0], stats[1], stats[2]
     token_loss = row_peak + jnp.log(row_total) - target_logit
     weights = jnp.exp(logits - row_peak[:, None])
     shares = weights / row_total[:, None]
@@ -43,9 +122,9 @@
     grad_term = lax.dot_general(
         grad_logits, out_weight, (((1,), (1,)), ((), ())), preferred_element_type=jnp.float32
     )
+    blocks = grad_term.reshape(n_sec, rows_per_sec, n_ten, feature_width).transpose(0, 2, 1, 3)
     with jax.named_scope("grad_rows_reduce_scatter"):
-        partial_value = lax.psum_scatter(grad_term, "tensor", scatter_dimension=1, tiled=True)
-        grad_normed = lax.psum_scatter(partial_value, "section", scatter_dimension=0, tiled=True)
+        grad_normed = reduce_scatter_blocks(blocks)
     return (token_loss, grad_normed.astype(jnp.bfloat16), grad_weight, normed_rows)
 
 

time: 496 us -> 319 us (0.64)
  waiting for transfers between devices: 449 us -> 188 us
  starting transfers between devices: 0.16 us -> 77.6 us
  local copies, waits for them, and re-layouts: 5.72 us -> 15.2 us
    reduce_scatter x2 -> x0, waiting for transfers between devices: 213 us -> none  [the longest x1 155 us: local(): lax.psum_scatter(grad_term, 'tensor', scatter_dimension=1, tiled=True)]
    all_gather x1 -> x0, waiting for transfers between devices: 164 us -> none  [local(): every = lax.all_gather(stats, ALL, axis=0)]
    ppermute x0 -> x20, waiting for transfers between devices: none -> 116 us  [the longest x8 87.3 us: reduce_scatter_blocks(): lax.ppermute(sent, name, xor_pairs(lax.axis_size(name), mask))]
    ppermute x0 -> x20, starting transfers between devices: none -> 77.5 us  [the longest x8 29.7 us: reduce_scatter_blocks(): lax.ppermute(sent, name, xor_pairs(lax.axis_size(name), mask))]
    add x0 -> x16, other arithmetic: none -> 8.92 us  [the longest x8 8.81 us: reduce_scatter_blocks(): keep + lax.ppermute(sent, name, xor_pairs(lax.axis_size(name), mask))]
    slice x1 -> x0, other arithmetic: 6.18 us -> none  [local(): every[:, 1] * jnp.exp(every[:, 0] - row_peak[None, :])]
  transfers between devices with their start and end apart: 4 -> 21, of which waited for: 4 -> 18; matrix products, arithmetic and copies ran while one was open for 1% -> 2% of each run, Pallas kernels for 0% -> 0%
where the time goes in v3:
time: 319 us; the launch traced here: 318 us
  waiting for transfers between devices  188 us (59%)
  starting transfers between devices  77.6 us (24%)
  local copies, waits for them, and re-layouts  15.2 us (5%)
  between operations  14.7 us (5%)
  other arithmetic  14.5 us (5%)
  matrix products  8.63 us (3%)
    ppermute x8, waiting for transfers between devices, reduce_scatter_blocks(): lax.ppermute(sent, name, xor_pairs(lax.axis_size(name), mask))  87.3 us
    all_gather x1, waiting for transfers between devices, local(): normed = lax.all_gather(normed_part, 'section', axis=0, tiled=True)  71.5 us
    ppermute x8, starting transfers between devices, reduce_scatter_blocks(): lax.ppermute(sent, name, xor_pairs(lax.axis_size(name), mask))  29.7 us
    ppermute x8, starting transfers between devices, exchange_stats(): other = lax.ppermute(stats, name, xor_pairs(lax.axis_size(name), mask))  28.3 us
    ppermute x8, waiting for transfers between devices, exchange_stats(): other = lax.ppermute(stats, name, xor_pairs(lax.axis_size(name), mask))  20.3 us
    ppermute x2, starting transfers between devices, reduce_scatter_blocks(): total = total + lax.ppermute(sent, 'section', pairs)  9.75 us
    ppermute x2, starting transfers between devices, exchange_stats(): received.append(lax.ppermute(stats, 'section', pairs))  9.75 us
    add x8, other arithmetic, reduce_scatter_blocks(): keep + lax.ppermute(sent, name, xor_pairs(lax.axis_size(name), mask))  8.81 us
  transfers between devices with their start and end apart: 21, of which 18 were waited for; matrix products, arithmetic and copies ran while one was open for 2% of the time, Pallas kernels for 0%

profile of v3, /device:TPU:6, one launch (start us, length us, event | category | flops | bytes accessed | tf_op | source)
XLA Modules:
  0.0 318.3 jit_solution(6722838642471185130)
XLA Ops:
  11.1 71.5 %all-gather.2.cloned.1.call-done = bf16[192,8192]{1,0:T(8,128)(2,1)} async-done(((bf16[16,8192]{1,0:T(8,128)(2,1)}), bf16[192,8192]{1,0:T(8,128)(2,1)}) %all-gather.2.cloned.1.call-update) | async-done | bytes 3145744 | tf_op jit(solution)/shard_map/all_gather | solution.py:102
  82.6 2.9 fusion.26
  88.9 3.4 %collective-permute-start.1 = (f32[3,192]{1,0:T(4,128)S(1)}, f32[3,192]{1,0:T(4,128)S(1)}, u32[]{:S(2)}, u32[]{:S(2)}) collective-permute-start(f32[3,192]{1,0:T(4,128)S(1)} %pad_maximum_fusion.2), channel_id=1, source_target_pairs={{0,2},{1,3},{2,0},{3,1},{4,6},{5,7},{6,4},{7,5},{8,10},{9,11},{10,... | collective-permute-start | bytes 6920 | tf_op jit(solution)/shard_map/softmax_stats_exchange/ppermute | solution.py:48
  94.5 2.8 collective-permute-start.2
  100.1 4.3 %collective-permute-start.3 = (f32[3,192]{1,0:T(4,128)S(1)}, f32[3,192]{1,0:T(4,128)S(1)}, u32[]{:S(2)}, u32[]{:S(2)}) collective-permute-start(f32[3,192]{1,0:T(4,128)S(1)} %pad_maximum_fusion.4), channel_id=1, source_target_pairs={{0,4},{1,5},{2,6},{3,7},{4,0},{5,1},{6,2},{7,3},{8,12},{9,13},{10,... | collective-permute-start | bytes 6920 | tf_op jit(solution)/shard_map/softmax_stats_exchange/ppermute | solution.py:48
  106.5 3.4 %collective-permute-start.4 = (f32[3,192]{1,0:T(4,128)S(1)}, f32[3,192]{1,0:T(4,128)S(1)}, u32[]{:S(2)}, u32[]{:S(2)}) collective-permute-start(f32[3,192]{1,0:T(4,128)S(1)} %pad_maximum_fusion.5), channel_id=1, source_target_pairs={{0,32},{1,33},{2,34},{3,35},{4,36},{5,37},{6,38},{7,39},{8,40},{9,... | collective-permute-start | bytes 6920 | tf_op jit(solution)/shard_map/softmax_stats_exchange/ppermute | solution.py:48
  109.9 3.6 %collective-permute-done.4 = f32[3,192]{1,0:T(4,128)S(1)} collective-permute-done((f32[3,192]{1,0:T(4,128)S(1)}, f32[3,192]{1,0:T(4,128)S(1)}, u32[]{:S(2)}, u32[]{:S(2)}) %collective-permute-start.4) | collective-permute-done | bytes 2336 | tf_op jit(solution)/shard_map/softmax_stats_exchange/ppermute | solution.py:48
  113.6 7.4 %collective-permute-start.5 = (f32[3,192]{1,0:T(4,128)S(1)}, f32[3,192]{1,0:T(4,128)S(1)}, u32[]{:S(2)}, u32[]{:S(2)}) collective-permute-start(f32[3,192]{1,0:T(4,128)S(1)} %pad_maximum_fusion.6), channel_id=1, source_target_pairs={{0,8},{1,9},{2,10},{3,11},{4,12},{5,13},{6,14},{7,15},{8,0},{9,1},... | collective-permute-start | bytes 6920 | tf_op jit(solution)/shard_map/softmax_stats_exchange/ppermute | solution.py:48
  125.0 3.5 %collective-permute-done.6 = f32[3,192]{1,0:T(4,128)S(1)} collective-permute-done((f32[3,192]{1,0:T(4,128)S(1)}, f32[3,192]{1,0:T(4,128)S(1)}, u32[]{:S(2)}, u32[]{:S(2)}) %collective-permute-start.6) | collective-permute-done | bytes 2336 | tf_op jit(solution)/shard_map/softmax_stats_exchange/ppermute | solution.py:48
  128.6 3.2 %collective-permute-start.7 = (f32[3,192]{1,0:T(4,128)S(1)}, f32[3,192]{1,0:T(4,128)S(1)}, u32[]{:S(2)}, u32[]{:S(2)}) collective-permute-start(f32[3,192]{1,0:T(4,128)S(1)} %pad_maximum_fusion.8), channel_id=1, source_target_pairs={{0,128},{64,192},{128,0},{192,64},{256,384},{320,448},{384,256},{4... | collective-permute-start | bytes 6920 | tf_op jit(solution)/shard_map/softmax_stats_exchange/ppermute | solution.py:48
  131.8 3.1 collective-permute-done.7
  135.0 4.9 %collective-permute-start.8 = (f32[3,192]{1,0:T(4,128)S(1)}, f32[3,192]{1,0:T(4,128)S(1)}, u32[]{:S(2)}, u32[]{:S(2)}) collective-permute-start(f32[3,192]{1,0:T(4,128)S(1)} %get-tuple-element.57), channel_id=1, source_target_pairs={{0,256},{64,320},{128,384},{192,448},{256,512},{320,576},{384,640}... | collective-permute-start | bytes 6920 | tf_op jit(solution)/shard_map/softmax_stats_exchange/ppermute | solution.py:58
  139.9 4.9 %collective-permute-start.9 = (f32[3,192]{1,0:T(4,128)S(1)}, f32[3,192]{1,0:T(4,128)S(1)}, u32[]{:S(2)}, u32[]{:S(2)}) collective-permute-start(f32[3,192]{1,0:T(4,128)S(1)} %get-tuple-element.57), channel_id=1, source_target_pairs={{0,512},{64,576},{128,640},{192,704},{256,0},{320,64},{384,128},{4... | collective-permute-start | bytes 6920 | tf_op jit(solution)/shard_map/softmax_stats_exchange/ppermute | solution.py:58
  144.8 4.5 %collective-permute-done.9 = f32[3,192]{1,0:T(4,128)S(1)} collective-permute-done((f32[3,192]{1,0:T(4,128)S(1)}, f32[3,192]{1,0:T(4,128)S(1)}, u32[]{:S(2)}, u32[]{:S(2)}) %collective-permute-start.9) | collective-permute-done | bytes 2336 | tf_op jit(solution)/shard_map/softmax_stats_exchange/ppermute | solution.py:58
  152.3 4.4 %copy.23 = f32[12,16,64,128]{3,1,2,0:T(8,128)S(1)} copy(f32[12,16,64,128]{3,2,1,0:T(8,128)S(1)} %bitcast.78) | data formatting | bytes 12582912 | tf_op jit(solution)/shard_map/reshape | solution.py:125
  162.2 5.9 %collective-permute-done.10 = f32[3,2,2,2,2,2,2,2,16,128]{9,8,7,6,5,4,3,2,1,0:T(8,128)} collective-permute-done((f32[3,2,2,2,2,2,2,2,16,128]{9,8,7,6,5,4,3,2,1,0:T(8,128)}, f32[3,2,2,2,2,2,2,2,16,128]{9,8,7,6,5,4,3,2,1,0:T(8,128)}, u32[]{:S(2)}, u32[]{:S(2)}) %collective-permute-start.10) | collective-permute-done | bytes 3145760 | tf_op jit(solution)/shard_map/grad_rows_reduce_scatter/ppermute | solution.py:78
  168.1 4.0 %bitcast_add_fusion = f32[3,2,2,2,2,2,2,2,16,128]{9,8,7,6,5,4,3,2,1,0:T(8,128)S(1)} fusion(f32[3,2,2,2,2,2,2,2,16,128]{9,8,7,6,5,4,3,2,1,0:T(8,128)} %collective-permute-done.10, f32[3,2,2,2,2,2,2,2,2,16,128]{10,9,8,7,6,5,4,3,2,1,0:T(8,128)} %bitcast.77, s32[]{:T(128)S(6)} %select_n.254), kind=kLoop, calls=%fused_computation.2 | loop fusion | flops 786432 | bytes 9437188 | tf_op jit(solution)/shard_map/grad_rows_reduce_scatter/add | solution.py:78
  175.1 3.4 %collective-permute-start.11 = (f32[3,2,2,2,2,2,2,16,128]{8,7,6,5,4,3,2,1,0:T(8,128)}, f32[3,2,2,2,2,2,2,16,128]{8,7,6,5,4,3,2,1,0:T(8,128)}, u32[]{:S(2)}, u32[]{:S(2)}) collective-permute-start(f32[3,2,2,2,2,2,2,16,128]{8,7,6,5,4,3,2,1,0:T(8,128)} %dynamic-slice_bitcast_fusion.1), channel_id=1, source_target_pairs={{0,2},{1,3},{2,0},{3,1},{4,6},{5,7},{6,4},{7,5},{8,10},{9,11},{10,... | collective-permute-start | bytes 4718600 | tf_op jit(solution)/shard_map/grad_rows_reduce_scatter/ppermute | solution.py:78
  178.5 35.2 %collective-permute-done.11 = f32[3,2,2,2,2,2,2,16,128]{8,7,6,5,4,3,2,1,0:T(8,128)} collective-permute-done((f32[3,2,2,2,2,2,2,16,128]{8,7,6,5,4,3,2,1,0:T(8,128)}, f32[3,2,2,2,2,2,2,16,128]{8,7,6,5,4,3,2,1,0:T(8,128)}, u32[]{:S(2)}, u32[]{:S(2)}) %collective-permute-start.11) | collective-permute-done | bytes 1572896 | tf_op jit(solution)/shard_map/grad_rows_reduce_scatter/ppermute | solution.py:78
  217.1 2.9 collective-permute-start.12
  220.1 17.8 %collective-permute-done.12 = f32[3,2,2,2,2,2,16,128]{7,6,4,3,2,1,0,5:T(8,128)} collective-permute-done((f32[3,2,2,2,2,2,16,128]{7,6,4,3,2,1,0,5:T(8,128)S(1)}, f32[3,2,2,2,2,2,16,128]{7,6,4,3,2,1,0,5:T(8,128)}, u32[]{:S(2)}, u32[]{:S(2)}) %collective-permute-start.12) | collective-permute-done | bytes 786464 | tf_op jit(solution)/shard_map/grad_rows_reduce_scatter/ppermute | solution.py:78
  239.4 4.3 %collective-permute-start.13 = (f32[3,2,2,2,2,16,128]{6,5,4,3,2,1,0:T(8,128)S(1)}, f32[3,2,2,2,2,16,128]{6,5,4,3,2,1,0:T(8,128)}, u32[]{:S(2)}, u32[]{:S(2)}) collective-permute-start(f32[3,2,2,2,2,16,128]{6,5,4,3,2,1,0:T(8,128)S(1)} %dynamic-slice_bitcast_fusion.2), channel_id=1, source_target_pairs={{0,4},{1,5},{2,6},{3,7},{4,0},{5,1},{6,2},{7,3},{8,12},{9,13},{10,... | collective-permute-start | bytes 1179656 | tf_op jit(solution)/shard_map/grad_rows_reduce_scatter/ppermute | solution.py:78
  243.8 16.4 %collective-permute-done.13 = f32[3,2,2,2,2,16,128]{6,5,4,3,2,1,0:T(8,128)} collective-permute-done((f32[3,2,2,2,2,16,128]{6,5,4,3,2,1,0:T(8,128)S(1)}, f32[3,2,2,2,2,16,128]{6,5,4,3,2,1,0:T(8,128)}, u32[]{:S(2)}, u32[]{:S(2)}) %collective-permute-start.13) | collective-permute-done | bytes 393248 | tf_op jit(solution)/shard_map/grad_rows_reduce_scatter/ppermute | solution.py:78
  261.2 3.4 %collective-permute-start.14 = (f32[3,2,2,2,16,128]{5,4,3,2,1,0:T(8,128)S(1)}, f32[3,2,2,2,16,128]{5,4,3,2,1,0:T(8,128)S(1)}, u32[]{:S(2)}, u32[]{:S(2)}) collective-permute-start(f32[3,2,2,2,16,128]{5,4,3,2,1,0:T(8,128)S(1)} %dynamic-slice_bitcast_fusion.3), channel_id=1, source_target_pairs={{0,32},{1,33},{2,34},{3,35},{4,36},{5,37},{6,38},{7,39},{8,40},{9,... | collective-permute-start | bytes 589832 | tf_op jit(solution)/shard_map/grad_rows_reduce_scatter/ppermute | solution.py:78
  264.6 5.8 %collective-permute-done.14 = f32[3,2,2,2,16,128]{5,4,3,2,1,0:T(8,128)S(1)} collective-permute-done((f32[3,2,2,2,16,128]{5,4,3,2,1,0:T(8,128)S(1)}, f32[3,2,2,2,16,128]{5,4,3,2,1,0:T(8,128)S(1)}, u32[]{:S(2)}, u32[]{:S(2)}) %collective-permute-start.14) | collective-permute-done | bytes 196640 | tf_op jit(solution)/shard_map/grad_rows_reduce_scatter/ppermute | solution.py:78
  270.5 8.3 %collective-permute-start.15 = (f32[3,2,2,16,128]{4,3,1,0,2:T(8,128)S(1)}, f32[3,2,2,16,128]{4,3,1,0,2:T(8,128)S(1)}, u32[]{:S(2)}, u32[]{:S(2)}) collective-permute-start(f32[3,2,2,16,128]{4,3,1,0,2:T(8,128)S(1)} %bitcast.80), channel_id=1, source_target_pairs={{0,8},{1,9},{2,10},{3,11},{4,12},{5,13},{6,14},{7,15},{8,0},{9,1},... | collective-permute-start | bytes 294920 | tf_op jit(solution)/shard_map/grad_rows_reduce_scatter/ppermute | solution.py:78
  278.9 3.6 %collective-permute-done.15 = f32[3,2,2,16,128]{4,3,1,0,2:T(8,128)S(1)} collective-permute-done((f32[3,2,2,16,128]{4,3,1,0,2:T(8,128)S(1)}, f32[3,2,2,16,128]{4,3,1,0,2:T(8,128)S(1)}, u32[]{:S(2)}, u32[]{:S(2)}) %collective-permute-start.15) | collective-permute-done | bytes 98336 | tf_op jit(solution)/shard_map/grad_rows_reduce_scatter/ppermute | solution.py:78
  288.5 3.3 %collective-permute-start.17 = (f32[3,16,128]{2,1,0:T(8,128)S(1)}, f32[3,16,128]{2,1,0:T(8,128)S(1)}, u32[]{:S(2)}, u32[]{:S(2)}) collective-permute-start(f32[3,16,128]{2,1,0:T(8,128)S(1)} %dynamic-slice_bitcast_fusion.5), channel_id=1, source_target_pairs={{0,128},{64,192},{128,0},{192,64},{256,384},{320,448},{384,256},{4... | collective-permute-start | bytes 73736 | tf_op jit(solution)/shard_map/grad_rows_reduce_scatter/ppermute | solution.py:78
  291.9 4.6 %convolution_convert_fusion = bf16[8192,128]{1,0:T(8,128)(2,1)} fusion(bf16[192,8192]{1,0:T(8,128)(2,1)} %all-gather.2.cloned.1.call-done, f32[192,128]{1,0:T(8,128)S(1)} %get-tuple-element.59, f32[192]{0:T(256)S(1)} %fusion.15, f32[192]{0:T(256)S(1)} %get-tuple-element.6), kind=kOutput, calls=%fused_computation.1 | convolution fusion | flops 403775488 | bytes 5342720 | tf_op jit(solution)/shard_map/dot_general | solution.py:119
  296.5 4.9 %collective-permute-start.18 = (f32[16,128]{1,0:T(8,128)S(1)}, f32[16,128]{1,0:T(8,128)S(1)}, u32[]{:S(2)}, u32[]{:S(2)}) collective-permute-start(f32[16,128]{1,0:T(8,128)S(1)} %get-tuple-element.28), channel_id=1, source_target_pairs={{0,256},{64,320},{128,384},{192,448},{256,512},{320,576},{384,640}... | collective-permute-start | bytes 24584 | tf_op jit(solution)/shard_map/grad_rows_reduce_scatter/ppermute | solution.py:85
  301.4 4.8 %collective-permute-start.19 = (f32[16,128]{1,0:T(8,128)S(1)}, f32[16,128]{1,0:T(8,128)S(1)}, u32[]{:S(2)}, u32[]{:S(2)}) collective-permute-start(f32[16,128]{1,0:T(8,128)S(1)} %get-tuple-element.29), channel_id=1, source_target_pairs={{0,512},{64,576},{128,640},{192,704},{256,0},{320,64},{384,128},{4... | collective-permute-start | bytes 24584 | tf_op jit(solution)/shard_map/grad_rows_reduce_scatter/ppermute | solution.py:85
  306.9 4.0 %collective-permute-done.19 = f32[16,128]{1,0:T(8,128)S(1)} collective-permute-done((f32[16,128]{1,0:T(8,128)S(1)}, f32[16,128]{1,0:T(8,128)S(1)}, u32[]{:S(2)}, u32[]{:S(2)}) %collective-permute-start.19) | collective-permute-done | bytes 8224 | tf_op jit(solution)/shard_map/grad_rows_reduce_scatter/ppermute | solution.py:85
  (85 shorter events, 43.0 us)
Async XLA Ops:
  7.2 75.4 %copy-start = (bf16[8192,128]{1,0:T(8,128)(2,1)S(1)}, bf16[8192,128]{1,0:T(8,128)(2,1)}, u32[]{:S(2)}) copy-start(bf16[8192,128]{1,0:T(8,128)(2,1)} %param.7) | copy-start | bytes 6291460
  7.2 75.4 %all-gather.2.cloned.1.call-start = ((), (), s32[]{:S(2)}) async-start(), calls=%async_computation | async-start | bytes 3407872 | tf_op jit(solution)/shard_map/all_gather | solution.py:102
  11.1 74.5 %copy-start.3 = (s32[192]{0:T(256)S(1)}, s32[192]{0:T(256)}, u32[]{:S(2)}) copy-start(s32[192]{0:T(256)} %param.6) | copy-start | bytes 2308
  85.8 3.1 collective-permute-start
  88.9 5.5 %collective-permute-start.1 = (f32[3,192]{1,0:T(4,128)S(1)}, f32[3,192]{1,0:T(4,128)S(1)}, u32[]{:S(2)}, u32[]{:S(2)}) collective-permute-start(f32[3,192]{1,0:T(4,128)S(1)} %pad_maximum_fusion.2), channel_id=1, source_target_pairs={{0,2},{1,3},{2,0},{3,1},{4,6},{5,7},{6,4},{7,5},{8,10},{9,11},{10,... | collective-permute-start | bytes 6920 | tf_op jit(solution)/shard_map/softmax_stats_exchange/ppermute | solution.py:48
  94.5 5.5 %collective-permute-start.2 = (f32[3,192]{1,0:T(4,128)S(1)}, f32[3,192]{1,0:T(4,128)S(1)}, u32[]{:S(2)}, u32[]{:S(2)}) collective-permute-start(f32[3,192]{1,0:T(4,128)S(1)} %pad_maximum_fusion.3), channel_id=1, source_target_pairs={{0,16},{1,17},{2,18},{3,19},{4,20},{5,21},{6,22},{7,23},{8,24},{9,... | collective-permute-start | bytes 6920 | tf_op jit(solution)/shard_map/softmax_stats_exchange/ppermute | solution.py:48
  100.1 6.4 %collective-permute-start.3 = (f32[3,192]{1,0:T(4,128)S(1)}, f32[3,192]{1,0:T(4,128)S(1)}, u32[]{:S(2)}, u32[]{:S(2)}) collective-permute-start(f32[3,192]{1,0:T(4,128)S(1)} %pad_maximum_fusion.4), channel_id=1, source_target_pairs={{0,4},{1,5},{2,6},{3,7},{4,0},{5,1},{6,2},{7,3},{8,12},{9,13},{10,... | collective-permute-start | bytes 6920 | tf_op jit(solution)/shard_map/softmax_stats_exchange/ppermute | solution.py:48
  106.5 7.0 %collective-permute-start.4 = (f32[3,192]{1,0:T(4,128)S(1)}, f32[3,192]{1,0:T(4,128)S(1)}, u32[]{:S(2)}, u32[]{:S(2)}) collective-permute-start(f32[3,192]{1,0:T(4,128)S(1)} %pad_maximum_fusion.5), channel_id=1, source_target_pairs={{0,32},{1,33},{2,34},{3,35},{4,36},{5,37},{6,38},{7,39},{8,40},{9,... | collective-permute-start | bytes 6920 | tf_op jit(solution)/shard_map/softmax_stats_exchange/ppermute | solution.py:48
  113.6 9.4 %collective-permute-start.5 = (f32[3,192]{1,0:T(4,128)S(1)}, f32[3,192]{1,0:T(4,128)S(1)}, u32[]{:S(2)}, u32[]{:S(2)}) collective-permute-start(f32[3,192]{1,0:T(4,128)S(1)} %pad_maximum_fusion.6), channel_id=1, source_target_pairs={{0,8},{1,9},{2,10},{3,11},{4,12},{5,13},{6,14},{7,15},{8,0},{9,1},... | collective-permute-start | bytes 6920 | tf_op jit(solution)/shard_map/softmax_stats_exchange/ppermute | solution.py:48
  123.0 5.5 %collective-permute-start.6 = (f32[3,192]{1,0:T(4,128)S(1)}, f32[3,192]{1,0:T(4,128)S(1)}, u32[]{:S(2)}, u32[]{:S(2)}) collective-permute-start(f32[3,192]{1,0:T(4,128)S(1)} %pad_maximum_fusion.7), channel_id=1, source_target_pairs={{0,64},{64,0},{128,192},{192,128},{256,320},{320,256},{384,448},{4... | collective-permute-start | bytes 6920 | tf_op jit(solution)/shard_map/softmax_stats_exchange/ppermute | solution.py:48
  128.6 6.4 %collective-permute-start.7 = (f32[3,192]{1,0:T(4,128)S(1)}, f32[3,192]{1,0:T(4,128)S(1)}, u32[]{:S(2)}, u32[]{:S(2)}) collective-permute-start(f32[3,192]{1,0:T(4,128)S(1)} %pad_maximum_fusion.8), channel_id=1, source_target_pairs={{0,128},{64,192},{128,0},{192,64},{256,384},{320,448},{384,256},{4... | collective-permute-start | bytes 6920 | tf_op jit(solution)/shard_map/softmax_stats_exchange/ppermute | solution.py:48
  135.0 9.8 %collective-permute-start.8 = (f32[3,192]{1,0:T(4,128)S(1)}, f32[3,192]{1,0:T(4,128)S(1)}, u32[]{:S(2)}, u32[]{:S(2)}) collective-permute-start(f32[3,192]{1,0:T(4,128)S(1)} %get-tuple-element.57), channel_id=1, source_target_pairs={{0,256},{64,320},{128,384},{192,448},{256,512},{320,576},{384,640}... | collective-permute-start | bytes 6920 | tf_op jit(solution)/shard_map/softmax_stats_exchange/ppermute | solution.py:58
  139.9 9.4 %collective-permute-start.9 = (f32[3,192]{1,0:T(4,128)S(1)}, f32[3,192]{1,0:T(4,128)S(1)}, u32[]{:S(2)}, u32[]{:S(2)}) collective-permute-start(f32[3,192]{1,0:T(4,128)S(1)} %get-tuple-element.57), channel_id=1, source_target_pairs={{0,512},{64,576},{128,640},{192,704},{256,0},{320,64},{384,128},{4... | collective-permute-start | bytes 6920 | tf_op jit(solution)/shard_map/softmax_stats_exchange/ppermute | solution.py:58
  156.7 3.6 %copy-start.1 = (f32[12,16,64,128]{3,1,2,0:T(8,128)}, f32[12,16,64,128]{3,1,2,0:T(8,128)S(1)}, u32[]{:S(2)}) copy-start(f32[12,16,64,128]{3,1,2,0:T(8,128)S(1)} %copy.23) | copy-start | bytes 18874372
  160.3 7.9 %collective-permute-start.10 = (f32[3,2,2,2,2,2,2,2,16,128]{9,8,7,6,5,4,3,2,1,0:T(8,128)}, f32[3,2,2,2,2,2,2,2,16,128]{9,8,7,6,5,4,3,2,1,0:T(8,128)}, u32[]{:S(2)}, u32[]{:S(2)}) collective-permute-start(f32[3,2,2,2,2,2,2,2,16,128]{9,8,7,6,5,4,3,2,1,0:T(8,128)} %dynamic-slice_bitcast_fusion), channel_id=1, source_target_pairs={{0,1},{1,0},{2,3},{3,2},{4,5},{5,4},{6,7},{7,6},{8,9},{9,8},{10,11... | collective-permute-start | bytes 9437192 | tf_op jit(solution)/shard_map/grad_rows_reduce_scatter/ppermute | solution.py:78
  172.1 1.6 copy-start.2
  175.1 38.6 %collective-permute-start.11 = (f32[3,2,2,2,2,2,2,16,128]{8,7,6,5,4,3,2,1,0:T(8,128)}, f32[3,2,2,2,2,2,2,16,128]{8,7,6,5,4,3,2,1,0:T(8,128)}, u32[]{:S(2)}, u32[]{:S(2)}) collective-permute-start(f32[3,2,2,2,2,2,2,16,128]{8,7,6,5,4,3,2,1,0:T(8,128)} %dynamic-slice_bitcast_fusion.1), channel_id=1, source_target_pairs={{0,2},{1,3},{2,0},{3,1},{4,6},{5,7},{6,4},{7,5},{8,10},{9,11},{10,... | collective-permute-start | bytes 4718600 | tf_op jit(solution)/shard_map/grad_rows_reduce_scatter/ppermute | solution.py:78
  217.1 20.8 %collective-permute-start.12 = (f32[3,2,2,2,2,2,16,128]{7,6,4,3,2,1,0,5:T(8,128)S(1)}, f32[3,2,2,2,2,2,16,128]{7,6,4,3,2,1,0,5:T(8,128)}, u32[]{:S(2)}, u32[]{:S(2)}) collective-permute-start(f32[3,2,2,2,2,2,16,128]{7,6,4,3,2,1,0,5:T(8,128)S(1)} %bitcast.79), channel_id=1, source_target_pairs={{0,16},{1,17},{2,18},{3,19},{4,20},{5,21},{6,22},{7,23},{8,24},{9,... | collective-permute-start | bytes 2359304 | tf_op jit(solution)/shard_map/grad_rows_reduce_scatter/ppermute | solution.py:78
  239.4 20.7 %collective-permute-start.13 = (f32[3,2,2,2,2,16,128]{6,5,4,3,2,1,0:T(8,128)S(1)}, f32[3,2,2,2,2,16,128]{6,5,4,3,2,1,0:T(8,128)}, u32[]{:S(2)}, u32[]{:S(2)}) collective-permute-start(f32[3,2,2,2,2,16,128]{6,5,4,3,2,1,0:T(8,128)S(1)} %dynamic-slice_bitcast_fusion.2), channel_id=1, source_target_pairs={{0,4},{1,5},{2,6},{3,7},{4,0},{5,1},{6,2},{7,3},{8,12},{9,13},{10,... | collective-permute-start | bytes 1179656 | tf_op jit(solution)/shard_map/grad_rows_reduce_scatter/ppermute | solution.py:78
  261.2 9.2 %collective-permute-start.14 = (f32[3,2,2,2,16,128]{5,4,3,2,1,0:T(8,128)S(1)}, f32[3,2,2,2,16,128]{5,4,3,2,1,0:T(8,128)S(1)}, u32[]{:S(2)}, u32[]{:S(2)}) collective-permute-start(f32[3,2,2,2,16,128]{5,4,3,2,1,0:T(8,128)S(1)} %dynamic-slice_bitcast_fusion.3), channel_id=1, source_target_pairs={{0,32},{1,33},{2,34},{3,35},{4,36},{5,37},{6,38},{7,39},{8,40},{9,... | collective-permute-start | bytes 589832 | tf_op jit(solution)/shard_map/grad_rows_reduce_scatter/ppermute | solution.py:78
  270.5 12.0 %collective-permute-start.15 = (f32[3,2,2,16,128]{4,3,1,0,2:T(8,128)S(1)}, f32[3,2,2,16,128]{4,3,1,0,2:T(8,128)S(1)}, u32[]{:S(2)}, u32[]{:S(2)}) collective-permute-start(f32[3,2,2,16,128]{4,3,1,0,2:T(8,128)S(1)} %bitcast.80), channel_id=1, source_target_pairs={{0,8},{1,9},{2,10},{3,11},{4,12},{5,13},{6,14},{7,15},{8,0},{9,1},... | collective-permute-start | bytes 294920 | tf_op jit(solution)/shard_map/grad_rows_reduce_scatter/ppermute | solution.py:78
  282.5 6.0 %collective-permute-start.16 = (f32[3,2,16,128]{3,2,1,0:T(8,128)S(1)}, f32[3,2,16,128]{3,2,1,0:T(8,128)S(1)}, u32[]{:S(2)}, u32[]{:S(2)}) collective-permute-start(f32[3,2,16,128]{3,2,1,0:T(8,128)S(1)} %dynamic-slice_bitcast_fusion.4), channel_id=1, source_target_pairs={{0,64},{64,0},{128,192},{192,128},{256,320},{320,256},{384,448},{4... | collective-permute-start | bytes 147464 | tf_op jit(solution)/shard_map/grad_rows_reduce_scatter/ppermute | solution.py:78
  288.5 8.0 %collective-permute-start.17 = (f32[3,16,128]{2,1,0:T(8,128)S(1)}, f32[3,16,128]{2,1,0:T(8,128)S(1)}, u32[]{:S(2)}, u32[]{:S(2)}) collective-permute-start(f32[3,16,128]{2,1,0:T(8,128)S(1)} %dynamic-slice_bitcast_fusion.5), channel_id=1, source_target_pairs={{0,128},{64,192},{128,0},{192,64},{256,384},{320,448},{384,256},{4... | collective-permute-start | bytes 73736 | tf_op jit(solution)/shard_map/grad_rows_reduce_scatter/ppermute | solution.py:78
  296.5 10.3 %collective-permute-start.18 = (f32[16,128]{1,0:T(8,128)S(1)}, f32[16,128]{1,0:T(8,128)S(1)}, u32[]{:S(2)}, u32[]{:S(2)}) collective-permute-start(f32[16,128]{1,0:T(8,128)S(1)} %get-tuple-element.28), channel_id=1, source_target_pairs={{0,256},{64,320},{128,384},{192,448},{256,512},{320,576},{384,640}... | collective-permute-start | bytes 24584 | tf_op jit(solution)/shard_map/grad_rows_reduce_scatter/ppermute | solution.py:85
  301.4 9.5 %collective-permute-start.19 = (f32[16,128]{1,0:T(8,128)S(1)}, f32[16,128]{1,0:T(8,128)S(1)}, u32[]{:S(2)}, u32[]{:S(2)}) collective-permute-start(f32[16,128]{1,0:T(8,128)S(1)} %get-tuple-element.29), channel_id=1, source_target_pairs={{0,512},{64,576},{128,640},{192,704},{256,0},{320,64},{384,128},{4... | collective-permute-start | bytes 24584 | tf_op jit(solution)/shard_map/grad_rows_reduce_scatter/ppermute | solution.py:85
Sparse Core Ops, SparseCore 0:
  11.2 71.3 all-gather.1

commit v4 on v3

--- a/solution.py
+++ b/solution.py
@@ -4,6 +4,25 @@
 from jax.sharding import PartitionSpec as P
 
 TENSOR_MASK_ORDER = (1, 2, 16, 4, 32, 8)
+
+
+def tensor_geometry(count):
+    along_y = min(8, count // 2)
+    return count // 2 // along_y, along_y
+
+
+def labelled(index, count):
+    n_x, n_y = tensor_geometry(count)
+    core, chip = index % 2, index // 2
+    x, y = chip // n_y, chip % n_y
+    return ((x + core) % n_x * n_y + (y + core) % n_y) * 2 + core
+
+
+def unlabelled(label, count):
+    n_x, n_y = tensor_geometry(count)
+    core, chip = label % 2, label // 2
+    x, y = chip // n_y, chip % n_y
+    return ((x - core) % n_x * n_y + (y - core) % n_y) * 2 + core
 
 
 def split_pow2(count):
@@ -68,14 +87,28 @@
     s_bits = low.bit_length() - 1
     labels = ["group"] + [("section", 1 << j) for j in reversed(range(s_bits))]
     labels += [("tensor", 1 << j) for j in reversed(range(t_bits))]
-    value = blocks.reshape((groups,) + (2,) * (s_bits + t_bits) + blocks.shape[2:])
+    n_x, n_y = tensor_geometry(n_ten)
+    chips = blocks.reshape((n_sec, n_x, n_y, 2) + blocks.shape[2:])
+    shifted = jnp.roll(chips[:, :, :, 1], shift=(1, 1), axis=(1, 2))
+    chips = jnp.stack([chips[:, :, :, 0], shifted], axis=3)
+    value = chips.reshape((groups,) + (2,) * (s_bits + t_bits) + blocks.shape[2:])
     steps = [("tensor", m) for m in tensor_masks(n_ten)] + [("section", m) for m in section_masks(n_sec)]
+    t = lax.axis_index("tensor")
+    core = t % 2
+    chip = t // 2
+    t_label = (((chip // n_y) + core) % n_x * n_y + ((chip % n_y) + core) % n_y) * 2 + core
     for name, mask in steps:
         axis = labels.index((name, mask))
-        mine = (lax.axis_index(name) & mask) // mask
+        size = lax.axis_size(name)
+        if name == "tensor":
+            mine = (t_label & mask) // mask
+            pairs = [(i, unlabelled(labelled(i, size) ^ mask, size)) for i in range(size)]
+        else:
+            mine = (lax.axis_index(name) & mask) // mask
+            pairs = xor_pairs(size, mask)
         keep = lax.dynamic_index_in_dim(value, mine, axis, keepdims=False)
         sent = lax.dynamic_index_in_dim(value, 1 - mine, axis, keepdims=False)
-        value = keep + lax.ppermute(sent, name, xor_pairs(lax.axis_size(name), mask))
+        value = keep + lax.ppermute(sent, name, pairs)
         labels.pop(axis)
     group = lax.axis_index("section") // low
     total = lax.dynamic_index_in_dim(value, group, 0, keepdims=False)
@@ -99,7 +132,18 @@
     normed_rows = lax.dynamic_slice_in_dim(
         normed_part, lax.axis_index("tensor") * feature_width, feature_width, 1
     )
-    normed = lax.all_gather(normed_part, "section", axis=0, tiled=True)
+    core = lax.axis_index("tensor") % 2
+    half = normed_part.shape[1] // 2
+    with jax.named_scope("normed_rows_gather"):
+        own_half = lax.all_gather(
+            lax.dynamic_slice_in_dim(normed_part, core * half, half, 1), "section", axis=0, tiled=True
+        )
+        other_half = lax.ppermute(own_half, "tensor", xor_pairs(n_ten, 1))
+    normed = jnp.where(
+        core == 0,
+        jnp.concatenate([own_half, other_half], axis=1),
+        jnp.concatenate([other_half, own_half], axis=1),
+    )
     logits = jnp.dot(normed, out_weight, preferred_element_type=jnp.float32)
     shard_width = out_weight.shape[1]
     offset = (lax.axis_index("section") * n_ten + lax.axis_index("tensor")) * shard_width

time: 319 us -> 349 us (1.094)
  local copies, waits for them, and re-layouts: 15.2 us -> 35.3 us
  waiting for transfers between devices: 188 us -> 196 us
    slice x0 -> x3, local copies, waits for them, and re-layouts: none -> 17.1 us  [reduce_scatter_blocks(): shifted = jnp.roll(chips[:, :, :, 1], shift=(1, 1), axis=(1, 2))]
    ppermute x8 -> x9, waiting for transfers between devices: 87.3 us -> 100 us  [the longest x8 96.8 us: reduce_scatter_blocks(): value = keep + lax.ppermute(sent, name, pairs)]
    unnamed x9 -> x14, local copies, waits for them, and re-layouts: 3.93 us -> 9.73 us
    reshape x1 -> x0, local copies, waits for them, and re-layouts: 4.35 us -> none  [local(): grad_term.reshape(n_sec, rows_per_sec, n_ten, feature_width)]
    all_gather x1, waiting for transfers between devices: 71.5 us -> 67.2 us  [local(): lax.all_gather(lax.dynamic_slice_in_dim(normed_part, core * half, half, 1...]
    ppermute x8 -> x9, starting transfers between devices: 29.7 us -> 27.5 us  [the longest x8 25.6 us: reduce_scatter_blocks(): value = keep + lax.ppermute(sent, name, pairs)]
  transfers between devices with their start and end apart: 21 -> 22, of which waited for: 18 -> 19; matrix products, arithmetic and copies ran while one was open for 2% -> 2% of each run, Pallas kernels for 0% -> 0%
where the time goes in v4:
time: 349 us; the launch traced here: 347 us
  waiting for transfers between devices  196 us (56%)
  starting transfers between devices  75.4 us (22%)
  local copies, waits for them, and re-layouts  35.3 us (10%)
  between operations  14.9 us (4%)
  other arithmetic  14.3 us (4%)
  matrix products  10.9 us (3%)
    ppermute x8, waiting for transfers between devices, reduce_scatter_blocks(): value = keep + lax.ppermute(sent, name, pairs)  96.8 us
    all_gather x1, waiting for transfers between devices, local(): lax.all_gather(lax.dynamic_slice_in_dim(normed_part, core * half, half, 1...  67.2 us
    ppermute x8, starting transfers between devices, exchange_stats(): other = lax.ppermute(stats, name, xor_pairs(lax.axis_size(name), mask))  28.2 us
    ppermute x8, starting transfers between devices, reduce_scatter_blocks(): value = keep + lax.ppermute(sent, name, pairs)  25.6 us
    ppermute x8, waiting for transfers between devices, exchange_stats(): other = lax.ppermute(stats, name, xor_pairs(lax.axis_size(name), mask))  20.3 us
    slice x3, local copies, waits for them, and re-layouts, reduce_scatter_blocks(): shifted = jnp.roll(chips[:, :, :, 1], shift=(1, 1), axis=(1, 2))  17.1 us
    ppermute x2, starting transfers between devices, exchange_stats(): received.append(lax.ppermute(stats, 'section', pairs))  9.93 us
    ppermute x2, starting transfers between devices, reduce_scatter_blocks(): total = total + lax.ppermute(sent, 'section', pairs)  9.75 us
  transfers between devices with their start and end apart: 22, of which 19 were waited for; matrix products, arithmetic and copies ran while one was open for 2% of the time, Pallas kernels for 0%

profile of v4, /device:TPU:6, one launch (start us, length us, event | category | flops | bytes accessed | tf_op | source)
XLA Modules:
  0.0 347.0 jit_solution(16725596017928329091)
XLA Ops:
  11.0 67.2 %all-gather.2.cloned.1.call-done = bf16[192,4096]{1,0:T(8,128)(2,1)} async-done(((bf16[16,4096]{1,0:T(8,128)(2,1)}), bf16[192,4096]{1,0:T(8,128)(2,1)}) %all-gather.2.cloned.1.call-update) | async-done | bytes 1572880 | tf_op jit(solution)/shard_map/normed_rows_gather/all_gather | solution.py:138
  80.2 3.7 %collective-permute-done = bf16[192,4096]{1,0:T(8,128)(2,1)} collective-permute-done((bf16[192,4096]{1,0:T(8,128)(2,1)}, bf16[192,4096]{1,0:T(8,128)(2,1)}, u32[]{:S(2)}, u32[]{:S(2)}) %collective-permute-start) | collective-permute-done | bytes 1572896 | tf_op jit(solution)/shard_map/normed_rows_gather/ppermute | solution.py:141
  83.9 4.1 %fusion.31 = (f32[192]{0:T(256)S(1)}, f32[192,128]{1,0:T(8,128)S(1)}) fusion(bf16[8192,128]{1,0:T(8,128)(2,1)S(1)} %copy-done, bf16[192,4096]{1,0:T(8,128)(2,1)} %collective-permute-done, bf16[192,4096]{1,0:T(8,128)(2,1)} %all-gather.2.cloned.1.call-done, pred[]{:T(512)S(6)} %eq.26), kind=kOutput, calls=%fused_computation.138 | convolution fusion | flops 416833344 | bytes 5341953 | tf_op jit(solution)/shard_map/dot_general | solution.py:147
  91.4 3.4 collective-permute-start.2
  102.5 4.3 %collective-permute-start.4 = (f32[3,192]{1,0:T(4,128)S(1)}, f32[3,192]{1,0:T(4,128)S(1)}, u32[]{:S(2)}, u32[]{:S(2)}) collective-permute-start(f32[3,192]{1,0:T(4,128)S(1)} %pad_maximum_fusion.6), channel_id=1, source_target_pairs={{0,4},{1,5},{2,6},{3,7},{4,0},{5,1},{6,2},{7,3},{8,12},{9,13},{10,... | collective-permute-start | bytes 6920 | tf_op jit(solution)/shard_map/softmax_stats_exchange/ppermute | solution.py:67
  109.0 3.4 collective-permute-start.5
  112.3 3.6 %collective-permute-done.5 = f32[3,192]{1,0:T(4,128)S(1)} collective-permute-done((f32[3,192]{1,0:T(4,128)S(1)}, f32[3,192]{1,0:T(4,128)S(1)}, u32[]{:S(2)}, u32[]{:S(2)}) %collective-permute-start.5) | collective-permute-done | bytes 2336 | tf_op jit(solution)/shard_map/softmax_stats_exchange/ppermute | solution.py:67
  116.0 7.4 %collective-permute-start.6 = (f32[3,192]{1,0:T(4,128)S(1)}, f32[3,192]{1,0:T(4,128)S(1)}, u32[]{:S(2)}, u32[]{:S(2)}) collective-permute-start(f32[3,192]{1,0:T(4,128)S(1)} %pad_maximum_fusion.8), channel_id=1, source_target_pairs={{0,8},{1,9},{2,10},{3,11},{4,12},{5,13},{6,14},{7,15},{8,0},{9,1},... | collective-permute-start | bytes 6920 | tf_op jit(solution)/shard_map/softmax_stats_exchange/ppermute | solution.py:67
  127.4 3.5 %collective-permute-done.7 = f32[3,192]{1,0:T(4,128)S(1)} collective-permute-done((f32[3,192]{1,0:T(4,128)S(1)}, f32[3,192]{1,0:T(4,128)S(1)}, u32[]{:S(2)}, u32[]{:S(2)}) %collective-permute-start.7) | collective-permute-done | bytes 2336 | tf_op jit(solution)/shard_map/softmax_stats_exchange/ppermute | solution.py:67
  131.0 3.0 collective-permute-start.8
  134.1 3.3 collective-permute-done.8
  137.5 4.8 %collective-permute-start.9 = (f32[3,192]{1,0:T(4,128)S(1)}, f32[3,192]{1,0:T(4,128)S(1)}, u32[]{:S(2)}, u32[]{:S(2)}) collective-permute-start(f32[3,192]{1,0:T(4,128)S(1)} %get-tuple-element.57), channel_id=1, source_target_pairs={{0,256},{64,320},{128,384},{192,448},{256,512},{320,576},{384,640}... | collective-permute-start | bytes 6920 | tf_op jit(solution)/shard_map/softmax_stats_exchange/ppermute | solution.py:77
  142.3 5.1 %collective-permute-start.10 = (f32[3,192]{1,0:T(4,128)S(1)}, f32[3,192]{1,0:T(4,128)S(1)}, u32[]{:S(2)}, u32[]{:S(2)}) collective-permute-start(f32[3,192]{1,0:T(4,128)S(1)} %get-tuple-element.57), channel_id=1, source_target_pairs={{0,512},{64,576},{128,640},{192,704},{256,0},{320,64},{384,128},{4... | collective-permute-start | bytes 6920 | tf_op jit(solution)/shard_map/softmax_stats_exchange/ppermute | solution.py:77
  147.5 4.2 %collective-permute-done.10 = f32[3,192]{1,0:T(4,128)S(1)} collective-permute-done((f32[3,192]{1,0:T(4,128)S(1)}, f32[3,192]{1,0:T(4,128)S(1)}, u32[]{:S(2)}, u32[]{:S(2)}) %collective-permute-start.10) | collective-permute-done | bytes 2336 | tf_op jit(solution)/shard_map/softmax_stats_exchange/ppermute | solution.py:77
  153.5 3.8 %copy.27 = f32[24,8,64,128]{3,2,1,0:T(8,128)} copy(f32[24,8,64,128]{3,1,2,0:T(8,128)S(1)} %convolution_bitcast_fusion) | data formatting | bytes 12582912
  157.3 13.9 %fusion.30 = (f32[12,4,8,1,16,128]{5,3,2,1,4,0:T(1,128)}, f32[12,4,8,1,16,128]{5,3,2,1,4,0:T(1,128)}) fusion(f32[12,4,8,2,16,128]{5,3,2,1,4,0:T(2,128)} %bitcast.77), kind=kLoop, calls=%fused_computation.137 | loop fusion | bytes 12582912 | tf_op jit(solution)/shard_map/grad_rows_reduce_scatter/slice | solution.py:92
  184.4 39.1 %collective-permute-done.11 = f32[3,2,2,2,2,2,2,2,16,128]{9,8,6,5,3,2,1,0,4,7:T(8,128)} collective-permute-done((f32[3,2,2,2,2,2,2,2,16,128]{9,8,6,5,3,2,1,0,4,7:T(8,128)}, f32[3,2,2,2,2,2,2,2,16,128]{9,8,6,5,3,2,1,0,4,7:T(8,128)}, u32[]{:S(2)}, u32[]{:S(2)}) %collective-permute-start.11) | collective-permute-done | bytes 3145760 | tf_op jit(solution)/shard_map/grad_rows_reduce_scatter/ppermute | solution.py:111
  223.4 3.9 %bitcast_add_fusion = f32[3,2,2,2,2,2,2,2,16,128]{9,8,6,5,3,2,1,0,4,7:T(8,128)S(1)} fusion(f32[3,2,2,2,2,2,2,2,16,128]{9,8,6,5,3,2,1,0,4,7:T(8,128)} %collective-permute-done.11, f32[3,2,2,2,2,2,2,2,2,16,128]{10,9,6,5,3,2,1,0,4,7,8:T(8,128)} %copy-done.1, s32[]{:T(128)S(6)} %select_n.298), kind=kLoop, calls=%fused_computation.6 | loop fusion | flops 786432 | bytes 9437188 | tf_op jit(solution)/shard_map/grad_rows_reduce_scatter/add | solution.py:111
  232.6 20.4 %collective-permute-done.12 = f32[3,2,2,2,2,2,2,16,128]{8,7,6,5,3,2,1,0,4:T(8,128)} collective-permute-done((f32[3,2,2,2,2,2,2,16,128]{8,7,6,5,3,2,1,0,4:T(8,128)}, f32[3,2,2,2,2,2,2,16,128]{8,7,6,5,3,2,1,0,4:T(8,128)}, u32[]{:S(2)}, u32[]{:S(2)}) %collective-permute-start.12) | collective-permute-done | bytes 1572896 | tf_op jit(solution)/shard_map/grad_rows_reduce_scatter/ppermute | solution.py:111
  259.2 11.2 %collective-permute-done.13 = f32[3,2,2,2,2,2,16,128]{7,6,5,4,3,2,1,0:T(8,128)} collective-permute-done((f32[3,2,2,2,2,2,16,128]{7,6,5,4,3,2,1,0:T(8,128)S(1)}, f32[3,2,2,2,2,2,16,128]{7,6,5,4,3,2,1,0:T(8,128)}, u32[]{:S(2)}, u32[]{:S(2)}) %collective-permute-start.13) | collective-permute-done | bytes 786464 | tf_op jit(solution)/shard_map/grad_rows_reduce_scatter/ppermute | solution.py:111
  272.7 3.1 collective-permute-start.14
  275.8 13.4 %collective-permute-done.14 = f32[3,2,2,2,2,16,128]{6,5,4,3,2,1,0:T(8,128)} collective-permute-done((f32[3,2,2,2,2,16,128]{6,5,4,3,2,1,0:T(8,128)}, f32[3,2,2,2,2,16,128]{6,5,4,3,2,1,0:T(8,128)}, u32[]{:S(2)}, u32[]{:S(2)}) %collective-permute-start.14) | collective-permute-done | bytes 393248 | tf_op jit(solution)/shard_map/grad_rows_reduce_scatter/ppermute | solution.py:111
  290.4 3.4 collective-permute-start.15
  293.8 5.7 %collective-permute-done.15 = f32[3,2,2,2,16,128]{5,4,2,1,0,3:T(8,128)S(1)} collective-permute-done((f32[3,2,2,2,16,128]{5,4,2,1,0,3:T(8,128)S(1)}, f32[3,2,2,2,16,128]{5,4,2,1,0,3:T(8,128)S(1)}, u32[]{:S(2)}, u32[]{:S(2)}) %collective-permute-start.15) | collective-permute-done | bytes 196640 | tf_op jit(solution)/shard_map/grad_rows_reduce_scatter/ppermute | solution.py:111
  299.5 6.5 %collective-permute-start.16 = (f32[3,2,2,16,128]{4,3,2,1,0:T(8,128)S(1)}, f32[3,2,2,16,128]{4,3,2,1,0:T(8,128)S(1)}, u32[]{:S(2)}, u32[]{:S(2)}) collective-permute-start(f32[3,2,2,16,128]{4,3,2,1,0:T(8,128)S(1)} %dynamic-slice_bitcast_fusion.4), channel_id=1, source_target_pairs={{0,8},{1,9},{2,10},{3,11},{4,12},{5,13},{6,14},{7,15},{8,0},{9,1},... | collective-permute-start | bytes 294920 | tf_op jit(solution)/shard_map/grad_rows_reduce_scatter/ppermute | solution.py:111
  306.0 4.0 %collective-permute-done.16 = f32[3,2,2,16,128]{4,3,2,1,0:T(8,128)S(1)} collective-permute-done((f32[3,2,2,16,128]{4,3,2,1,0:T(8,128)S(1)}, f32[3,2,2,16,128]{4,3,2,1,0:T(8,128)S(1)}, u32[]{:S(2)}, u32[]{:S(2)}) %collective-permute-start.16) | collective-permute-done | bytes 98336 | tf_op jit(solution)/shard_map/grad_rows_reduce_scatter/ppermute | solution.py:111
  313.4 3.0 collective-permute-done.17
  316.4 3.1 collective-permute-start.18
  319.5 5.7 %convolution_convert_fusion = bf16[8192,128]{1,0:T(8,128)(2,1)} fusion(bf16[192,4096]{1,0:T(8,128)(2,1)} %collective-permute-done, bf16[192,4096]{1,0:T(8,128)(2,1)} %all-gather.2.cloned.1.call-done, pred[]{:T(512)S(6)} %eq.26, f32[192,128]{1,0:T(8,128)S(1)} %get-tuple-element.59, f32[192]{0:T(256)S(1)} %fusion.17, f32[192]{0:T(256)S(1)} %get-tuple-element.6), kind=kOutput, calls=%fused_computation.1 | convolution fusion | flops 417931264 | bytes 5342721 | tf_op jit(solution)/shard_map/dot_general | solution.py:163
  325.3 4.8 %collective-permute-start.19 = (f32[16,128]{1,0:T(8,128)S(1)}, f32[16,128]{1,0:T(8,128)S(1)}, u32[]{:S(2)}, u32[]{:S(2)}) collective-permute-start(f32[16,128]{1,0:T(8,128)S(1)} %get-tuple-element.28), channel_id=1, source_target_pairs={{0,256},{64,320},{128,384},{192,448},{256,512},{320,576},{384,640}... | collective-permute-start | bytes 24584 | tf_op jit(solution)/shard_map/grad_rows_reduce_scatter/ppermute | solution.py:118
  330.1 5.0 %collective-permute-start.20 = (f32[16,128]{1,0:T(8,128)S(1)}, f32[16,128]{1,0:T(8,128)S(1)}, u32[]{:S(2)}, u32[]{:S(2)}) collective-permute-start(f32[16,128]{1,0:T(8,128)S(1)} %get-tuple-element.29), channel_id=1, source_target_pairs={{0,512},{64,576},{128,640},{192,704},{256,0},{320,64},{384,128},{4... | collective-permute-start | bytes 24584 | tf_op jit(solution)/shard_map/grad_rows_reduce_scatter/ppermute | solution.py:118
  335.6 3.9 %collective-permute-done.20 = f32[16,128]{1,0:T(8,128)S(1)} collective-permute-done((f32[16,128]{1,0:T(8,128)S(1)}, f32[16,128]{1,0:T(8,128)S(1)}, u32[]{:S(2)}, u32[]{:S(2)}) %collective-permute-start.20) | collective-permute-done | bytes 8224 | tf_op jit(solution)/shard_map/grad_rows_reduce_scatter/ppermute | solution.py:118
  (96 shorter events, 57.1 us)
Async XLA Ops:
  7.2 76.7 %copy-start = (bf16[8192,128]{1,0:T(8,128)(2,1)S(1)}, bf16[8192,128]{1,0:T(8,128)(2,1)}, u32[]{:S(2)}) copy-start(bf16[8192,128]{1,0:T(8,128)(2,1)} %param.7) | copy-start | bytes 6291460
  7.2 71.1 %all-gather.2.cloned.1.call-start = ((), (), s32[]{:S(2)}) async-start(), calls=%async_computation | async-start | bytes 1703936 | tf_op jit(solution)/shard_map/normed_rows_gather/all_gather | solution.py:138
  78.3 5.6 %collective-permute-start = (bf16[192,4096]{1,0:T(8,128)(2,1)}, bf16[192,4096]{1,0:T(8,128)(2,1)}, u32[]{:S(2)}, u32[]{:S(2)}) collective-permute-start(bf16[192,4096]{1,0:T(8,128)(2,1)} %all-gather.2.cloned.1.call-done), channel_id=1, source_target_pairs={{0,1},{1,0},{2,3},{3,2},{4,5},{5,4},{6,7},{7,6},{8,9},{9,8},{10,11... | collective-permute-start | bytes 4718600 | tf_op jit(solution)/shard_map/normed_rows_gather/ppermute | solution.py:141
  80.2 7.8 %copy-start.5 = (s32[192]{0:T(256)S(1)}, s32[192]{0:T(256)}, u32[]{:S(2)}) copy-start(s32[192]{0:T(256)} %param.6) | copy-start | bytes 2308
  88.3 3.1 collective-permute-start.1
  91.4 5.5 %collective-permute-start.2 = (f32[3,192]{1,0:T(4,128)S(1)}, f32[3,192]{1,0:T(4,128)S(1)}, u32[]{:S(2)}, u32[]{:S(2)}) collective-permute-start(f32[3,192]{1,0:T(4,128)S(1)} %pad_maximum_fusion.4), channel_id=1, source_target_pairs={{0,2},{1,3},{2,0},{3,1},{4,6},{5,7},{6,4},{7,5},{8,10},{9,11},{10,... | collective-permute-start | bytes 6920 | tf_op jit(solution)/shard_map/softmax_stats_exchange/ppermute | solution.py:67
  96.9 5.5 %collective-permute-start.3 = (f32[3,192]{1,0:T(4,128)S(1)}, f32[3,192]{1,0:T(4,128)S(1)}, u32[]{:S(2)}, u32[]{:S(2)}) collective-permute-start(f32[3,192]{1,0:T(4,128)S(1)} %pad_maximum_fusion.5), channel_id=1, source_target_pairs={{0,16},{1,17},{2,18},{3,19},{4,20},{5,21},{6,22},{7,23},{8,24},{9,... | collective-permute-start | bytes 6920 | tf_op jit(solution)/shard_map/softmax_stats_exchange/ppermute | solution.py:67
  102.5 6.4 %collective-permute-start.4 = (f32[3,192]{1,0:T(4,128)S(1)}, f32[3,192]{1,0:T(4,128)S(1)}, u32[]{:S(2)}, u32[]{:S(2)}) collective-permute-start(f32[3,192]{1,0:T(4,128)S(1)} %pad_maximum_fusion.6), channel_id=1, source_target_pairs={{0,4},{1,5},{2,6},{3,7},{4,0},{5,1},{6,2},{7,3},{8,12},{9,13},{10,... | collective-permute-start | bytes 6920 | tf_op jit(solution)/shard_map/softmax_stats_exchange/ppermute | solution.py:67
  109.0 7.0 %collective-permute-start.5 = (f32[3,192]{1,0:T(4,128)S(1)}, f32[3,192]{1,0:T(4,128)S(1)}, u32[]{:S(2)}, u32[]{:S(2)}) collective-permute-start(f32[3,192]{1,0:T(4,128)S(1)} %pad_maximum_fusion.7), channel_id=1, source_target_pairs={{0,32},{1,33},{2,34},{3,35},{4,36},{5,37},{6,38},{7,39},{8,40},{9,... | collective-permute-start | bytes 6920 | tf_op jit(solution)/shard_map/softmax_stats_exchange/ppermute | solution.py:67
  116.0 9.4 %collective-permute-start.6 = (f32[3,192]{1,0:T(4,128)S(1)}, f32[3,192]{1,0:T(4,128)S(1)}, u32[]{:S(2)}, u32[]{:S(2)}) collective-permute-start(f32[3,192]{1,0:T(4,128)S(1)} %pad_maximum_fusion.8), channel_id=1, source_target_pairs={{0,8},{1,9},{2,10},{3,11},{4,12},{5,13},{6,14},{7,15},{8,0},{9,1},... | collective-permute-start | bytes 6920 | tf_op jit(solution)/shard_map/softmax_stats_exchange/ppermute | solution.py:67
  125.5 5.5 %collective-permute-start.7 = (f32[3,192]{1,0:T(4,128)S(1)}, f32[3,192]{1,0:T(4,128)S(1)}, u32[]{:S(2)}, u32[]{:S(2)}) collective-permute-start(f32[3,192]{1,0:T(4,128)S(1)} %pad_maximum_fusion.9), channel_id=1, source_target_pairs={{0,64},{64,0},{128,192},{192,128},{256,320},{320,256},{384,448},{4... | collective-permute-start | bytes 6920 | tf_op jit(solution)/shard_map/softmax_stats_exchange/ppermute | solution.py:67
  131.0 6.4 %collective-permute-start.8 = (f32[3,192]{1,0:T(4,128)S(1)}, f32[3,192]{1,0:T(4,128)S(1)}, u32[]{:S(2)}, u32[]{:S(2)}) collective-permute-start(f32[3,192]{1,0:T(4,128)S(1)} %pad_maximum_fusion.10), channel_id=1, source_target_pairs={{0,128},{64,192},{128,0},{192,64},{256,384},{320,448},{384,256},{4... | collective-permute-start | bytes 6920 | tf_op jit(solution)/shard_map/softmax_stats_exchange/ppermute | solution.py:67
  137.5 10.0 %collective-permute-start.9 = (f32[3,192]{1,0:T(4,128)S(1)}, f32[3,192]{1,0:T(4,128)S(1)}, u32[]{:S(2)}, u32[]{:S(2)}) collective-permute-start(f32[3,192]{1,0:T(4,128)S(1)} %get-tuple-element.57), channel_id=1, source_target_pairs={{0,256},{64,320},{128,384},{192,448},{256,512},{320,576},{384,640}... | collective-permute-start | bytes 6920 | tf_op jit(solution)/shard_map/softmax_stats_exchange/ppermute | solution.py:77
  142.3 9.4 %collective-permute-start.10 = (f32[3,192]{1,0:T(4,128)S(1)}, f32[3,192]{1,0:T(4,128)S(1)}, u32[]{:S(2)}, u32[]{:S(2)}) collective-permute-start(f32[3,192]{1,0:T(4,128)S(1)} %get-tuple-element.57), channel_id=1, source_target_pairs={{0,512},{64,576},{128,640},{192,704},{256,0},{320,64},{384,128},{4... | collective-permute-start | bytes 6920 | tf_op jit(solution)/shard_map/softmax_stats_exchange/ppermute | solution.py:77
  171.2 3.2 copy-start.3
  178.9 3.6 %copy-start.1 = (f32[3,2,2,2,2,2,2,2,2,16,128]{10,9,6,5,3,2,1,0,4,7,8:T(8,128)}, f32[3,2,2,2,2,2,2,2,2,16,128]{10,9,6,5,3,2,1,0,4,7,8:T(8,128)S(1)}, u32[]{:S(2)}) copy-start(f32[3,2,2,2,2,2,2,2,2,16,128]{10,9,6,5,3,2,1,0,4,7,8:T(8,128)S(1)} %copy_dynamic-update-slice_fusion) | copy-start | bytes 18874372
  182.4 41.0 %collective-permute-start.11 = (f32[3,2,2,2,2,2,2,2,16,128]{9,8,6,5,3,2,1,0,4,7:T(8,128)}, f32[3,2,2,2,2,2,2,2,16,128]{9,8,6,5,3,2,1,0,4,7:T(8,128)}, u32[]{:S(2)}, u32[]{:S(2)}) collective-permute-start(f32[3,2,2,2,2,2,2,2,16,128]{9,8,6,5,3,2,1,0,4,7:T(8,128)} %dynamic-slice_bitcast_fusion), channel_id=1, source_target_pairs={{0,63},{1,18},{2,49},{3,20},{4,51},{5,22},{6,53},{7,24},{8,55},{9,... | collective-permute-start | bytes 9437192 | tf_op jit(solution)/shard_map/grad_rows_reduce_scatter/ppermute | solution.py:111
  227.4 1.6 copy-start.2
  230.4 22.6 %collective-permute-start.12 = (f32[3,2,2,2,2,2,2,16,128]{8,7,6,5,3,2,1,0,4:T(8,128)}, f32[3,2,2,2,2,2,2,16,128]{8,7,6,5,3,2,1,0,4:T(8,128)}, u32[]{:S(2)}, u32[]{:S(2)}) collective-permute-start(f32[3,2,2,2,2,2,2,16,128]{8,7,6,5,3,2,1,0,4:T(8,128)} %dynamic-slice_bitcast_fusion.1), channel_id=1, source_target_pairs={{0,2},{1,15},{2,0},{3,5},{4,6},{5,3},{6,4},{7,9},{8,10},{9,7},{10,... | collective-permute-start | bytes 4718600 | tf_op jit(solution)/shard_map/grad_rows_reduce_scatter/ppermute | solution.py:111
  255.2 1.1 copy-start.4
  256.4 14.0 %collective-permute-start.13 = (f32[3,2,2,2,2,2,16,128]{7,6,5,4,3,2,1,0:T(8,128)S(1)}, f32[3,2,2,2,2,2,16,128]{7,6,5,4,3,2,1,0:T(8,128)}, u32[]{:S(2)}, u32[]{:S(2)}) collective-permute-start(f32[3,2,2,2,2,2,16,128]{7,6,5,4,3,2,1,0:T(8,128)S(1)} %dynamic-slice_bitcast_fusion.2), channel_id=1, source_target_pairs={{0,16},{1,49},{2,18},{3,51},{4,20},{5,53},{6,22},{7,55},{8,24},{9,... | collective-permute-start | bytes 2359304 | tf_op jit(solution)/shard_map/grad_rows_reduce_scatter/ppermute | solution.py:111
  272.7 16.5 %collective-permute-start.14 = (f32[3,2,2,2,2,16,128]{6,5,4,3,2,1,0:T(8,128)}, f32[3,2,2,2,2,16,128]{6,5,4,3,2,1,0:T(8,128)}, u32[]{:S(2)}, u32[]{:S(2)}) collective-permute-start(f32[3,2,2,2,2,16,128]{6,5,4,3,2,1,0:T(8,128)} %dynamic-slice_bitcast_fusion.3), channel_id=1, source_target_pairs={{0,4},{1,5},{2,6},{3,15},{4,0},{5,1},{6,2},{7,11},{8,12},{9,13},{1... | collective-permute-start | bytes 1179656 | tf_op jit(solution)/shard_map/grad_rows_reduce_scatter/ppermute | solution.py:111
  290.4 9.1 %collective-permute-start.15 = (f32[3,2,2,2,16,128]{5,4,2,1,0,3:T(8,128)S(1)}, f32[3,2,2,2,16,128]{5,4,2,1,0,3:T(8,128)S(1)}, u32[]{:S(2)}, u32[]{:S(2)}) collective-permute-start(f32[3,2,2,2,16,128]{5,4,2,1,0,3:T(8,128)S(1)} %bitcast.82), channel_id=1, source_target_pairs={{0,32},{1,33},{2,34},{3,35},{4,36},{5,37},{6,38},{7,39},{8,40},{9,... | collective-permute-start | bytes 589832 | tf_op jit(solution)/shard_map/grad_rows_reduce_scatter/ppermute | solution.py:111
  299.5 10.6 %collective-permute-start.16 = (f32[3,2,2,16,128]{4,3,2,1,0:T(8,128)S(1)}, f32[3,2,2,16,128]{4,3,2,1,0:T(8,128)S(1)}, u32[]{:S(2)}, u32[]{:S(2)}) collective-permute-start(f32[3,2,2,16,128]{4,3,2,1,0:T(8,128)S(1)} %dynamic-slice_bitcast_fusion.4), channel_id=1, source_target_pairs={{0,8},{1,9},{2,10},{3,11},{4,12},{5,13},{6,14},{7,15},{8,0},{9,1},... | collective-permute-start | bytes 294920 | tf_op jit(solution)/shard_map/grad_rows_reduce_scatter/ppermute | solution.py:111
  310.1 6.2 %collective-permute-start.17 = (f32[3,2,16,128]{3,2,1,0:T(8,128)S(1)}, f32[3,2,16,128]{3,2,1,0:T(8,128)S(1)}, u32[]{:S(2)}, u32[]{:S(2)}) collective-permute-start(f32[3,2,16,128]{3,2,1,0:T(8,128)S(1)} %dynamic-slice_bitcast_fusion.5), channel_id=1, source_target_pairs={{0,64},{64,0},{128,192},{192,128},{256,320},{320,256},{384,448},{4... | collective-permute-start | bytes 147464 | tf_op jit(solution)/shard_map/grad_rows_reduce_scatter/ppermute | solution.py:111
  316.4 8.9 %collective-permute-start.18 = (f32[3,16,128]{2,1,0:T(8,128)S(1)}, f32[3,16,128]{2,1,0:T(8,128)S(1)}, u32[]{:S(2)}, u32[]{:S(2)}) collective-permute-start(f32[3,16,128]{2,1,0:T(8,128)S(1)} %dynamic-slice_bitcast_fusion.6), channel_id=1, source_target_pairs={{0,128},{64,192},{128,0},{192,64},{256,384},{320,448},{384,256},{4... | collective-permute-start | bytes 73736 | tf_op jit(solution)/shard_map/grad_rows_reduce_scatter/ppermute | solution.py:111
  325.3 10.3 %collective-permute-start.19 = (f32[16,128]{1,0:T(8,128)S(1)}, f32[16,128]{1,0:T(8,128)S(1)}, u32[]{:S(2)}, u32[]{:S(2)}) collective-permute-start(f32[16,128]{1,0:T(8,128)S(1)} %get-tuple-element.28), channel_id=1, source_target_pairs={{0,256},{64,320},{128,384},{192,448},{256,512},{320,576},{384,640}... | collective-permute-start | bytes 24584 | tf_op jit(solution)/shard_map/grad_rows_reduce_scatter/ppermute | solution.py:118
  330.1 9.5 %collective-permute-start.20 = (f32[16,128]{1,0:T(8,128)S(1)}, f32[16,128]{1,0:T(8,128)S(1)}, u32[]{:S(2)}, u32[]{:S(2)}) collective-permute-start(f32[16,128]{1,0:T(8,128)S(1)} %get-tuple-element.29), channel_id=1, source_target_pairs={{0,512},{64,576},{128,640},{192,704},{256,0},{320,64},{384,128},{4... | collective-permute-start | bytes 24584 | tf_op jit(solution)/shard_map/grad_rows_reduce_scatter/ppermute | solution.py:118
Sparse Core Ops, SparseCore 0:
  11.1 67.0 all-gather.1

commit v5 on v3

--- a/solution.py
+++ b/solution.py
@@ -4,6 +4,7 @@
 from jax.sharding import PartitionSpec as P
 
 TENSOR_MASK_ORDER = (1, 2, 16, 4, 32, 8)
+SPLIT_BYTES = 256 * 1024
 
 
 def split_pow2(count):
@@ -75,7 +76,14 @@
         mine = (lax.axis_index(name) & mask) // mask
         keep = lax.dynamic_index_in_dim(value, mine, axis, keepdims=False)
         sent = lax.dynamic_index_in_dim(value, 1 - mine, axis, keepdims=False)
-        value = keep + lax.ppermute(sent, name, xor_pairs(lax.axis_size(name), mask))
+        pairs = xor_pairs(lax.axis_size(name), mask)
+        if name == "tensor" and mask != 1 and sent.size * 4 >= SPLIT_BYTES:
+            rows = sent.shape[-2] // 2
+            halves = [lax.slice_in_dim(sent, i * rows, (i + 1) * rows, axis=sent.ndim - 2) for i in range(2)]
+            sent_back = jnp.concatenate([lax.ppermute(h, name, pairs) for h in halves], axis=sent.ndim - 2)
+        else:
+            sent_back = lax.ppermute(sent, name, pairs)
+        value = keep + sent_back
         labels.pop(axis)
     group = lax.axis_index("section") // low
     total = lax.dynamic_index_in_dim(value, group, 0, keepdims=False)

time: 319 us -> 320 us (level)
  waiting for transfers between devices: 188 us -> 180 us
  starting transfers between devices: 77.6 us -> 85.5 us
    ppermute x8 -> x11, starting transfers between devices: 29.7 us -> 37.6 us  [the longest x5 19 us: reduce_scatter_blocks(): sent_back = lax.ppermute(sent, name, pairs)]
    ppermute x8 -> x11, waiting for transfers between devices: 87.3 us -> 79.5 us  [the longest x6 61.5 us: reduce_scatter_blocks(): lax.ppermute(h, name, pairs)]
  transfers between devices with their start and end apart: 21 -> 24, of which waited for: 18 -> 21; matrix products, arithmetic and copies ran while one was open for 2% -> 2% of each run, Pallas kernels for 0% -> 0%
where the time goes in v5:
time: 320 us; the launch traced here: 319 us
  waiting for transfers between devices  180 us (56%)
  starting transfers between devices  85.5 us (27%)
  local copies, waits for them, and re-layouts  16 us (5%)
  between operations  14.8 us (5%)
  other arithmetic  14 us (4%)
  matrix products  8.63 us (3%)
    all_gather x1, waiting for transfers between devices, local(): normed = lax.all_gather(normed_part, 'section', axis=0, tiled=True)  71.5 us
    ppermute x6, waiting for transfers between devices, reduce_scatter_blocks(): lax.ppermute(h, name, pairs)  61.5 us
    ppermute x8, starting transfers between devices, exchange_stats(): other = lax.ppermute(stats, name, xor_pairs(lax.axis_size(name), mask))  28.3 us
    ppermute x8, waiting for transfers between devices, exchange_stats(): other = lax.ppermute(stats, name, xor_pairs(lax.axis_size(name), mask))  20.3 us
    ppermute x5, starting transfers between devices, reduce_scatter_blocks(): sent_back = lax.ppermute(sent, name, pairs)  19 us
    ppermute x6, starting transfers between devices, reduce_scatter_blocks(): lax.ppermute(h, name, pairs)  18.6 us
    ppermute x5, waiting for transfers between devices, reduce_scatter_blocks(): sent_back = lax.ppermute(sent, name, pairs)  18 us
    ppermute x2, starting transfers between devices, exchange_stats(): received.append(lax.ppermute(stats, 'section', pairs))  9.75 us
  transfers between devices with their start and end apart: 24, of which 21 were waited for; matrix products, arithmetic and copies ran while one was open for 2% of the time, Pallas kernels for 0%

profile of v5, /device:TPU:6, one launch (start us, length us, event | category | flops | bytes accessed | tf_op | source)
XLA Modules:
  0.0 318.8 jit_solution(17309570401222671066)
XLA Ops:
  11.1 71.5 %all-gather.2.cloned.1.call-done = bf16[192,8192]{1,0:T(8,128)(2,1)} async-done(((bf16[16,8192]{1,0:T(8,128)(2,1)}), bf16[192,8192]{1,0:T(8,128)(2,1)}) %all-gather.2.cloned.1.call-update) | async-done | bytes 3145744 | tf_op jit(solution)/shard_map/all_gather | solution.py:110
  88.9 3.4 %collective-permute-start.1 = (f32[3,192]{1,0:T(4,128)S(1)}, f32[3,192]{1,0:T(4,128)S(1)}, u32[]{:S(2)}, u32[]{:S(2)}) collective-permute-start(f32[3,192]{1,0:T(4,128)S(1)} %pad_maximum_fusion.2), channel_id=1, source_target_pairs={{0,2},{1,3},{2,0},{3,1},{4,6},{5,7},{6,4},{7,5},{8,10},{9,11},{10,... | collective-permute-start | bytes 6920 | tf_op jit(solution)/shard_map/softmax_stats_exchange/ppermute | solution.py:49
  100.0 4.3 %collective-permute-start.3 = (f32[3,192]{1,0:T(4,128)S(1)}, f32[3,192]{1,0:T(4,128)S(1)}, u32[]{:S(2)}, u32[]{:S(2)}) collective-permute-start(f32[3,192]{1,0:T(4,128)S(1)} %pad_maximum_fusion.4), channel_id=1, source_target_pairs={{0,4},{1,5},{2,6},{3,7},{4,0},{5,1},{6,2},{7,3},{8,12},{9,13},{10,... | collective-permute-start | bytes 6920 | tf_op jit(solution)/shard_map/softmax_stats_exchange/ppermute | solution.py:49
  106.5 3.4 %collective-permute-start.4 = (f32[3,192]{1,0:T(4,128)S(1)}, f32[3,192]{1,0:T(4,128)S(1)}, u32[]{:S(2)}, u32[]{:S(2)}) collective-permute-start(f32[3,192]{1,0:T(4,128)S(1)} %pad_maximum_fusion.5), channel_id=1, source_target_pairs={{0,32},{1,33},{2,34},{3,35},{4,36},{5,37},{6,38},{7,39},{8,40},{9,... | collective-permute-start | bytes 6920 | tf_op jit(solution)/shard_map/softmax_stats_exchange/ppermute | solution.py:49
  109.9 3.6 %collective-permute-done.4 = f32[3,192]{1,0:T(4,128)S(1)} collective-permute-done((f32[3,192]{1,0:T(4,128)S(1)}, f32[3,192]{1,0:T(4,128)S(1)}, u32[]{:S(2)}, u32[]{:S(2)}) %collective-permute-start.4) | collective-permute-done | bytes 2336 | tf_op jit(solution)/shard_map/softmax_stats_exchange/ppermute | solution.py:49
  113.5 7.4 %collective-permute-start.5 = (f32[3,192]{1,0:T(4,128)S(1)}, f32[3,192]{1,0:T(4,128)S(1)}, u32[]{:S(2)}, u32[]{:S(2)}) collective-permute-start(f32[3,192]{1,0:T(4,128)S(1)} %pad_maximum_fusion.6), channel_id=1, source_target_pairs={{0,8},{1,9},{2,10},{3,11},{4,12},{5,13},{6,14},{7,15},{8,0},{9,1},... | collective-permute-start | bytes 6920 | tf_op jit(solution)/shard_map/softmax_stats_exchange/ppermute | solution.py:49
  124.9 3.5 %collective-permute-done.6 = f32[3,192]{1,0:T(4,128)S(1)} collective-permute-done((f32[3,192]{1,0:T(4,128)S(1)}, f32[3,192]{1,0:T(4,128)S(1)}, u32[]{:S(2)}, u32[]{:S(2)}) %collective-permute-start.6) | collective-permute-done | bytes 2336 | tf_op jit(solution)/shard_map/softmax_stats_exchange/ppermute | solution.py:49
  128.6 3.2 %collective-permute-start.7 = (f32[3,192]{1,0:T(4,128)S(1)}, f32[3,192]{1,0:T(4,128)S(1)}, u32[]{:S(2)}, u32[]{:S(2)}) collective-permute-start(f32[3,192]{1,0:T(4,128)S(1)} %pad_maximum_fusion.8), channel_id=1, source_target_pairs={{0,128},{64,192},{128,0},{192,64},{256,384},{320,448},{384,256},{4... | collective-permute-start | bytes 6920 | tf_op jit(solution)/shard_map/softmax_stats_exchange/ppermute | solution.py:49
  131.8 3.1 collective-permute-done.7
  135.0 4.9 %collective-permute-start.8 = (f32[3,192]{1,0:T(4,128)S(1)}, f32[3,192]{1,0:T(4,128)S(1)}, u32[]{:S(2)}, u32[]{:S(2)}) collective-permute-start(f32[3,192]{1,0:T(4,128)S(1)} %get-tuple-element.63), channel_id=1, source_target_pairs={{0,256},{64,320},{128,384},{192,448},{256,512},{320,576},{384,640}... | collective-permute-start | bytes 6920 | tf_op jit(solution)/shard_map/softmax_stats_exchange/ppermute | solution.py:59
  139.9 4.9 %collective-permute-start.9 = (f32[3,192]{1,0:T(4,128)S(1)}, f32[3,192]{1,0:T(4,128)S(1)}, u32[]{:S(2)}, u32[]{:S(2)}) collective-permute-start(f32[3,192]{1,0:T(4,128)S(1)} %get-tuple-element.63), channel_id=1, source_target_pairs={{0,512},{64,576},{128,640},{192,704},{256,0},{320,64},{384,128},{4... | collective-permute-start | bytes 6920 | tf_op jit(solution)/shard_map/softmax_stats_exchange/ppermute | solution.py:59
  144.8 4.5 %collective-permute-done.9 = f32[3,192]{1,0:T(4,128)S(1)} collective-permute-done((f32[3,192]{1,0:T(4,128)S(1)}, f32[3,192]{1,0:T(4,128)S(1)}, u32[]{:S(2)}, u32[]{:S(2)}) %collective-permute-start.9) | collective-permute-done | bytes 2336 | tf_op jit(solution)/shard_map/softmax_stats_exchange/ppermute | solution.py:59
  152.3 4.4 %copy.23 = f32[12,16,64,128]{3,1,2,0:T(8,128)S(1)} copy(f32[12,16,64,128]{3,2,1,0:T(8,128)S(1)} %bitcast.78) | data formatting | bytes 12582912 | tf_op jit(solution)/shard_map/reshape | solution.py:133
  162.1 5.9 %collective-permute-done.10 = f32[3,2,2,2,2,2,2,2,16,128]{9,8,7,6,5,4,3,2,1,0:T(8,128)} collective-permute-done((f32[3,2,2,2,2,2,2,2,16,128]{9,8,7,6,5,4,3,2,1,0:T(8,128)}, f32[3,2,2,2,2,2,2,2,16,128]{9,8,7,6,5,4,3,2,1,0:T(8,128)}, u32[]{:S(2)}, u32[]{:S(2)}) %collective-permute-start.10) | collective-permute-done | bytes 3145760 | tf_op jit(solution)/shard_map/grad_rows_reduce_scatter/ppermute | solution.py:85
  168.1 4.0 %bitcast_add_fusion = f32[3,2,2,2,2,2,2,2,16,128]{9,8,7,6,5,4,3,2,1,0:T(8,128)S(1)} fusion(f32[3,2,2,2,2,2,2,2,16,128]{9,8,7,6,5,4,3,2,1,0:T(8,128)} %collective-permute-done.10, f32[3,2,2,2,2,2,2,2,2,16,128]{10,9,8,7,6,5,4,3,2,1,0:T(8,128)} %bitcast.77, s32[]{:T(128)S(6)} %select_n.254), kind=kLoop, calls=%fused_computation.2 | loop fusion | flops 786432 | bytes 9437188 | tf_op jit(solution)/shard_map/grad_rows_reduce_scatter/add | solution.py:86
  174.2 3.4 %collective-permute-start.11 = (f32[3,2,2,2,2,2,2,8,128]{8,7,6,5,4,3,2,1,0:T(8,128)}, f32[3,2,2,2,2,2,2,8,128]{8,7,6,5,4,3,2,1,0:T(8,128)S(1)}, u32[]{:S(2)}, u32[]{:S(2)}) collective-permute-start(f32[3,2,2,2,2,2,2,8,128]{8,7,6,5,4,3,2,1,0:T(8,128)} %get-tuple-element.26), channel_id=1, source_target_pairs={{0,2},{1,3},{2,0},{3,1},{4,6},{5,7},{6,4},{7,5},{8,10},{9,11},{10,... | collective-permute-start | bytes 2359304 | tf_op jit(solution)/shard_map/grad_rows_reduce_scatter/ppermute | solution.py:83
  180.1 16.6 %collective-permute-done.11 = f32[3,2,2,2,2,2,2,8,128]{8,7,6,5,4,3,2,1,0:T(8,128)S(1)} collective-permute-done((f32[3,2,2,2,2,2,2,8,128]{8,7,6,5,4,3,2,1,0:T(8,128)}, f32[3,2,2,2,2,2,2,8,128]{8,7,6,5,4,3,2,1,0:T(8,128)S(1)}, u32[]{:S(2)}, u32[]{:S(2)}) %collective-permute-start.11) | collective-permute-done | bytes 786464 | tf_op jit(solution)/shard_map/grad_rows_reduce_scatter/ppermute | solution.py:83
  196.7 16.2 %collective-permute-done.12 = f32[3,2,2,2,2,2,2,8,128]{8,7,6,5,4,3,2,1,0:T(8,128)} collective-permute-done((f32[3,2,2,2,2,2,2,8,128]{8,7,6,5,4,3,2,1,0:T(8,128)}, f32[3,2,2,2,2,2,2,8,128]{8,7,6,5,4,3,2,1,0:T(8,128)}, u32[]{:S(2)}, u32[]{:S(2)}) %collective-permute-start.12) | collective-permute-done | bytes 786464 | tf_op jit(solution)/shard_map/grad_rows_reduce_scatter/ppermute | solution.py:83
  222.8 8.1 %collective-permute-done.13 = f32[3,2,2,2,2,2,8,128]{7,6,4,3,2,1,0,5:T(8,128)S(1)} collective-permute-done((f32[3,2,2,2,2,2,8,128]{7,6,4,3,2,1,0,5:T(8,128)}, f32[3,2,2,2,2,2,8,128]{7,6,4,3,2,1,0,5:T(8,128)S(1)}, u32[]{:S(2)}, u32[]{:S(2)}) %collective-permute-start.13) | collective-permute-done | bytes 393248 | tf_op jit(solution)/shard_map/grad_rows_reduce_scatter/ppermute | solution.py:83
  230.9 6.7 %collective-permute-done.14 = f32[3,2,2,2,2,2,8,128]{7,6,4,3,2,1,0,5:T(8,128)S(1)} collective-permute-done((f32[3,2,2,2,2,2,8,128]{7,6,4,3,2,1,0,5:T(8,128)S(1)}, f32[3,2,2,2,2,2,8,128]{7,6,4,3,2,1,0,5:T(8,128)S(1)}, u32[]{:S(2)}, u32[]{:S(2)}) %collective-permute-start.14) | collective-permute-done | bytes 393248 | tf_op jit(solution)/shard_map/grad_rows_reduce_scatter/ppermute | solution.py:83
  239.8 4.3 %collective-permute-start.15 = (f32[3,2,2,2,2,8,128]{6,5,4,3,2,1,0:T(8,128)S(1)}, f32[3,2,2,2,2,8,128]{6,5,4,3,2,1,0:T(8,128)}, u32[]{:S(2)}, u32[]{:S(2)}) collective-permute-start(f32[3,2,2,2,2,8,128]{6,5,4,3,2,1,0:T(8,128)S(1)} %get-tuple-element.30), channel_id=1, source_target_pairs={{0,4},{1,5},{2,6},{3,7},{4,0},{5,1},{6,2},{7,3},{8,12},{9,13},{10,... | collective-permute-start | bytes 589832 | tf_op jit(solution)/shard_map/grad_rows_reduce_scatter/ppermute | solution.py:83
  246.6 10.8 %collective-permute-done.15 = f32[3,2,2,2,2,8,128]{6,5,4,3,2,1,0:T(8,128)} collective-permute-done((f32[3,2,2,2,2,8,128]{6,5,4,3,2,1,0:T(8,128)S(1)}, f32[3,2,2,2,2,8,128]{6,5,4,3,2,1,0:T(8,128)}, u32[]{:S(2)}, u32[]{:S(2)}) %collective-permute-start.15) | collective-permute-done | bytes 196640 | tf_op jit(solution)/shard_map/grad_rows_reduce_scatter/ppermute | solution.py:83
  257.4 3.1 collective-permute-done.16
  261.7 3.3 %collective-permute-start.17 = (f32[3,2,2,2,16,128]{5,4,3,2,1,0:T(8,128)S(1)}, f32[3,2,2,2,16,128]{5,4,3,2,1,0:T(8,128)S(1)}, u32[]{:S(2)}, u32[]{:S(2)}) collective-permute-start(f32[3,2,2,2,16,128]{5,4,3,2,1,0:T(8,128)S(1)} %dynamic-slice_bitcast_fusion.3), channel_id=1, source_target_pairs={{0,32},{1,33},{2,34},{3,35},{4,36},{5,37},{6,38},{7,39},{8,40},{9,... | collective-permute-start | bytes 589832 | tf_op jit(solution)/shard_map/grad_rows_reduce_scatter/ppermute | solution.py:85
  265.1 5.8 %collective-permute-done.17 = f32[3,2,2,2,16,128]{5,4,3,2,1,0:T(8,128)S(1)} collective-permute-done((f32[3,2,2,2,16,128]{5,4,3,2,1,0:T(8,128)S(1)}, f32[3,2,2,2,16,128]{5,4,3,2,1,0:T(8,128)S(1)}, u32[]{:S(2)}, u32[]{:S(2)}) %collective-permute-start.17) | collective-permute-done | bytes 196640 | tf_op jit(solution)/shard_map/grad_rows_reduce_scatter/ppermute | solution.py:85
  271.0 8.3 %collective-permute-start.18 = (f32[3,2,2,16,128]{4,3,1,0,2:T(8,128)S(1)}, f32[3,2,2,16,128]{4,3,1,0,2:T(8,128)S(1)}, u32[]{:S(2)}, u32[]{:S(2)}) collective-permute-start(f32[3,2,2,16,128]{4,3,1,0,2:T(8,128)S(1)} %bitcast.80), channel_id=1, source_target_pairs={{0,8},{1,9},{2,10},{3,11},{4,12},{5,13},{6,14},{7,15},{8,0},{9,1},... | collective-permute-start | bytes 294920 | tf_op jit(solution)/shard_map/grad_rows_reduce_scatter/ppermute | solution.py:85
  279.3 3.6 %collective-permute-done.18 = f32[3,2,2,16,128]{4,3,1,0,2:T(8,128)S(1)} collective-permute-done((f32[3,2,2,16,128]{4,3,1,0,2:T(8,128)S(1)}, f32[3,2,2,16,128]{4,3,1,0,2:T(8,128)S(1)}, u32[]{:S(2)}, u32[]{:S(2)}) %collective-permute-start.18) | collective-permute-done | bytes 98336 | tf_op jit(solution)/shard_map/grad_rows_reduce_scatter/ppermute | solution.py:85
  289.0 3.3 %collective-permute-start.20 = (f32[3,16,128]{2,1,0:T(8,128)S(1)}, f32[3,16,128]{2,1,0:T(8,128)S(1)}, u32[]{:S(2)}, u32[]{:S(2)}) collective-permute-start(f32[3,16,128]{2,1,0:T(8,128)S(1)} %dynamic-slice_bitcast_fusion.5), channel_id=1, source_target_pairs={{0,128},{64,192},{128,0},{192,64},{256,384},{320,448},{384,256},{4... | collective-permute-start | bytes 73736 | tf_op jit(solution)/shard_map/grad_rows_reduce_scatter/ppermute | solution.py:85
  292.3 4.6 %convolution_convert_fusion = bf16[8192,128]{1,0:T(8,128)(2,1)} fusion(bf16[192,8192]{1,0:T(8,128)(2,1)} %all-gather.2.cloned.1.call-done, f32[192,128]{1,0:T(8,128)S(1)} %get-tuple-element.65, f32[192]{0:T(256)S(1)} %fusion.15, f32[192]{0:T(256)S(1)} %get-tuple-element.6), kind=kOutput, calls=%fused_computation.1 | convolution fusion | flops 403775488 | bytes 5342720 | tf_op jit(solution)/shard_map/dot_general | solution.py:127
  296.9 4.8 %collective-permute-start.21 = (f32[16,128]{1,0:T(8,128)S(1)}, f32[16,128]{1,0:T(8,128)S(1)}, u32[]{:S(2)}, u32[]{:S(2)}) collective-permute-start(f32[16,128]{1,0:T(8,128)S(1)} %get-tuple-element.34), channel_id=1, source_target_pairs={{0,256},{64,320},{128,384},{192,448},{256,512},{320,576},{384,640}... | collective-permute-start | bytes 24584 | tf_op jit(solution)/shard_map/grad_rows_reduce_scatter/ppermute | solution.py:93
  301.8 4.9 %collective-permute-start.22 = (f32[16,128]{1,0:T(8,128)S(1)}, f32[16,128]{1,0:T(8,128)S(1)}, u32[]{:S(2)}, u32[]{:S(2)}) collective-permute-start(f32[16,128]{1,0:T(8,128)S(1)} %get-tuple-element.35), channel_id=1, source_target_pairs={{0,512},{64,576},{128,640},{192,704},{256,0},{320,64},{384,128},{4... | collective-permute-start | bytes 24584 | tf_op jit(solution)/shard_map/grad_rows_reduce_scatter/ppermute | solution.py:93
  307.3 4.0 %collective-permute-done.22 = f32[16,128]{1,0:T(8,128)S(1)} collective-permute-done((f32[16,128]{1,0:T(8,128)S(1)}, f32[16,128]{1,0:T(8,128)S(1)}, u32[]{:S(2)}, u32[]{:S(2)}) %collective-permute-start.22) | collective-permute-done | bytes 8224 | tf_op jit(solution)/shard_map/grad_rows_reduce_scatter/ppermute | solution.py:93
  (96 shorter events, 59.9 us)
Async XLA Ops:
  7.2 75.4 %copy-start = (bf16[8192,128]{1,0:T(8,128)(2,1)S(1)}, bf16[8192,128]{1,0:T(8,128)(2,1)}, u32[]{:S(2)}) copy-start(bf16[8192,128]{1,0:T(8,128)(2,1)} %param.7) | copy-start | bytes 6291460
  7.2 75.4 %all-gather.2.cloned.1.call-start = ((), (), s32[]{:S(2)}) async-start(), calls=%async_computation | async-start | bytes 3407872 | tf_op jit(solution)/shard_map/all_gather | solution.py:110
  11.0 74.5 %copy-start.4 = (s32[192]{0:T(256)S(1)}, s32[192]{0:T(256)}, u32[]{:S(2)}) copy-start(s32[192]{0:T(256)} %param.6) | copy-start | bytes 2308
  85.8 3.1 collective-permute-start
  88.9 5.5 %collective-permute-start.1 = (f32[3,192]{1,0:T(4,128)S(1)}, f32[3,192]{1,0:T(4,128)S(1)}, u32[]{:S(2)}, u32[]{:S(2)}) collective-permute-start(f32[3,192]{1,0:T(4,128)S(1)} %pad_maximum_fusion.2), channel_id=1, source_target_pairs={{0,2},{1,3},{2,0},{3,1},{4,6},{5,7},{6,4},{7,5},{8,10},{9,11},{10,... | collective-permute-start | bytes 6920 | tf_op jit(solution)/shard_map/softmax_stats_exchange/ppermute | solution.py:49
  94.5 5.5 %collective-permute-start.2 = (f32[3,192]{1,0:T(4,128)S(1)}, f32[3,192]{1,0:T(4,128)S(1)}, u32[]{:S(2)}, u32[]{:S(2)}) collective-permute-start(f32[3,192]{1,0:T(4,128)S(1)} %pad_maximum_fusion.3), channel_id=1, source_target_pairs={{0,16},{1,17},{2,18},{3,19},{4,20},{5,21},{6,22},{7,23},{8,24},{9,... | collective-permute-start | bytes 6920 | tf_op jit(solution)/shard_map/softmax_stats_exchange/ppermute | solution.py:49
  100.0 6.4 %collective-permute-start.3 = (f32[3,192]{1,0:T(4,128)S(1)}, f32[3,192]{1,0:T(4,128)S(1)}, u32[]{:S(2)}, u32[]{:S(2)}) collective-permute-start(f32[3,192]{1,0:T(4,128)S(1)} %pad_maximum_fusion.4), channel_id=1, source_target_pairs={{0,4},{1,5},{2,6},{3,7},{4,0},{5,1},{6,2},{7,3},{8,12},{9,13},{10,... | collective-permute-start | bytes 6920 | tf_op jit(solution)/shard_map/softmax_stats_exchange/ppermute | solution.py:49
  106.5 7.0 %collective-permute-start.4 = (f32[3,192]{1,0:T(4,128)S(1)}, f32[3,192]{1,0:T(4,128)S(1)}, u32[]{:S(2)}, u32[]{:S(2)}) collective-permute-start(f32[3,192]{1,0:T(4,128)S(1)} %pad_maximum_fusion.5), channel_id=1, source_target_pairs={{0,32},{1,33},{2,34},{3,35},{4,36},{5,37},{6,38},{7,39},{8,40},{9,... | collective-permute-start | bytes 6920 | tf_op jit(solution)/shard_map/softmax_stats_exchange/ppermute | solution.py:49
  113.5 9.4 %collective-permute-start.5 = (f32[3,192]{1,0:T(4,128)S(1)}, f32[3,192]{1,0:T(4,128)S(1)}, u32[]{:S(2)}, u32[]{:S(2)}) collective-permute-start(f32[3,192]{1,0:T(4,128)S(1)} %pad_maximum_fusion.6), channel_id=1, source_target_pairs={{0,8},{1,9},{2,10},{3,11},{4,12},{5,13},{6,14},{7,15},{8,0},{9,1},... | collective-permute-start | bytes 6920 | tf_op jit(solution)/shard_map/softmax_stats_exchange/ppermute | solution.py:49
  123.0 5.5 %collective-permute-start.6 = (f32[3,192]{1,0:T(4,128)S(1)}, f32[3,192]{1,0:T(4,128)S(1)}, u32[]{:S(2)}, u32[]{:S(2)}) collective-permute-start(f32[3,192]{1,0:T(4,128)S(1)} %pad_maximum_fusion.7), channel_id=1, source_target_pairs={{0,64},{64,0},{128,192},{192,128},{256,320},{320,256},{384,448},{4... | collective-permute-start | bytes 6920 | tf_op jit(solution)/shard_map/softmax_stats_exchange/ppermute | solution.py:49
  128.6 6.4 %collective-permute-start.7 = (f32[3,192]{1,0:T(4,128)S(1)}, f32[3,192]{1,0:T(4,128)S(1)}, u32[]{:S(2)}, u32[]{:S(2)}) collective-permute-start(f32[3,192]{1,0:T(4,128)S(1)} %pad_maximum_fusion.8), channel_id=1, source_target_pairs={{0,128},{64,192},{128,0},{192,64},{256,384},{320,448},{384,256},{4... | collective-permute-start | bytes 6920 | tf_op jit(solution)/shard_map/softmax_stats_exchange/ppermute | solution.py:49
  135.0 9.8 %collective-permute-start.8 = (f32[3,192]{1,0:T(4,128)S(1)}, f32[3,192]{1,0:T(4,128)S(1)}, u32[]{:S(2)}, u32[]{:S(2)}) collective-permute-start(f32[3,192]{1,0:T(4,128)S(1)} %get-tuple-element.63), channel_id=1, source_target_pairs={{0,256},{64,320},{128,384},{192,448},{256,512},{320,576},{384,640}... | collective-permute-start | bytes 6920 | tf_op jit(solution)/shard_map/softmax_stats_exchange/ppermute | solution.py:59
  139.9 9.4 %collective-permute-start.9 = (f32[3,192]{1,0:T(4,128)S(1)}, f32[3,192]{1,0:T(4,128)S(1)}, u32[]{:S(2)}, u32[]{:S(2)}) collective-permute-start(f32[3,192]{1,0:T(4,128)S(1)} %get-tuple-element.63), channel_id=1, source_target_pairs={{0,512},{64,576},{128,640},{192,704},{256,0},{320,64},{384,128},{4... | collective-permute-start | bytes 6920 | tf_op jit(solution)/shard_map/softmax_stats_exchange/ppermute | solution.py:59
  156.6 3.6 %copy-start.1 = (f32[12,16,64,128]{3,1,2,0:T(8,128)}, f32[12,16,64,128]{3,1,2,0:T(8,128)S(1)}, u32[]{:S(2)}) copy-start(f32[12,16,64,128]{3,1,2,0:T(8,128)S(1)} %copy.23) | copy-start | bytes 18874372
  160.2 7.9 %collective-permute-start.10 = (f32[3,2,2,2,2,2,2,2,16,128]{9,8,7,6,5,4,3,2,1,0:T(8,128)}, f32[3,2,2,2,2,2,2,2,16,128]{9,8,7,6,5,4,3,2,1,0:T(8,128)}, u32[]{:S(2)}, u32[]{:S(2)}) collective-permute-start(f32[3,2,2,2,2,2,2,2,16,128]{9,8,7,6,5,4,3,2,1,0:T(8,128)} %dynamic-slice_bitcast_fusion), channel_id=1, source_target_pairs={{0,1},{1,0},{2,3},{3,2},{4,5},{5,4},{6,7},{7,6},{8,9},{9,8},{10,11... | collective-permute-start | bytes 9437192 | tf_op jit(solution)/shard_map/grad_rows_reduce_scatter/ppermute | solution.py:85
  172.1 2.2 copy-start.2
  174.2 22.5 %collective-permute-start.11 = (f32[3,2,2,2,2,2,2,8,128]{8,7,6,5,4,3,2,1,0:T(8,128)}, f32[3,2,2,2,2,2,2,8,128]{8,7,6,5,4,3,2,1,0:T(8,128)S(1)}, u32[]{:S(2)}, u32[]{:S(2)}) collective-permute-start(f32[3,2,2,2,2,2,2,8,128]{8,7,6,5,4,3,2,1,0:T(8,128)} %get-tuple-element.26), channel_id=1, source_target_pairs={{0,2},{1,3},{2,0},{3,1},{4,6},{5,7},{6,4},{7,5},{8,10},{9,11},{10,... | collective-permute-start | bytes 2359304 | tf_op jit(solution)/shard_map/grad_rows_reduce_scatter/ppermute | solution.py:83
  177.6 35.2 %collective-permute-start.12 = (f32[3,2,2,2,2,2,2,8,128]{8,7,6,5,4,3,2,1,0:T(8,128)}, f32[3,2,2,2,2,2,2,8,128]{8,7,6,5,4,3,2,1,0:T(8,128)}, u32[]{:S(2)}, u32[]{:S(2)}) collective-permute-start(f32[3,2,2,2,2,2,2,8,128]{8,7,6,5,4,3,2,1,0:T(8,128)} %get-tuple-element.27), channel_id=1, source_target_pairs={{0,2},{1,3},{2,0},{3,1},{4,6},{5,7},{6,4},{7,5},{8,10},{9,11},{10,... | collective-permute-start | bytes 2359304 | tf_op jit(solution)/shard_map/grad_rows_reduce_scatter/ppermute | solution.py:83
  216.8 14.1 %collective-permute-start.13 = (f32[3,2,2,2,2,2,8,128]{7,6,4,3,2,1,0,5:T(8,128)}, f32[3,2,2,2,2,2,8,128]{7,6,4,3,2,1,0,5:T(8,128)S(1)}, u32[]{:S(2)}, u32[]{:S(2)}) collective-permute-start(f32[3,2,2,2,2,2,8,128]{7,6,4,3,2,1,0,5:T(8,128)} %get-tuple-element.28), channel_id=1, source_target_pairs={{0,16},{1,17},{2,18},{3,19},{4,20},{5,21},{6,22},{7,23},{8,24},{9,... | collective-permute-start | bytes 1179656 | tf_op jit(solution)/shard_map/grad_rows_reduce_scatter/ppermute | solution.py:83
  219.7 17.9 %collective-permute-start.14 = (f32[3,2,2,2,2,2,8,128]{7,6,4,3,2,1,0,5:T(8,128)S(1)}, f32[3,2,2,2,2,2,8,128]{7,6,4,3,2,1,0,5:T(8,128)S(1)}, u32[]{:S(2)}, u32[]{:S(2)}) collective-permute-start(f32[3,2,2,2,2,2,8,128]{7,6,4,3,2,1,0,5:T(8,128)S(1)} %get-tuple-element.29), channel_id=1, source_target_pairs={{0,16},{1,17},{2,18},{3,19},{4,20},{5,21},{6,22},{7,23},{8,24},{9,... | collective-permute-start | bytes 1179656 | tf_op jit(solution)/shard_map/grad_rows_reduce_scatter/ppermute | solution.py:83
  237.6 0.7 copy-start.3
  239.8 17.6 %collective-permute-start.15 = (f32[3,2,2,2,2,8,128]{6,5,4,3,2,1,0:T(8,128)S(1)}, f32[3,2,2,2,2,8,128]{6,5,4,3,2,1,0:T(8,128)}, u32[]{:S(2)}, u32[]{:S(2)}) collective-permute-start(f32[3,2,2,2,2,8,128]{6,5,4,3,2,1,0:T(8,128)S(1)} %get-tuple-element.30), channel_id=1, source_target_pairs={{0,4},{1,5},{2,6},{3,7},{4,0},{5,1},{6,2},{7,3},{8,12},{9,13},{10,... | collective-permute-start | bytes 589832 | tf_op jit(solution)/shard_map/grad_rows_reduce_scatter/ppermute | solution.py:83
  244.2 16.4 %collective-permute-start.16 = (f32[3,2,2,2,2,8,128]{6,5,4,3,2,1,0:T(8,128)S(1)}, f32[3,2,2,2,2,8,128]{6,5,4,3,2,1,0:T(8,128)}, u32[]{:S(2)}, u32[]{:S(2)}) collective-permute-start(f32[3,2,2,2,2,8,128]{6,5,4,3,2,1,0:T(8,128)S(1)} %get-tuple-element.31), channel_id=1, source_target_pairs={{0,4},{1,5},{2,6},{3,7},{4,0},{5,1},{6,2},{7,3},{8,12},{9,13},{10,... | collective-permute-start | bytes 589832 | tf_op jit(solution)/shard_map/grad_rows_reduce_scatter/ppermute | solution.py:83
  261.7 9.2 %collective-permute-start.17 = (f32[3,2,2,2,16,128]{5,4,3,2,1,0:T(8,128)S(1)}, f32[3,2,2,2,16,128]{5,4,3,2,1,0:T(8,128)S(1)}, u32[]{:S(2)}, u32[]{:S(2)}) collective-permute-start(f32[3,2,2,2,16,128]{5,4,3,2,1,0:T(8,128)S(1)} %dynamic-slice_bitcast_fusion.3), channel_id=1, source_target_pairs={{0,32},{1,33},{2,34},{3,35},{4,36},{5,37},{6,38},{7,39},{8,40},{9,... | collective-permute-start | bytes 589832 | tf_op jit(solution)/shard_map/grad_rows_reduce_scatter/ppermute | solution.py:85
  271.0 11.9 %collective-permute-start.18 = (f32[3,2,2,16,128]{4,3,1,0,2:T(8,128)S(1)}, f32[3,2,2,16,128]{4,3,1,0,2:T(8,128)S(1)}, u32[]{:S(2)}, u32[]{:S(2)}) collective-permute-start(f32[3,2,2,16,128]{4,3,1,0,2:T(8,128)S(1)} %bitcast.80), channel_id=1, source_target_pairs={{0,8},{1,9},{2,10},{3,11},{4,12},{5,13},{6,14},{7,15},{8,0},{9,1},... | collective-permute-start | bytes 294920 | tf_op jit(solution)/shard_map/grad_rows_reduce_scatter/ppermute | solution.py:85
  282.9 6.0 %collective-permute-start.19 = (f32[3,2,16,128]{3,2,1,0:T(8,128)S(1)}, f32[3,2,16,128]{3,2,1,0:T(8,128)S(1)}, u32[]{:S(2)}, u32[]{:S(2)}) collective-permute-start(f32[3,2,16,128]{3,2,1,0:T(8,128)S(1)} %dynamic-slice_bitcast_fusion.4), channel_id=1, source_target_pairs={{0,64},{64,0},{128,192},{192,128},{256,320},{320,256},{384,448},{4... | collective-permute-start | bytes 147464 | tf_op jit(solution)/shard_map/grad_rows_reduce_scatter/ppermute | solution.py:85
  289.0 7.9 %collective-permute-start.20 = (f32[3,16,128]{2,1,0:T(8,128)S(1)}, f32[3,16,128]{2,1,0:T(8,128)S(1)}, u32[]{:S(2)}, u32[]{:S(2)}) collective-permute-start(f32[3,16,128]{2,1,0:T(8,128)S(1)} %dynamic-slice_bitcast_fusion.5), channel_id=1, source_target_pairs={{0,128},{64,192},{128,0},{192,64},{256,384},{320,448},{384,256},{4... | collective-permute-start | bytes 73736 | tf_op jit(solution)/shard_map/grad_rows_reduce_scatter/ppermute | solution.py:85
  296.9 10.3 %collective-permute-start.21 = (f32[16,128]{1,0:T(8,128)S(1)}, f32[16,128]{1,0:T(8,128)S(1)}, u32[]{:S(2)}, u32[]{:S(2)}) collective-permute-start(f32[16,128]{1,0:T(8,128)S(1)} %get-tuple-element.34), channel_id=1, source_target_pairs={{0,256},{64,320},{128,384},{192,448},{256,512},{320,576},{384,640}... | collective-permute-start | bytes 24584 | tf_op jit(solution)/shard_map/grad_rows_reduce_scatter/ppermute | solution.py:93
  301.8 9.5 %collective-permute-start.22 = (f32[16,128]{1,0:T(8,128)S(1)}, f32[16,128]{1,0:T(8,128)S(1)}, u32[]{:S(2)}, u32[]{:S(2)}) collective-permute-start(f32[16,128]{1,0:T(8,128)S(1)} %get-tuple-element.35), channel_id=1, source_target_pairs={{0,512},{64,576},{128,640},{192,704},{256,0},{320,64},{384,128},{4... | collective-permute-start | bytes 24584 | tf_op jit(solution)/shard_map/grad_rows_reduce_scatter/ppermute | solution.py:93
Sparse Core Ops, SparseCore 0:
  11.1 71.3 all-gather.1

commit v6 on v3

--- a/solution.py
+++ b/solution.py
@@ -69,7 +69,9 @@
     labels = ["group"] + [("section", 1 << j) for j in reversed(range(s_bits))]
     labels += [("tensor", 1 << j) for j in reversed(range(t_bits))]
     value = blocks.reshape((groups,) + (2,) * (s_bits + t_bits) + blocks.shape[2:])
-    steps = [("tensor", m) for m in tensor_masks(n_ten)] + [("section", m) for m in section_masks(n_sec)]
+    t_steps = [("tensor", m) for m in tensor_masks(n_ten)]
+    s_steps = [("section", m) for m in section_masks(n_sec)]
+    steps = t_steps[:3] + s_steps[:1] + t_steps[3:5] + s_steps[1:2] + t_steps[5:] + s_steps[2:]
     for name, mask in steps:
         axis = labels.index((name, mask))
         mine = (lax.axis_index(name) & mask) // mask

time: 319 us -> 313 us (0.981)
  waiting for transfers between devices: 188 us -> 182 us
    ppermute x8, waiting for transfers between devices: 87.3 us -> 82.3 us  [reduce_scatter_blocks(): lax.ppermute(sent, name, xor_pairs(lax.axis_size(name), mask))]
where the time goes in v6:
time: 313 us; the launch traced here: 312 us
  waiting for transfers between devices  182 us (58%)
  starting transfers between devices  76.6 us (24%)
  local copies, waits for them, and re-layouts  15.2 us (5%)
  between operations  14.7 us (5%)
  other arithmetic  14.5 us (5%)
  matrix products  8.63 us (3%)
    ppermute x8, waiting for transfers between devices, reduce_scatter_blocks(): lax.ppermute(sent, name, xor_pairs(lax.axis_size(name), mask))  82.3 us
    all_gather x1, waiting for transfers between devices, local(): normed = lax.all_gather(normed_part, 'section', axis=0, tiled=True)  71.5 us
    ppermute x8, starting transfers between devices, reduce_scatter_blocks(): lax.ppermute(sent, name, xor_pairs(lax.axis_size(name), mask))  28.8 us
    ppermute x8, starting transfers between devices, exchange_stats(): other = lax.ppermute(stats, name, xor_pairs(lax.axis_size(name), mask))  28.3 us
    ppermute x8, waiting for transfers between devices, exchange_stats(): other = lax.ppermute(stats, name, xor_pairs(lax.axis_size(name), mask))  20.3 us
    ppermute x2, starting transfers between devices, reduce_scatter_blocks(): total = total + lax.ppermute(sent, 'section', pairs)  9.75 us
    ppermute x2, starting transfers between devices, exchange_stats(): received.append(lax.ppermute(stats, 'section', pairs))  9.75 us
    add x8, other arithmetic, reduce_scatter_blocks(): keep + lax.ppermute(sent, name, xor_pairs(lax.axis_size(name), mask))  8.83 us
  transfers between devices with their start and end apart: 21, of which 18 were waited for; matrix products, arithmetic and copies ran while one was open for 2% of the time, Pallas kernels for 0%

profile of v6, /device:TPU:6, one launch (start us, length us, event | category | flops | bytes accessed | tf_op | source)
XLA Modules:
  0.0 311.9 jit_solution(18219764817197518583)
XLA Ops:
  11.1 71.5 %all-gather.2.cloned.1.call-done = bf16[192,8192]{1,0:T(8,128)(2,1)} async-done(((bf16[16,8192]{1,0:T(8,128)(2,1)}), bf16[192,8192]{1,0:T(8,128)(2,1)}) %all-gather.2.cloned.1.call-update) | async-done | bytes 3145744 | tf_op jit(solution)/shard_map/all_gather | solution.py:104
  82.6 2.9 fusion.26
  88.9 3.4 %collective-permute-start.1 = (f32[3,192]{1,0:T(4,128)S(1)}, f32[3,192]{1,0:T(4,128)S(1)}, u32[]{:S(2)}, u32[]{:S(2)}) collective-permute-start(f32[3,192]{1,0:T(4,128)S(1)} %pad_maximum_fusion.2), channel_id=1, source_target_pairs={{0,2},{1,3},{2,0},{3,1},{4,6},{5,7},{6,4},{7,5},{8,10},{9,11},{10,... | collective-permute-start | bytes 6920 | tf_op jit(solution)/shard_map/softmax_stats_exchange/ppermute | solution.py:48
  94.5 2.8 collective-permute-start.2
  100.1 4.3 %collective-permute-start.3 = (f32[3,192]{1,0:T(4,128)S(1)}, f32[3,192]{1,0:T(4,128)S(1)}, u32[]{:S(2)}, u32[]{:S(2)}) collective-permute-start(f32[3,192]{1,0:T(4,128)S(1)} %pad_maximum_fusion.4), channel_id=1, source_target_pairs={{0,4},{1,5},{2,6},{3,7},{4,0},{5,1},{6,2},{7,3},{8,12},{9,13},{10,... | collective-permute-start | bytes 6920 | tf_op jit(solution)/shard_map/softmax_stats_exchange/ppermute | solution.py:48
  106.5 3.4 %collective-permute-start.4 = (f32[3,192]{1,0:T(4,128)S(1)}, f32[3,192]{1,0:T(4,128)S(1)}, u32[]{:S(2)}, u32[]{:S(2)}) collective-permute-start(f32[3,192]{1,0:T(4,128)S(1)} %pad_maximum_fusion.5), channel_id=1, source_target_pairs={{0,32},{1,33},{2,34},{3,35},{4,36},{5,37},{6,38},{7,39},{8,40},{9,... | collective-permute-start | bytes 6920 | tf_op jit(solution)/shard_map/softmax_stats_exchange/ppermute | solution.py:48
  109.9 3.6 %collective-permute-done.4 = f32[3,192]{1,0:T(4,128)S(1)} collective-permute-done((f32[3,192]{1,0:T(4,128)S(1)}, f32[3,192]{1,0:T(4,128)S(1)}, u32[]{:S(2)}, u32[]{:S(2)}) %collective-permute-start.4) | collective-permute-done | bytes 2336 | tf_op jit(solution)/shard_map/softmax_stats_exchange/ppermute | solution.py:48
  113.6 7.4 %collective-permute-start.5 = (f32[3,192]{1,0:T(4,128)S(1)}, f32[3,192]{1,0:T(4,128)S(1)}, u32[]{:S(2)}, u32[]{:S(2)}) collective-permute-start(f32[3,192]{1,0:T(4,128)S(1)} %pad_maximum_fusion.6), channel_id=1, source_target_pairs={{0,8},{1,9},{2,10},{3,11},{4,12},{5,13},{6,14},{7,15},{8,0},{9,1},... | collective-permute-start | bytes 6920 | tf_op jit(solution)/shard_map/softmax_stats_exchange/ppermute | solution.py:48
  125.0 3.5 %collective-permute-done.6 = f32[3,192]{1,0:T(4,128)S(1)} collective-permute-done((f32[3,192]{1,0:T(4,128)S(1)}, f32[3,192]{1,0:T(4,128)S(1)}, u32[]{:S(2)}, u32[]{:S(2)}) %collective-permute-start.6) | collective-permute-done | bytes 2336 | tf_op jit(solution)/shard_map/softmax_stats_exchange/ppermute | solution.py:48
  128.6 3.2 %collective-permute-start.7 = (f32[3,192]{1,0:T(4,128)S(1)}, f32[3,192]{1,0:T(4,128)S(1)}, u32[]{:S(2)}, u32[]{:S(2)}) collective-permute-start(f32[3,192]{1,0:T(4,128)S(1)} %pad_maximum_fusion.8), channel_id=1, source_target_pairs={{0,128},{64,192},{128,0},{192,64},{256,384},{320,448},{384,256},{4... | collective-permute-start | bytes 6920 | tf_op jit(solution)/shard_map/softmax_stats_exchange/ppermute | solution.py:48
  131.8 3.1 %collective-permute-done.7 = f32[3,192]{1,0:T(4,128)S(1)} collective-permute-done((f32[3,192]{1,0:T(4,128)S(1)}, f32[3,192]{1,0:T(4,128)S(1)}, u32[]{:S(2)}, u32[]{:S(2)}) %collective-permute-start.7) | collective-permute-done | bytes 2336 | tf_op jit(solution)/shard_map/softmax_stats_exchange/ppermute | solution.py:48
  135.0 4.9 %collective-permute-start.8 = (f32[3,192]{1,0:T(4,128)S(1)}, f32[3,192]{1,0:T(4,128)S(1)}, u32[]{:S(2)}, u32[]{:S(2)}) collective-permute-start(f32[3,192]{1,0:T(4,128)S(1)} %get-tuple-element.57), channel_id=1, source_target_pairs={{0,256},{64,320},{128,384},{192,448},{256,512},{320,576},{384,640}... | collective-permute-start | bytes 6920 | tf_op jit(solution)/shard_map/softmax_stats_exchange/ppermute | solution.py:58
  139.9 4.9 %collective-permute-start.9 = (f32[3,192]{1,0:T(4,128)S(1)}, f32[3,192]{1,0:T(4,128)S(1)}, u32[]{:S(2)}, u32[]{:S(2)}) collective-permute-start(f32[3,192]{1,0:T(4,128)S(1)} %get-tuple-element.57), channel_id=1, source_target_pairs={{0,512},{64,576},{128,640},{192,704},{256,0},{320,64},{384,128},{4... | collective-permute-start | bytes 6920 | tf_op jit(solution)/shard_map/softmax_stats_exchange/ppermute | solution.py:58
  144.8 4.5 %collective-permute-done.9 = f32[3,192]{1,0:T(4,128)S(1)} collective-permute-done((f32[3,192]{1,0:T(4,128)S(1)}, f32[3,192]{1,0:T(4,128)S(1)}, u32[]{:S(2)}, u32[]{:S(2)}) %collective-permute-start.9) | collective-permute-done | bytes 2336 | tf_op jit(solution)/shard_map/softmax_stats_exchange/ppermute | solution.py:58
  152.3 4.4 %copy.23 = f32[12,16,64,128]{3,1,2,0:T(8,128)S(1)} copy(f32[12,16,64,128]{3,2,1,0:T(8,128)S(1)} %bitcast.78) | data formatting | bytes 12582912 | tf_op jit(solution)/shard_map/reshape | solution.py:127
  162.2 5.9 %collective-permute-done.10 = f32[3,2,2,2,2,2,2,2,16,128]{9,8,7,6,5,4,3,2,1,0:T(8,128)} collective-permute-done((f32[3,2,2,2,2,2,2,2,16,128]{9,8,7,6,5,4,3,2,1,0:T(8,128)}, f32[3,2,2,2,2,2,2,2,16,128]{9,8,7,6,5,4,3,2,1,0:T(8,128)}, u32[]{:S(2)}, u32[]{:S(2)}) %collective-permute-start.10) | collective-permute-done | bytes 3145760 | tf_op jit(solution)/shard_map/grad_rows_reduce_scatter/ppermute | solution.py:80
  168.1 4.0 %bitcast_add_fusion = f32[3,2,2,2,2,2,2,2,16,128]{9,8,7,6,5,4,3,2,1,0:T(8,128)S(1)} fusion(f32[3,2,2,2,2,2,2,2,16,128]{9,8,7,6,5,4,3,2,1,0:T(8,128)} %collective-permute-done.10, f32[3,2,2,2,2,2,2,2,2,16,128]{10,9,8,7,6,5,4,3,2,1,0:T(8,128)} %bitcast.77, s32[]{:T(128)S(6)} %select_n.254), kind=kLoop, calls=%fused_computation.2 | loop fusion | flops 786432 | bytes 9437188 | tf_op jit(solution)/shard_map/grad_rows_reduce_scatter/add | solution.py:80
  175.1 3.4 %collective-permute-start.11 = (f32[3,2,2,2,2,2,2,16,128]{8,7,6,5,4,3,2,1,0:T(8,128)}, f32[3,2,2,2,2,2,2,16,128]{8,7,6,5,4,3,2,1,0:T(8,128)}, u32[]{:S(2)}, u32[]{:S(2)}) collective-permute-start(f32[3,2,2,2,2,2,2,16,128]{8,7,6,5,4,3,2,1,0:T(8,128)} %dynamic-slice_bitcast_fusion.1), channel_id=1, source_target_pairs={{0,2},{1,3},{2,0},{3,1},{4,6},{5,7},{6,4},{7,5},{8,10},{9,11},{10,... | collective-permute-start | bytes 4718600 | tf_op jit(solution)/shard_map/grad_rows_reduce_scatter/ppermute | solution.py:80
  178.5 35.2 %collective-permute-done.11 = f32[3,2,2,2,2,2,2,16,128]{8,7,6,5,4,3,2,1,0:T(8,128)} collective-permute-done((f32[3,2,2,2,2,2,2,16,128]{8,7,6,5,4,3,2,1,0:T(8,128)}, f32[3,2,2,2,2,2,2,16,128]{8,7,6,5,4,3,2,1,0:T(8,128)}, u32[]{:S(2)}, u32[]{:S(2)}) %collective-permute-start.11) | collective-permute-done | bytes 1572896 | tf_op jit(solution)/shard_map/grad_rows_reduce_scatter/ppermute | solution.py:80
  217.1 2.9 collective-permute-start.12
  220.0 17.8 %collective-permute-done.12 = f32[3,2,2,2,2,2,16,128]{7,6,5,4,3,1,0,2:T(8,128)} collective-permute-done((f32[3,2,2,2,2,2,16,128]{7,6,5,4,3,1,0,2:T(8,128)S(1)}, f32[3,2,2,2,2,2,16,128]{7,6,5,4,3,1,0,2:T(8,128)}, u32[]{:S(2)}, u32[]{:S(2)}) %collective-permute-start.12) | collective-permute-done | bytes 786464 | tf_op jit(solution)/shard_map/grad_rows_reduce_scatter/ppermute | solution.py:80
  241.6 9.2 %collective-permute-done.13 = f32[3,2,2,2,2,16,128]{6,5,4,3,2,1,0:T(8,128)} collective-permute-done((f32[3,2,2,2,2,16,128]{6,5,4,3,2,1,0:T(8,128)S(1)}, f32[3,2,2,2,2,16,128]{6,5,4,3,2,1,0:T(8,128)}, u32[]{:S(2)}, u32[]{:S(2)}) %collective-permute-start.13) | collective-permute-done | bytes 393248 | tf_op jit(solution)/shard_map/grad_rows_reduce_scatter/ppermute | solution.py:80
  251.9 4.3 %collective-permute-start.14 = (f32[3,2,2,2,16,128]{5,4,3,2,1,0:T(8,128)S(1)}, f32[3,2,2,2,16,128]{5,4,3,2,1,0:T(8,128)S(1)}, u32[]{:S(2)}, u32[]{:S(2)}) collective-permute-start(f32[3,2,2,2,16,128]{5,4,3,2,1,0:T(8,128)S(1)} %dynamic-slice_bitcast_fusion.3), channel_id=1, source_target_pairs={{0,4},{1,5},{2,6},{3,7},{4,0},{5,1},{6,2},{7,3},{8,12},{9,13},{10,... | collective-permute-start | bytes 589832 | tf_op jit(solution)/shard_map/grad_rows_reduce_scatter/ppermute | solution.py:80
  256.2 6.9 %collective-permute-done.14 = f32[3,2,2,2,16,128]{5,4,3,2,1,0:T(8,128)S(1)} collective-permute-done((f32[3,2,2,2,16,128]{5,4,3,2,1,0:T(8,128)S(1)}, f32[3,2,2,2,16,128]{5,4,3,2,1,0:T(8,128)S(1)}, u32[]{:S(2)}, u32[]{:S(2)}) %collective-permute-start.14) | collective-permute-done | bytes 196640 | tf_op jit(solution)/shard_map/grad_rows_reduce_scatter/ppermute | solution.py:80
  263.2 3.4 %collective-permute-start.15 = (f32[3,2,2,16,128]{4,3,2,0,1:T(8,128)S(1)}, f32[3,2,2,16,128]{4,3,2,0,1:T(8,128)S(1)}, u32[]{:S(2)}, u32[]{:S(2)}) collective-permute-start(f32[3,2,2,16,128]{4,3,2,0,1:T(8,128)S(1)} %bitcast.80), channel_id=1, source_target_pairs={{0,32},{1,33},{2,34},{3,35},{4,36},{5,37},{6,38},{7,39},{8,40},{9,... | collective-permute-start | bytes 294920 | tf_op jit(solution)/shard_map/grad_rows_reduce_scatter/ppermute | solution.py:80
  266.6 4.6 %collective-permute-done.15 = f32[3,2,2,16,128]{4,3,2,0,1:T(8,128)S(1)} collective-permute-done((f32[3,2,2,16,128]{4,3,2,0,1:T(8,128)S(1)}, f32[3,2,2,16,128]{4,3,2,0,1:T(8,128)S(1)}, u32[]{:S(2)}, u32[]{:S(2)}) %collective-permute-start.15) | collective-permute-done | bytes 98336 | tf_op jit(solution)/shard_map/grad_rows_reduce_scatter/ppermute | solution.py:80
  271.3 3.3 %collective-permute-start.16 = (f32[3,2,16,128]{3,2,1,0:T(8,128)S(1)}, f32[3,2,16,128]{3,2,1,0:T(8,128)S(1)}, u32[]{:S(2)}, u32[]{:S(2)}) collective-permute-start(f32[3,2,16,128]{3,2,1,0:T(8,128)S(1)} %dynamic-slice_bitcast_fusion.4), channel_id=1, source_target_pairs={{0,128},{64,192},{128,0},{192,64},{256,384},{320,448},{384,256},{4... | collective-permute-start | bytes 147464 | tf_op jit(solution)/shard_map/grad_rows_reduce_scatter/ppermute | solution.py:80
  278.5 7.4 %collective-permute-start.17 = (f32[3,16,128]{2,1,0:T(8,128)S(1)}, f32[3,16,128]{2,1,0:T(8,128)S(1)}, u32[]{:S(2)}, u32[]{:S(2)}) collective-permute-start(f32[3,16,128]{2,1,0:T(8,128)S(1)} %dynamic-slice_bitcast_fusion.5), channel_id=1, source_target_pairs={{0,8},{1,9},{2,10},{3,11},{4,12},{5,13},{6,14},{7,15},{8,0},{9,1},... | collective-permute-start | bytes 73736 | tf_op jit(solution)/shard_map/grad_rows_reduce_scatter/ppermute | solution.py:80
  285.9 4.6 %convolution_convert_fusion = bf16[8192,128]{1,0:T(8,128)(2,1)} fusion(bf16[192,8192]{1,0:T(8,128)(2,1)} %all-gather.2.cloned.1.call-done, f32[192,128]{1,0:T(8,128)S(1)} %get-tuple-element.59, f32[192]{0:T(256)S(1)} %fusion.15, f32[192]{0:T(256)S(1)} %get-tuple-element.6), kind=kOutput, calls=%fused_computation.1 | convolution fusion | flops 403775488 | bytes 5342720 | tf_op jit(solution)/shard_map/dot_general | solution.py:121
  290.5 4.5 %collective-permute-start.18 = (f32[16,128]{1,0:T(8,128)S(1)}, f32[16,128]{1,0:T(8,128)S(1)}, u32[]{:S(2)}, u32[]{:S(2)}) collective-permute-start(f32[16,128]{1,0:T(8,128)S(1)} %get-tuple-element.28), channel_id=1, source_target_pairs={{0,256},{64,320},{128,384},{192,448},{256,512},{320,576},{384,640}... | collective-permute-start | bytes 24584 | tf_op jit(solution)/shard_map/grad_rows_reduce_scatter/ppermute | solution.py:87
  295.0 5.2 %collective-permute-start.19 = (f32[16,128]{1,0:T(8,128)S(1)}, f32[16,128]{1,0:T(8,128)S(1)}, u32[]{:S(2)}, u32[]{:S(2)}) collective-permute-start(f32[16,128]{1,0:T(8,128)S(1)} %get-tuple-element.29), channel_id=1, source_target_pairs={{0,512},{64,576},{128,640},{192,704},{256,0},{320,64},{384,128},{4... | collective-permute-start | bytes 24584 | tf_op jit(solution)/shard_map/grad_rows_reduce_scatter/ppermute | solution.py:87
  300.9 3.6 %collective-permute-done.19 = f32[16,128]{1,0:T(8,128)S(1)} collective-permute-done((f32[16,128]{1,0:T(8,128)S(1)}, f32[16,128]{1,0:T(8,128)S(1)}, u32[]{:S(2)}, u32[]{:S(2)}) %collective-permute-start.19) | collective-permute-done | bytes 8224 | tf_op jit(solution)/shard_map/grad_rows_reduce_scatter/ppermute | solution.py:87
  (85 shorter events, 43.0 us)
Async XLA Ops:
  7.2 75.4 %copy-start = (bf16[8192,128]{1,0:T(8,128)(2,1)S(1)}, bf16[8192,128]{1,0:T(8,128)(2,1)}, u32[]{:S(2)}) copy-start(bf16[8192,128]{1,0:T(8,128)(2,1)} %param.7) | copy-start | bytes 6291460
  7.2 75.4 %all-gather.2.cloned.1.call-start = ((), (), s32[]{:S(2)}) async-start(), calls=%async_computation | async-start | bytes 3407872 | tf_op jit(solution)/shard_map/all_gather | solution.py:104
  11.1 74.5 %copy-start.3 = (s32[192]{0:T(256)S(1)}, s32[192]{0:T(256)}, u32[]{:S(2)}) copy-start(s32[192]{0:T(256)} %param.6) | copy-start | bytes 2308
  85.8 3.1 collective-permute-start
  88.9 5.5 %collective-permute-start.1 = (f32[3,192]{1,0:T(4,128)S(1)}, f32[3,192]{1,0:T(4,128)S(1)}, u32[]{:S(2)}, u32[]{:S(2)}) collective-permute-start(f32[3,192]{1,0:T(4,128)S(1)} %pad_maximum_fusion.2), channel_id=1, source_target_pairs={{0,2},{1,3},{2,0},{3,1},{4,6},{5,7},{6,4},{7,5},{8,10},{9,11},{10,... | collective-permute-start | bytes 6920 | tf_op jit(solution)/shard_map/softmax_stats_exchange/ppermute | solution.py:48
  94.5 5.5 %collective-permute-start.2 = (f32[3,192]{1,0:T(4,128)S(1)}, f32[3,192]{1,0:T(4,128)S(1)}, u32[]{:S(2)}, u32[]{:S(2)}) collective-permute-start(f32[3,192]{1,0:T(4,128)S(1)} %pad_maximum_fusion.3), channel_id=1, source_target_pairs={{0,16},{1,17},{2,18},{3,19},{4,20},{5,21},{6,22},{7,23},{8,24},{9,... | collective-permute-start | bytes 6920 | tf_op jit(solution)/shard_map/softmax_stats_exchange/ppermute | solution.py:48
  100.1 6.4 %collective-permute-start.3 = (f32[3,192]{1,0:T(4,128)S(1)}, f32[3,192]{1,0:T(4,128)S(1)}, u32[]{:S(2)}, u32[]{:S(2)}) collective-permute-start(f32[3,192]{1,0:T(4,128)S(1)} %pad_maximum_fusion.4), channel_id=1, source_target_pairs={{0,4},{1,5},{2,6},{3,7},{4,0},{5,1},{6,2},{7,3},{8,12},{9,13},{10,... | collective-permute-start | bytes 6920 | tf_op jit(solution)/shard_map/softmax_stats_exchange/ppermute | solution.py:48
  106.5 7.0 %collective-permute-start.4 = (f32[3,192]{1,0:T(4,128)S(1)}, f32[3,192]{1,0:T(4,128)S(1)}, u32[]{:S(2)}, u32[]{:S(2)}) collective-permute-start(f32[3,192]{1,0:T(4,128)S(1)} %pad_maximum_fusion.5), channel_id=1, source_target_pairs={{0,32},{1,33},{2,34},{3,35},{4,36},{5,37},{6,38},{7,39},{8,40},{9,... | collective-permute-start | bytes 6920 | tf_op jit(solution)/shard_map/softmax_stats_exchange/ppermute | solution.py:48
  113.6 9.4 %collective-permute-start.5 = (f32[3,192]{1,0:T(4,128)S(1)}, f32[3,192]{1,0:T(4,128)S(1)}, u32[]{:S(2)}, u32[]{:S(2)}) collective-permute-start(f32[3,192]{1,0:T(4,128)S(1)} %pad_maximum_fusion.6), channel_id=1, source_target_pairs={{0,8},{1,9},{2,10},{3,11},{4,12},{5,13},{6,14},{7,15},{8,0},{9,1},... | collective-permute-start | bytes 6920 | tf_op jit(solution)/shard_map/softmax_stats_exchange/ppermute | solution.py:48
  123.0 5.5 %collective-permute-start.6 = (f32[3,192]{1,0:T(4,128)S(1)}, f32[3,192]{1,0:T(4,128)S(1)}, u32[]{:S(2)}, u32[]{:S(2)}) collective-permute-start(f32[3,192]{1,0:T(4,128)S(1)} %pad_maximum_fusion.7), channel_id=1, source_target_pairs={{0,64},{64,0},{128,192},{192,128},{256,320},{320,256},{384,448},{4... | collective-permute-start | bytes 6920 | tf_op jit(solution)/shard_map/softmax_stats_exchange/ppermute | solution.py:48
  128.6 6.4 %collective-permute-start.7 = (f32[3,192]{1,0:T(4,128)S(1)}, f32[3,192]{1,0:T(4,128)S(1)}, u32[]{:S(2)}, u32[]{:S(2)}) collective-permute-start(f32[3,192]{1,0:T(4,128)S(1)} %pad_maximum_fusion.8), channel_id=1, source_target_pairs={{0,128},{64,192},{128,0},{192,64},{256,384},{320,448},{384,256},{4... | collective-permute-start | bytes 6920 | tf_op jit(solution)/shard_map/softmax_stats_exchange/ppermute | solution.py:48
  135.0 9.8 %collective-permute-start.8 = (f32[3,192]{1,0:T(4,128)S(1)}, f32[3,192]{1,0:T(4,128)S(1)}, u32[]{:S(2)}, u32[]{:S(2)}) collective-permute-start(f32[3,192]{1,0:T(4,128)S(1)} %get-tuple-element.57), channel_id=1, source_target_pairs={{0,256},{64,320},{128,384},{192,448},{256,512},{320,576},{384,640}... | collective-permute-start | bytes 6920 | tf_op jit(solution)/shard_map/softmax_stats_exchange/ppermute | solution.py:58
  139.9 9.4 %collective-permute-start.9 = (f32[3,192]{1,0:T(4,128)S(1)}, f32[3,192]{1,0:T(4,128)S(1)}, u32[]{:S(2)}, u32[]{:S(2)}) collective-permute-start(f32[3,192]{1,0:T(4,128)S(1)} %get-tuple-element.57), channel_id=1, source_target_pairs={{0,512},{64,576},{128,640},{192,704},{256,0},{320,64},{384,128},{4... | collective-permute-start | bytes 6920 | tf_op jit(solution)/shard_map/softmax_stats_exchange/ppermute | solution.py:58
  156.7 3.6 %copy-start.1 = (f32[12,16,64,128]{3,1,2,0:T(8,128)}, f32[12,16,64,128]{3,1,2,0:T(8,128)S(1)}, u32[]{:S(2)}) copy-start(f32[12,16,64,128]{3,1,2,0:T(8,128)S(1)} %copy.23) | copy-start | bytes 18874372
  160.3 7.9 %collective-permute-start.10 = (f32[3,2,2,2,2,2,2,2,16,128]{9,8,7,6,5,4,3,2,1,0:T(8,128)}, f32[3,2,2,2,2,2,2,2,16,128]{9,8,7,6,5,4,3,2,1,0:T(8,128)}, u32[]{:S(2)}, u32[]{:S(2)}) collective-permute-start(f32[3,2,2,2,2,2,2,2,16,128]{9,8,7,6,5,4,3,2,1,0:T(8,128)} %dynamic-slice_bitcast_fusion), channel_id=1, source_target_pairs={{0,1},{1,0},{2,3},{3,2},{4,5},{5,4},{6,7},{7,6},{8,9},{9,8},{10,11... | collective-permute-start | bytes 9437192 | tf_op jit(solution)/shard_map/grad_rows_reduce_scatter/ppermute | solution.py:80
  172.1 1.6 copy-start.2
  175.1 38.6 %collective-permute-start.11 = (f32[3,2,2,2,2,2,2,16,128]{8,7,6,5,4,3,2,1,0:T(8,128)}, f32[3,2,2,2,2,2,2,16,128]{8,7,6,5,4,3,2,1,0:T(8,128)}, u32[]{:S(2)}, u32[]{:S(2)}) collective-permute-start(f32[3,2,2,2,2,2,2,16,128]{8,7,6,5,4,3,2,1,0:T(8,128)} %dynamic-slice_bitcast_fusion.1), channel_id=1, source_target_pairs={{0,2},{1,3},{2,0},{3,1},{4,6},{5,7},{6,4},{7,5},{8,10},{9,11},{10,... | collective-permute-start | bytes 4718600 | tf_op jit(solution)/shard_map/grad_rows_reduce_scatter/ppermute | solution.py:80
  217.1 20.8 %collective-permute-start.12 = (f32[3,2,2,2,2,2,16,128]{7,6,5,4,3,1,0,2:T(8,128)S(1)}, f32[3,2,2,2,2,2,16,128]{7,6,5,4,3,1,0,2:T(8,128)}, u32[]{:S(2)}, u32[]{:S(2)}) collective-permute-start(f32[3,2,2,2,2,2,16,128]{7,6,5,4,3,1,0,2:T(8,128)S(1)} %bitcast.79), channel_id=1, source_target_pairs={{0,16},{1,17},{2,18},{3,19},{4,20},{5,21},{6,22},{7,23},{8,24},{9,... | collective-permute-start | bytes 2359304 | tf_op jit(solution)/shard_map/grad_rows_reduce_scatter/ppermute | solution.py:80
  239.4 11.4 %collective-permute-start.13 = (f32[3,2,2,2,2,16,128]{6,5,4,3,2,1,0:T(8,128)S(1)}, f32[3,2,2,2,2,16,128]{6,5,4,3,2,1,0:T(8,128)}, u32[]{:S(2)}, u32[]{:S(2)}) collective-permute-start(f32[3,2,2,2,2,16,128]{6,5,4,3,2,1,0:T(8,128)S(1)} %dynamic-slice_bitcast_fusion.2), channel_id=1, source_target_pairs={{0,64},{64,0},{128,192},{192,128},{256,320},{320,256},{384,448},{4... | collective-permute-start | bytes 1179656 | tf_op jit(solution)/shard_map/grad_rows_reduce_scatter/ppermute | solution.py:80
  251.9 11.3 %collective-permute-start.14 = (f32[3,2,2,2,16,128]{5,4,3,2,1,0:T(8,128)S(1)}, f32[3,2,2,2,16,128]{5,4,3,2,1,0:T(8,128)S(1)}, u32[]{:S(2)}, u32[]{:S(2)}) collective-permute-start(f32[3,2,2,2,16,128]{5,4,3,2,1,0:T(8,128)S(1)} %dynamic-slice_bitcast_fusion.3), channel_id=1, source_target_pairs={{0,4},{1,5},{2,6},{3,7},{4,0},{5,1},{6,2},{7,3},{8,12},{9,13},{10,... | collective-permute-start | bytes 589832 | tf_op jit(solution)/shard_map/grad_rows_reduce_scatter/ppermute | solution.py:80
  263.2 8.0 %collective-permute-start.15 = (f32[3,2,2,16,128]{4,3,2,0,1:T(8,128)S(1)}, f32[3,2,2,16,128]{4,3,2,0,1:T(8,128)S(1)}, u32[]{:S(2)}, u32[]{:S(2)}) collective-permute-start(f32[3,2,2,16,128]{4,3,2,0,1:T(8,128)S(1)} %bitcast.80), channel_id=1, source_target_pairs={{0,32},{1,33},{2,34},{3,35},{4,36},{5,37},{6,38},{7,39},{8,40},{9,... | collective-permute-start | bytes 294920 | tf_op jit(solution)/shard_map/grad_rows_reduce_scatter/ppermute | solution.py:80
  271.3 7.2 %collective-permute-start.16 = (f32[3,2,16,128]{3,2,1,0:T(8,128)S(1)}, f32[3,2,16,128]{3,2,1,0:T(8,128)S(1)}, u32[]{:S(2)}, u32[]{:S(2)}) collective-permute-start(f32[3,2,16,128]{3,2,1,0:T(8,128)S(1)} %dynamic-slice_bitcast_fusion.4), channel_id=1, source_target_pairs={{0,128},{64,192},{128,0},{192,64},{256,384},{320,448},{384,256},{4... | collective-permute-start | bytes 147464 | tf_op jit(solution)/shard_map/grad_rows_reduce_scatter/ppermute | solution.py:80
  278.5 12.0 %collective-permute-start.17 = (f32[3,16,128]{2,1,0:T(8,128)S(1)}, f32[3,16,128]{2,1,0:T(8,128)S(1)}, u32[]{:S(2)}, u32[]{:S(2)}) collective-permute-start(f32[3,16,128]{2,1,0:T(8,128)S(1)} %dynamic-slice_bitcast_fusion.5), channel_id=1, source_target_pairs={{0,8},{1,9},{2,10},{3,11},{4,12},{5,13},{6,14},{7,15},{8,0},{9,1},... | collective-permute-start | bytes 73736 | tf_op jit(solution)/shard_map/grad_rows_reduce_scatter/ppermute | solution.py:80
  290.5 10.3 %collective-permute-start.18 = (f32[16,128]{1,0:T(8,128)S(1)}, f32[16,128]{1,0:T(8,128)S(1)}, u32[]{:S(2)}, u32[]{:S(2)}) collective-permute-start(f32[16,128]{1,0:T(8,128)S(1)} %get-tuple-element.28), channel_id=1, source_target_pairs={{0,256},{64,320},{128,384},{192,448},{256,512},{320,576},{384,640}... | collective-permute-start | bytes 24584 | tf_op jit(solution)/shard_map/grad_rows_reduce_scatter/ppermute | solution.py:87
  295.0 9.5 %collective-permute-start.19 = (f32[16,128]{1,0:T(8,128)S(1)}, f32[16,128]{1,0:T(8,128)S(1)}, u32[]{:S(2)}, u32[]{:S(2)}) collective-permute-start(f32[16,128]{1,0:T(8,128)S(1)} %get-tuple-element.29), channel_id=1, source_target_pairs={{0,512},{64,576},{128,640},{192,704},{256,0},{320,64},{384,128},{4... | collective-permute-start | bytes 24584 | tf_op jit(solution)/shard_map/grad_rows_reduce_scatter/ppermute | solution.py:87
Sparse Core Ops, SparseCore 0:
  11.2 71.3 all-gather.1

commit v7 on v6

--- a/solution.py
+++ b/solution.py
@@ -61,7 +61,7 @@
     return stats
 
 
-def reduce_scatter_blocks(blocks):
+def reduce_scatter_blocks(blocks, rider):
     n_sec, n_ten = blocks.shape[0], blocks.shape[1]
     low, groups = split_pow2(n_sec)
     t_bits = n_ten.bit_length() - 1
@@ -77,7 +77,10 @@
         mine = (lax.axis_index(name) & mask) // mask
         keep = lax.dynamic_index_in_dim(value, mine, axis, keepdims=False)
         sent = lax.dynamic_index_in_dim(value, 1 - mine, axis, keepdims=False)
-        value = keep + lax.ppermute(sent, name, xor_pairs(lax.axis_size(name), mask))
+        received = lax.ppermute(sent, name, xor_pairs(lax.axis_size(name), mask))
+        if (name, mask) == steps[1]:
+            keep, rider = lax.optimization_barrier((keep, rider))
+        value = keep + received
         labels.pop(axis)
     group = lax.axis_index("section") // low
     total = lax.dynamic_index_in_dim(value, group, 0, keepdims=False)
@@ -85,7 +88,7 @@
         sent = lax.dynamic_index_in_dim(value, (group + shift) % groups, 0, keepdims=False)
         pairs = [(i, (i + shift * low) % n_sec) for i in range(n_sec)]
         total = total + lax.ppermute(sent, "section", pairs)
-    return total
+    return total, rider
 
 
 def local(hidden, norm_gain, targets, out_weight):
@@ -126,7 +129,7 @@
     )
     blocks = grad_term.reshape(n_sec, rows_per_sec, n_ten, feature_width).transpose(0, 2, 1, 3)
     with jax.named_scope("grad_rows_reduce_scatter"):
-        grad_normed = reduce_scatter_blocks(blocks)
+        grad_normed, grad_weight = reduce_scatter_blocks(blocks, grad_weight)
     return (token_loss, grad_normed.astype(jnp.bfloat16), grad_weight, normed_rows)
 
 

time: 313 us -> 309 us (0.987)
  transfers between devices with their start and end apart: 21 -> 21, of which waited for: 18 -> 19; matrix products, arithmetic and copies ran while one was open for 2% -> 2% of each run, Pallas kernels for 0% -> 0%
where the time goes in v7:
time: 309 us; the launch traced here: 308 us
  waiting for transfers between devices  180 us (58%)
  starting transfers between devices  76.6 us (25%)
  between operations  14.7 us (5%)
  local copies, waits for them, and re-layouts  14.3 us (5%)
  other arithmetic  14 us (5%)
  matrix products  8.74 us (3%)
    ppermute x8, waiting for transfers between devices, reduce_scatter_blocks(): received = lax.ppermute(sent, name, xor_pairs(lax.axis_size(name), mask))  79.8 us
    all_gather x1, waiting for transfers between devices, local(): normed = lax.all_gather(normed_part, 'section', axis=0, tiled=True)  71.5 us
    ppermute x8, starting transfers between devices, reduce_scatter_blocks(): received = lax.ppermute(sent, name, xor_pairs(lax.axis_size(name), mask))  28.8 us
    ppermute x8, starting transfers between devices, exchange_stats(): other = lax.ppermute(stats, name, xor_pairs(lax.axis_size(name), mask))  28.3 us
    ppermute x8, waiting for transfers between devices, exchange_stats(): other = lax.ppermute(stats, name, xor_pairs(lax.axis_size(name), mask))  20.3 us
    ppermute x2, starting transfers between devices, exchange_stats(): received.append(lax.ppermute(stats, 'section', pairs))  9.75 us
    ppermute x2, starting transfers between devices, reduce_scatter_blocks(): total = total + lax.ppermute(sent, 'section', pairs)  9.75 us
    add x8, other arithmetic, reduce_scatter_blocks(): value = keep + received  8.33 us
  transfers between devices with their start and end apart: 21, of which 19 were waited for; matrix products, arithmetic and copies ran while one was open for 2% of the time, Pallas kernels for 0%

profile of v7, /device:TPU:6, one launch (start us, length us, event | category | flops | bytes accessed | tf_op | source)
XLA Modules:
  0.0 308.1 jit_solution(4384948021633239463)
XLA Ops:
  11.1 71.5 %all-gather.2.cloned.1.call-done = bf16[192,8192]{1,0:T(8,128)(2,1)} async-done(((bf16[16,8192]{1,0:T(8,128)(2,1)}), bf16[192,8192]{1,0:T(8,128)(2,1)}) %all-gather.2.cloned.1.call-update) | async-done | bytes 3145744 | tf_op jit(solution)/shard_map/all_gather | solution.py:107
  82.6 2.9 fusion.26
  88.9 3.4 %collective-permute-start.1 = (f32[3,192]{1,0:T(4,128)S(1)}, f32[3,192]{1,0:T(4,128)S(1)}, u32[]{:S(2)}, u32[]{:S(2)}) collective-permute-start(f32[3,192]{1,0:T(4,128)S(1)} %pad_maximum_fusion.2), channel_id=1, source_target_pairs={{0,2},{1,3},{2,0},{3,1},{4,6},{5,7},{6,4},{7,5},{8,10},{9,11},{10,... | collective-permute-start | bytes 6920 | tf_op jit(solution)/shard_map/softmax_stats_exchange/ppermute | solution.py:48
  100.0 4.3 %collective-permute-start.3 = (f32[3,192]{1,0:T(4,128)S(1)}, f32[3,192]{1,0:T(4,128)S(1)}, u32[]{:S(2)}, u32[]{:S(2)}) collective-permute-start(f32[3,192]{1,0:T(4,128)S(1)} %pad_maximum_fusion.4), channel_id=1, source_target_pairs={{0,4},{1,5},{2,6},{3,7},{4,0},{5,1},{6,2},{7,3},{8,12},{9,13},{10,... | collective-permute-start | bytes 6920 | tf_op jit(solution)/shard_map/softmax_stats_exchange/ppermute | solution.py:48
  106.5 3.4 %collective-permute-start.4 = (f32[3,192]{1,0:T(4,128)S(1)}, f32[3,192]{1,0:T(4,128)S(1)}, u32[]{:S(2)}, u32[]{:S(2)}) collective-permute-start(f32[3,192]{1,0:T(4,128)S(1)} %pad_maximum_fusion.5), channel_id=1, source_target_pairs={{0,32},{1,33},{2,34},{3,35},{4,36},{5,37},{6,38},{7,39},{8,40},{9,... | collective-permute-start | bytes 6920 | tf_op jit(solution)/shard_map/softmax_stats_exchange/ppermute | solution.py:48
  109.9 3.6 %collective-permute-done.4 = f32[3,192]{1,0:T(4,128)S(1)} collective-permute-done((f32[3,192]{1,0:T(4,128)S(1)}, f32[3,192]{1,0:T(4,128)S(1)}, u32[]{:S(2)}, u32[]{:S(2)}) %collective-permute-start.4) | collective-permute-done | bytes 2336 | tf_op jit(solution)/shard_map/softmax_stats_exchange/ppermute | solution.py:48
  113.6 7.4 %collective-permute-start.5 = (f32[3,192]{1,0:T(4,128)S(1)}, f32[3,192]{1,0:T(4,128)S(1)}, u32[]{:S(2)}, u32[]{:S(2)}) collective-permute-start(f32[3,192]{1,0:T(4,128)S(1)} %pad_maximum_fusion.6), channel_id=1, source_target_pairs={{0,8},{1,9},{2,10},{3,11},{4,12},{5,13},{6,14},{7,15},{8,0},{9,1},... | collective-permute-start | bytes 6920 | tf_op jit(solution)/shard_map/softmax_stats_exchange/ppermute | solution.py:48
  125.0 3.5 %collective-permute-done.6 = f32[3,192]{1,0:T(4,128)S(1)} collective-permute-done((f32[3,192]{1,0:T(4,128)S(1)}, f32[3,192]{1,0:T(4,128)S(1)}, u32[]{:S(2)}, u32[]{:S(2)}) %collective-permute-start.6) | collective-permute-done | bytes 2336 | tf_op jit(solution)/shard_map/softmax_stats_exchange/ppermute | solution.py:48
  128.6 3.2 %collective-permute-start.7 = (f32[3,192]{1,0:T(4,128)S(1)}, f32[3,192]{1,0:T(4,128)S(1)}, u32[]{:S(2)}, u32[]{:S(2)}) collective-permute-start(f32[3,192]{1,0:T(4,128)S(1)} %pad_maximum_fusion.8), channel_id=1, source_target_pairs={{0,128},{64,192},{128,0},{192,64},{256,384},{320,448},{384,256},{4... | collective-permute-start | bytes 6920 | tf_op jit(solution)/shard_map/softmax_stats_exchange/ppermute | solution.py:48
  131.8 3.1 %collective-permute-done.7 = f32[3,192]{1,0:T(4,128)S(1)} collective-permute-done((f32[3,192]{1,0:T(4,128)S(1)}, f32[3,192]{1,0:T(4,128)S(1)}, u32[]{:S(2)}, u32[]{:S(2)}) %collective-permute-start.7) | collective-permute-done | bytes 2336 | tf_op jit(solution)/shard_map/softmax_stats_exchange/ppermute | solution.py:48
  135.0 4.9 %collective-permute-start.8 = (f32[3,192]{1,0:T(4,128)S(1)}, f32[3,192]{1,0:T(4,128)S(1)}, u32[]{:S(2)}, u32[]{:S(2)}) collective-permute-start(f32[3,192]{1,0:T(4,128)S(1)} %get-tuple-element.63), channel_id=1, source_target_pairs={{0,256},{64,320},{128,384},{192,448},{256,512},{320,576},{384,640}... | collective-permute-start | bytes 6920 | tf_op jit(solution)/shard_map/softmax_stats_exchange/ppermute | solution.py:58
  139.9 4.9 %collective-permute-start.9 = (f32[3,192]{1,0:T(4,128)S(1)}, f32[3,192]{1,0:T(4,128)S(1)}, u32[]{:S(2)}, u32[]{:S(2)}) collective-permute-start(f32[3,192]{1,0:T(4,128)S(1)} %get-tuple-element.63), channel_id=1, source_target_pairs={{0,512},{64,576},{128,640},{192,704},{256,0},{320,64},{384,128},{4... | collective-permute-start | bytes 6920 | tf_op jit(solution)/shard_map/softmax_stats_exchange/ppermute | solution.py:58
  144.8 4.5 %collective-permute-done.9 = f32[3,192]{1,0:T(4,128)S(1)} collective-permute-done((f32[3,192]{1,0:T(4,128)S(1)}, f32[3,192]{1,0:T(4,128)S(1)}, u32[]{:S(2)}, u32[]{:S(2)}) %collective-permute-start.9) | collective-permute-done | bytes 2336 | tf_op jit(solution)/shard_map/softmax_stats_exchange/ppermute | solution.py:58
  152.3 4.4 %copy.23 = f32[12,16,64,128]{3,1,2,0:T(8,128)S(1)} copy(f32[12,16,64,128]{3,2,1,0:T(8,128)S(1)} %bitcast.78) | data formatting | bytes 12582912 | tf_op jit(solution)/shard_map/reshape | solution.py:130
  162.2 5.9 %collective-permute-done.10 = f32[3,2,2,2,2,2,2,2,16,128]{9,8,7,6,5,4,3,2,1,0:T(8,128)} collective-permute-done((f32[3,2,2,2,2,2,2,2,16,128]{9,8,7,6,5,4,3,2,1,0:T(8,128)}, f32[3,2,2,2,2,2,2,2,16,128]{9,8,7,6,5,4,3,2,1,0:T(8,128)}, u32[]{:S(2)}, u32[]{:S(2)}) %collective-permute-start.10) | collective-permute-done | bytes 3145760 | tf_op jit(solution)/shard_map/grad_rows_reduce_scatter/ppermute | solution.py:80
  168.1 4.0 %bitcast_add_fusion = f32[3,2,2,2,2,2,2,2,16,128]{9,8,7,6,5,4,3,2,1,0:T(8,128)S(1)} fusion(f32[3,2,2,2,2,2,2,2,16,128]{9,8,7,6,5,4,3,2,1,0:T(8,128)} %collective-permute-done.10, f32[3,2,2,2,2,2,2,2,2,16,128]{10,9,8,7,6,5,4,3,2,1,0:T(8,128)} %bitcast.77, s32[]{:T(128)S(6)} %select_n.254), kind=kLoop, calls=%fused_computation.2 | loop fusion | flops 786432 | bytes 9437188 | tf_op jit(solution)/shard_map/grad_rows_reduce_scatter/add | solution.py:83
  174.2 3.6 %collective-permute-start.11 = (f32[3,2,2,2,2,2,2,16,128]{8,7,6,5,4,3,2,1,0:T(8,128)}, f32[3,2,2,2,2,2,2,16,128]{8,7,6,5,4,3,2,1,0:T(8,128)}, u32[]{:S(2)}, u32[]{:S(2)}) collective-permute-start(f32[3,2,2,2,2,2,2,16,128]{8,7,6,5,4,3,2,1,0:T(8,128)} %get-tuple-element.28), channel_id=1, source_target_pairs={{0,2},{1,3},{2,0},{3,1},{4,6},{5,7},{6,4},{7,5},{8,10},{9,11},{10,... | collective-permute-start | bytes 4718600 | tf_op jit(solution)/shard_map/grad_rows_reduce_scatter/ppermute | solution.py:80
  177.8 4.7 %convolution_convert_fusion = bf16[8192,128]{1,0:T(8,128)(2,1)} fusion(bf16[192,8192]{1,0:T(8,128)(2,1)} %all-gather.2.cloned.1.call-done, f32[192,128]{1,0:T(8,128)S(1)} %get-tuple-element.65, f32[192]{0:T(256)S(1)} %fusion.15, f32[192]{0:T(256)S(1)} %get-tuple-element.10), kind=kOutput, calls=%fused_computation.1 | convolution fusion | flops 403775488 | bytes 5342720 | tf_op jit(solution)/shard_map/dot_general | solution.py:124
  182.5 30.3 %collective-permute-done.11 = f32[3,2,2,2,2,2,2,16,128]{8,7,6,5,4,3,2,1,0:T(8,128)} collective-permute-done((f32[3,2,2,2,2,2,2,16,128]{8,7,6,5,4,3,2,1,0:T(8,128)}, f32[3,2,2,2,2,2,2,16,128]{8,7,6,5,4,3,2,1,0:T(8,128)}, u32[]{:S(2)}, u32[]{:S(2)}) %collective-permute-start.11) | collective-permute-done | bytes 1572896 | tf_op jit(solution)/shard_map/grad_rows_reduce_scatter/ppermute | solution.py:80
  215.7 2.8 collective-permute-start.12
  218.5 18.0 %collective-permute-done.12 = f32[3,2,2,2,2,2,16,128]{7,6,5,4,3,1,0,2:T(8,128)} collective-permute-done((f32[3,2,2,2,2,2,16,128]{7,6,5,4,3,1,0,2:T(8,128)S(1)}, f32[3,2,2,2,2,2,16,128]{7,6,5,4,3,1,0,2:T(8,128)}, u32[]{:S(2)}, u32[]{:S(2)}) %collective-permute-start.12) | collective-permute-done | bytes 786464 | tf_op jit(solution)/shard_map/grad_rows_reduce_scatter/ppermute | solution.py:80
  240.2 9.2 %collective-permute-done.13 = f32[3,2,2,2,2,16,128]{6,5,4,3,2,1,0:T(8,128)} collective-permute-done((f32[3,2,2,2,2,16,128]{6,5,4,3,2,1,0:T(8,128)S(1)}, f32[3,2,2,2,2,16,128]{6,5,4,3,2,1,0:T(8,128)}, u32[]{:S(2)}, u32[]{:S(2)}) %collective-permute-start.13) | collective-permute-done | bytes 393248 | tf_op jit(solution)/shard_map/grad_rows_reduce_scatter/ppermute | solution.py:80
  250.5 4.3 %collective-permute-start.14 = (f32[3,2,2,2,16,128]{5,4,3,2,1,0:T(8,128)S(1)}, f32[3,2,2,2,16,128]{5,4,3,2,1,0:T(8,128)S(1)}, u32[]{:S(2)}, u32[]{:S(2)}) collective-permute-start(f32[3,2,2,2,16,128]{5,4,3,2,1,0:T(8,128)S(1)} %dynamic-slice_bitcast_fusion.4), channel_id=1, source_target_pairs={{0,4},{1,5},{2,6},{3,7},{4,0},{5,1},{6,2},{7,3},{8,12},{9,13},{10,... | collective-permute-start | bytes 589832 | tf_op jit(solution)/shard_map/grad_rows_reduce_scatter/ppermute | solution.py:80
  254.8 6.9 %collective-permute-done.14 = f32[3,2,2,2,16,128]{5,4,3,2,1,0:T(8,128)S(1)} collective-permute-done((f32[3,2,2,2,16,128]{5,4,3,2,1,0:T(8,128)S(1)}, f32[3,2,2,2,16,128]{5,4,3,2,1,0:T(8,128)S(1)}, u32[]{:S(2)}, u32[]{:S(2)}) %collective-permute-start.14) | collective-permute-done | bytes 196640 | tf_op jit(solution)/shard_map/grad_rows_reduce_scatter/ppermute | solution.py:80
  261.8 3.4 %collective-permute-start.15 = (f32[3,2,2,16,128]{4,3,2,0,1:T(8,128)S(1)}, f32[3,2,2,16,128]{4,3,2,0,1:T(8,128)S(1)}, u32[]{:S(2)}, u32[]{:S(2)}) collective-permute-start(f32[3,2,2,16,128]{4,3,2,0,1:T(8,128)S(1)} %bitcast.80), channel_id=1, source_target_pairs={{0,32},{1,33},{2,34},{3,35},{4,36},{5,37},{6,38},{7,39},{8,40},{9,... | collective-permute-start | bytes 294920 | tf_op jit(solution)/shard_map/grad_rows_reduce_scatter/ppermute | solution.py:80
  265.2 4.6 %collective-permute-done.15 = f32[3,2,2,16,128]{4,3,2,0,1:T(8,128)S(1)} collective-permute-done((f32[3,2,2,16,128]{4,3,2,0,1:T(8,128)S(1)}, f32[3,2,2,16,128]{4,3,2,0,1:T(8,128)S(1)}, u32[]{:S(2)}, u32[]{:S(2)}) %collective-permute-start.15) | collective-permute-done | bytes 98336 | tf_op jit(solution)/shard_map/grad_rows_reduce_scatter/ppermute | solution.py:80
  269.9 3.3 %collective-permute-start.16 = (f32[3,2,16,128]{3,2,1,0:T(8,128)S(1)}, f32[3,2,16,128]{3,2,1,0:T(8,128)S(1)}, u32[]{:S(2)}, u32[]{:S(2)}) collective-permute-start(f32[3,2,16,128]{3,2,1,0:T(8,128)S(1)} %dynamic-slice_bitcast_fusion.5), channel_id=1, source_target_pairs={{0,128},{64,192},{128,0},{192,64},{256,384},{320,448},{384,256},{4... | collective-permute-start | bytes 147464 | tf_op jit(solution)/shard_map/grad_rows_reduce_scatter/ppermute | solution.py:80
  273.3 3.8 %collective-permute-done.16 = f32[3,2,16,128]{3,2,1,0:T(8,128)S(1)} collective-permute-done((f32[3,2,16,128]{3,2,1,0:T(8,128)S(1)}, f32[3,2,16,128]{3,2,1,0:T(8,128)S(1)}, u32[]{:S(2)}, u32[]{:S(2)}) %collective-permute-start.16) | collective-permute-done | bytes 49184 | tf_op jit(solution)/shard_map/grad_rows_reduce_scatter/ppermute | solution.py:80
  277.1 7.4 %collective-permute-start.17 = (f32[3,16,128]{2,1,0:T(8,128)S(1)}, f32[3,16,128]{2,1,0:T(8,128)S(1)}, u32[]{:S(2)}, u32[]{:S(2)}) collective-permute-start(f32[3,16,128]{2,1,0:T(8,128)S(1)} %dynamic-slice_bitcast_fusion.6), channel_id=1, source_target_pairs={{0,8},{1,9},{2,10},{3,11},{4,12},{5,13},{6,14},{7,15},{8,0},{9,1},... | collective-permute-start | bytes 73736 | tf_op jit(solution)/shard_map/grad_rows_reduce_scatter/ppermute | solution.py:80
  286.7 4.5 %collective-permute-start.18 = (f32[16,128]{1,0:T(8,128)S(1)}, f32[16,128]{1,0:T(8,128)S(1)}, u32[]{:S(2)}, u32[]{:S(2)}) collective-permute-start(f32[16,128]{1,0:T(8,128)S(1)} %get-tuple-element.34), channel_id=1, source_target_pairs={{0,256},{64,320},{128,384},{192,448},{256,512},{320,576},{384,640}... | collective-permute-start | bytes 24584 | tf_op jit(solution)/shard_map/grad_rows_reduce_scatter/ppermute | solution.py:90
  291.2 5.3 %collective-permute-start.19 = (f32[16,128]{1,0:T(8,128)S(1)}, f32[16,128]{1,0:T(8,128)S(1)}, u32[]{:S(2)}, u32[]{:S(2)}) collective-permute-start(f32[16,128]{1,0:T(8,128)S(1)} %get-tuple-element.35), channel_id=1, source_target_pairs={{0,512},{64,576},{128,640},{192,704},{256,0},{320,64},{384,128},{4... | collective-permute-start | bytes 24584 | tf_op jit(solution)/shard_map/grad_rows_reduce_scatter/ppermute | solution.py:90
  297.1 3.6 %collective-permute-done.19 = f32[16,128]{1,0:T(8,128)S(1)} collective-permute-done((f32[16,128]{1,0:T(8,128)S(1)}, f32[16,128]{1,0:T(8,128)S(1)}, u32[]{:S(2)}, u32[]{:S(2)}) %collective-permute-start.19) | collective-permute-done | bytes 8224 | tf_op jit(solution)/shard_map/grad_rows_reduce_scatter/ppermute | solution.py:90
  (85 shorter events, 42.8 us)
Async XLA Ops:
  7.2 75.4 %copy-start = (bf16[8192,128]{1,0:T(8,128)(2,1)S(1)}, bf16[8192,128]{1,0:T(8,128)(2,1)}, u32[]{:S(2)}) copy-start(bf16[8192,128]{1,0:T(8,128)(2,1)} %param.7) | copy-start | bytes 6291460
  7.2 75.4 %all-gather.2.cloned.1.call-start = ((), (), s32[]{:S(2)}) async-start(), calls=%async_computation | async-start | bytes 3407872 | tf_op jit(solution)/shard_map/all_gather | solution.py:107
  11.1 74.5 %copy-start.3 = (s32[192]{0:T(256)S(1)}, s32[192]{0:T(256)}, u32[]{:S(2)}) copy-start(s32[192]{0:T(256)} %param.6) | copy-start | bytes 2308
  85.8 3.1 collective-permute-start
  88.9 5.5 %collective-permute-start.1 = (f32[3,192]{1,0:T(4,128)S(1)}, f32[3,192]{1,0:T(4,128)S(1)}, u32[]{:S(2)}, u32[]{:S(2)}) collective-permute-start(f32[3,192]{1,0:T(4,128)S(1)} %pad_maximum_fusion.2), channel_id=1, source_target_pairs={{0,2},{1,3},{2,0},{3,1},{4,6},{5,7},{6,4},{7,5},{8,10},{9,11},{10,... | collective-permute-start | bytes 6920 | tf_op jit(solution)/shard_map/softmax_stats_exchange/ppermute | solution.py:48
  94.5 5.5 %collective-permute-start.2 = (f32[3,192]{1,0:T(4,128)S(1)}, f32[3,192]{1,0:T(4,128)S(1)}, u32[]{:S(2)}, u32[]{:S(2)}) collective-permute-start(f32[3,192]{1,0:T(4,128)S(1)} %pad_maximum_fusion.3), channel_id=1, source_target_pairs={{0,16},{1,17},{2,18},{3,19},{4,20},{5,21},{6,22},{7,23},{8,24},{9,... | collective-permute-start | bytes 6920 | tf_op jit(solution)/shard_map/softmax_stats_exchange/ppermute | solution.py:48
  100.0 6.4 %collective-permute-start.3 = (f32[3,192]{1,0:T(4,128)S(1)}, f32[3,192]{1,0:T(4,128)S(1)}, u32[]{:S(2)}, u32[]{:S(2)}) collective-permute-start(f32[3,192]{1,0:T(4,128)S(1)} %pad_maximum_fusion.4), channel_id=1, source_target_pairs={{0,4},{1,5},{2,6},{3,7},{4,0},{5,1},{6,2},{7,3},{8,12},{9,13},{10,... | collective-permute-start | bytes 6920 | tf_op jit(solution)/shard_map/softmax_stats_exchange/ppermute | solution.py:48
  106.5 7.0 %collective-permute-start.4 = (f32[3,192]{1,0:T(4,128)S(1)}, f32[3,192]{1,0:T(4,128)S(1)}, u32[]{:S(2)}, u32[]{:S(2)}) collective-permute-start(f32[3,192]{1,0:T(4,128)S(1)} %pad_maximum_fusion.5), channel_id=1, source_target_pairs={{0,32},{1,33},{2,34},{3,35},{4,36},{5,37},{6,38},{7,39},{8,40},{9,... | collective-permute-start | bytes 6920 | tf_op jit(solution)/shard_map/softmax_stats_exchange/ppermute | solution.py:48
  113.6 9.4 %collective-permute-start.5 = (f32[3,192]{1,0:T(4,128)S(1)}, f32[3,192]{1,0:T(4,128)S(1)}, u32[]{:S(2)}, u32[]{:S(2)}) collective-permute-start(f32[3,192]{1,0:T(4,128)S(1)} %pad_maximum_fusion.6), channel_id=1, source_target_pairs={{0,8},{1,9},{2,10},{3,11},{4,12},{5,13},{6,14},{7,15},{8,0},{9,1},... | collective-permute-start | bytes 6920 | tf_op jit(solution)/shard_map/softmax_stats_exchange/ppermute | solution.py:48
  123.0 5.5 %collective-permute-start.6 = (f32[3,192]{1,0:T(4,128)S(1)}, f32[3,192]{1,0:T(4,128)S(1)}, u32[]{:S(2)}, u32[]{:S(2)}) collective-permute-start(f32[3,192]{1,0:T(4,128)S(1)} %pad_maximum_fusion.7), channel_id=1, source_target_pairs={{0,64},{64,0},{128,192},{192,128},{256,320},{320,256},{384,448},{4... | collective-permute-start | bytes 6920 | tf_op jit(solution)/shard_map/softmax_stats_exchange/ppermute | solution.py:48
  128.6 6.4 %collective-permute-start.7 = (f32[3,192]{1,0:T(4,128)S(1)}, f32[3,192]{1,0:T(4,128)S(1)}, u32[]{:S(2)}, u32[]{:S(2)}) collective-permute-start(f32[3,192]{1,0:T(4,128)S(1)} %pad_maximum_fusion.8), channel_id=1, source_target_pairs={{0,128},{64,192},{128,0},{192,64},{256,384},{320,448},{384,256},{4... | collective-permute-start | bytes 6920 | tf_op jit(solution)/shard_map/softmax_stats_exchange/ppermute | solution.py:48
  135.0 9.8 %collective-permute-start.8 = (f32[3,192]{1,0:T(4,128)S(1)}, f32[3,192]{1,0:T(4,128)S(1)}, u32[]{:S(2)}, u32[]{:S(2)}) collective-permute-start(f32[3,192]{1,0:T(4,128)S(1)} %get-tuple-element.63), channel_id=1, source_target_pairs={{0,256},{64,320},{128,384},{192,448},{256,512},{320,576},{384,640}... | collective-permute-start | bytes 6920 | tf_op jit(solution)/shard_map/softmax_stats_exchange/ppermute | solution.py:58
  139.9 9.4 %collective-permute-start.9 = (f32[3,192]{1,0:T(4,128)S(1)}, f32[3,192]{1,0:T(4,128)S(1)}, u32[]{:S(2)}, u32[]{:S(2)}) collective-permute-start(f32[3,192]{1,0:T(4,128)S(1)} %get-tuple-element.63), channel_id=1, source_target_pairs={{0,512},{64,576},{128,640},{192,704},{256,0},{320,64},{384,128},{4... | collective-permute-start | bytes 6920 | tf_op jit(solution)/shard_map/softmax_stats_exchange/ppermute | solution.py:58
  156.7 3.6 %copy-start.1 = (f32[12,16,64,128]{3,1,2,0:T(8,128)}, f32[12,16,64,128]{3,1,2,0:T(8,128)S(1)}, u32[]{:S(2)}) copy-start(f32[12,16,64,128]{3,1,2,0:T(8,128)S(1)} %copy.23) | copy-start | bytes 18874372
  160.2 7.9 %collective-permute-start.10 = (f32[3,2,2,2,2,2,2,2,16,128]{9,8,7,6,5,4,3,2,1,0:T(8,128)}, f32[3,2,2,2,2,2,2,2,16,128]{9,8,7,6,5,4,3,2,1,0:T(8,128)}, u32[]{:S(2)}, u32[]{:S(2)}) collective-permute-start(f32[3,2,2,2,2,2,2,2,16,128]{9,8,7,6,5,4,3,2,1,0:T(8,128)} %dynamic-slice_bitcast_fusion), channel_id=1, source_target_pairs={{0,1},{1,0},{2,3},{3,2},{4,5},{5,4},{6,7},{7,6},{8,9},{9,8},{10,11... | collective-permute-start | bytes 9437192 | tf_op jit(solution)/shard_map/grad_rows_reduce_scatter/ppermute | solution.py:80
  174.2 38.6 %collective-permute-start.11 = (f32[3,2,2,2,2,2,2,16,128]{8,7,6,5,4,3,2,1,0:T(8,128)}, f32[3,2,2,2,2,2,2,16,128]{8,7,6,5,4,3,2,1,0:T(8,128)}, u32[]{:S(2)}, u32[]{:S(2)}) collective-permute-start(f32[3,2,2,2,2,2,2,16,128]{8,7,6,5,4,3,2,1,0:T(8,128)} %get-tuple-element.28), channel_id=1, source_target_pairs={{0,2},{1,3},{2,0},{3,1},{4,6},{5,7},{6,4},{7,5},{8,10},{9,11},{10,... | collective-permute-start | bytes 4718600 | tf_op jit(solution)/shard_map/grad_rows_reduce_scatter/ppermute | solution.py:80
  177.8 35.0 %copy-start.2 = (f32[3,2,2,2,2,2,2,16,128]{8,7,6,5,4,3,2,1,0:T(8,128)S(1)}, f32[3,2,2,2,2,2,2,16,128]{8,7,6,5,4,3,2,1,0:T(8,128)}, u32[]{:S(2)}) copy-start(f32[3,2,2,2,2,2,2,16,128]{8,7,6,5,4,3,2,1,0:T(8,128)} %get-tuple-element.6) | copy-start | bytes 4718596
  215.7 20.8 %collective-permute-start.12 = (f32[3,2,2,2,2,2,16,128]{7,6,5,4,3,1,0,2:T(8,128)S(1)}, f32[3,2,2,2,2,2,16,128]{7,6,5,4,3,1,0,2:T(8,128)}, u32[]{:S(2)}, u32[]{:S(2)}) collective-permute-start(f32[3,2,2,2,2,2,16,128]{7,6,5,4,3,1,0,2:T(8,128)S(1)} %bitcast.79), channel_id=1, source_target_pairs={{0,16},{1,17},{2,18},{3,19},{4,20},{5,21},{6,22},{7,23},{8,24},{9,... | collective-permute-start | bytes 2359304 | tf_op jit(solution)/shard_map/grad_rows_reduce_scatter/ppermute | solution.py:80
  238.0 11.4 %collective-permute-start.13 = (f32[3,2,2,2,2,16,128]{6,5,4,3,2,1,0:T(8,128)S(1)}, f32[3,2,2,2,2,16,128]{6,5,4,3,2,1,0:T(8,128)}, u32[]{:S(2)}, u32[]{:S(2)}) collective-permute-start(f32[3,2,2,2,2,16,128]{6,5,4,3,2,1,0:T(8,128)S(1)} %dynamic-slice_bitcast_fusion.3), channel_id=1, source_target_pairs={{0,64},{64,0},{128,192},{192,128},{256,320},{320,256},{384,448},{4... | collective-permute-start | bytes 1179656 | tf_op jit(solution)/shard_map/grad_rows_reduce_scatter/ppermute | solution.py:80
  250.5 11.3 %collective-permute-start.14 = (f32[3,2,2,2,16,128]{5,4,3,2,1,0:T(8,128)S(1)}, f32[3,2,2,2,16,128]{5,4,3,2,1,0:T(8,128)S(1)}, u32[]{:S(2)}, u32[]{:S(2)}) collective-permute-start(f32[3,2,2,2,16,128]{5,4,3,2,1,0:T(8,128)S(1)} %dynamic-slice_bitcast_fusion.4), channel_id=1, source_target_pairs={{0,4},{1,5},{2,6},{3,7},{4,0},{5,1},{6,2},{7,3},{8,12},{9,13},{10,... | collective-permute-start | bytes 589832 | tf_op jit(solution)/shard_map/grad_rows_reduce_scatter/ppermute | solution.py:80
  261.8 8.0 %collective-permute-start.15 = (f32[3,2,2,16,128]{4,3,2,0,1:T(8,128)S(1)}, f32[3,2,2,16,128]{4,3,2,0,1:T(8,128)S(1)}, u32[]{:S(2)}, u32[]{:S(2)}) collective-permute-start(f32[3,2,2,16,128]{4,3,2,0,1:T(8,128)S(1)} %bitcast.80), channel_id=1, source_target_pairs={{0,32},{1,33},{2,34},{3,35},{4,36},{5,37},{6,38},{7,39},{8,40},{9,... | collective-permute-start | bytes 294920 | tf_op jit(solution)/shard_map/grad_rows_reduce_scatter/ppermute | solution.py:80
  269.9 7.2 %collective-permute-start.16 = (f32[3,2,16,128]{3,2,1,0:T(8,128)S(1)}, f32[3,2,16,128]{3,2,1,0:T(8,128)S(1)}, u32[]{:S(2)}, u32[]{:S(2)}) collective-permute-start(f32[3,2,16,128]{3,2,1,0:T(8,128)S(1)} %dynamic-slice_bitcast_fusion.5), channel_id=1, source_target_pairs={{0,128},{64,192},{128,0},{192,64},{256,384},{320,448},{384,256},{4... | collective-permute-start | bytes 147464 | tf_op jit(solution)/shard_map/grad_rows_reduce_scatter/ppermute | solution.py:80
  277.1 9.6 %collective-permute-start.17 = (f32[3,16,128]{2,1,0:T(8,128)S(1)}, f32[3,16,128]{2,1,0:T(8,128)S(1)}, u32[]{:S(2)}, u32[]{:S(2)}) collective-permute-start(f32[3,16,128]{2,1,0:T(8,128)S(1)} %dynamic-slice_bitcast_fusion.6), channel_id=1, source_target_pairs={{0,8},{1,9},{2,10},{3,11},{4,12},{5,13},{6,14},{7,15},{8,0},{9,1},... | collective-permute-start | bytes 73736 | tf_op jit(solution)/shard_map/grad_rows_reduce_scatter/ppermute | solution.py:80
  286.7 10.3 %collective-permute-start.18 = (f32[16,128]{1,0:T(8,128)S(1)}, f32[16,128]{1,0:T(8,128)S(1)}, u32[]{:S(2)}, u32[]{:S(2)}) collective-permute-start(f32[16,128]{1,0:T(8,128)S(1)} %get-tuple-element.34), channel_id=1, source_target_pairs={{0,256},{64,320},{128,384},{192,448},{256,512},{320,576},{384,640}... | collective-permute-start | bytes 24584 | tf_op jit(solution)/shard_map/grad_rows_reduce_scatter/ppermute | solution.py:90
  291.2 9.5 %collective-permute-start.19 = (f32[16,128]{1,0:T(8,128)S(1)}, f32[16,128]{1,0:T(8,128)S(1)}, u32[]{:S(2)}, u32[]{:S(2)}) collective-permute-start(f32[16,128]{1,0:T(8,128)S(1)} %get-tuple-element.35), channel_id=1, source_target_pairs={{0,512},{64,576},{128,640},{192,704},{256,0},{320,64},{384,128},{4... | collective-permute-start | bytes 24584 | tf_op jit(solution)/shard_map/grad_rows_reduce_scatter/ppermute | solution.py:90
Sparse Core Ops, SparseCore 0:
  11.2 71.3 all-gather.1

commit v8 on v7

--- a/solution.py
+++ b/solution.py
@@ -129,7 +129,9 @@
     )
     blocks = grad_term.reshape(n_sec, rows_per_sec, n_ten, feature_width).transpose(0, 2, 1, 3)
     with jax.named_scope("grad_rows_reduce_scatter"):
-        grad_normed, grad_weight = reduce_scatter_blocks(blocks, grad_weight)
+        grad_normed, (grad_weight, normed_rows, token_loss) = reduce_scatter_blocks(
+            blocks, (grad_weight, normed_rows, token_loss)
+        )
     return (token_loss, grad_normed.astype(jnp.bfloat16), grad_weight, normed_rows)
 
 

time: 309 us -> 309 us (level)
  no operation moved by 1% of the time
where the time goes in v8:
time: 309 us; the launch traced here: 308 us
  waiting for transfers between devices  180 us (58%)
  starting transfers between devices  76.6 us (25%)
  between operations  14.8 us (5%)
  local copies, waits for them, and re-layouts  14.3 us (5%)
  other arithmetic  14 us (5%)
  matrix products  8.74 us (3%)
    ppermute x8, waiting for transfers between devices, reduce_scatter_blocks(): received = lax.ppermute(sent, name, xor_pairs(lax.axis_size(name), mask))  79.1 us
    all_gather x1, waiting for transfers between devices, local(): normed = lax.all_gather(normed_part, 'section', axis=0, tiled=True)  71.5 us
    ppermute x8, starting transfers between devices, reduce_scatter_blocks(): received = lax.ppermute(sent, name, xor_pairs(lax.axis_size(name), mask))  28.8 us
    ppermute x8, starting transfers between devices, exchange_stats(): other = lax.ppermute(stats, name, xor_pairs(lax.axis_size(name), mask))  28.3 us
    ppermute x8, waiting for transfers between devices, exchange_stats(): other = lax.ppermute(stats, name, xor_pairs(lax.axis_size(name), mask))  20.3 us
    ppermute x2, starting transfers between devices, exchange_stats(): received.append(lax.ppermute(stats, 'section', pairs))  9.75 us
    ppermute x2, starting transfers between devices, reduce_scatter_blocks(): total = total + lax.ppermute(sent, 'section', pairs)  9.75 us
    add x8, other arithmetic, reduce_scatter_blocks(): value = keep + received  8.33 us
  transfers between devices with their start and end apart: 21, of which 19 were waited for; matrix products, arithmetic and copies ran while one was open for 2% of the time, Pallas kernels for 0%

profile of v8, /device:TPU:6, one launch (start us, length us, event | category | flops | bytes accessed | tf_op | source)
XLA Modules:
  0.0 308.1 jit_solution(9499949047976292346)
XLA Ops:
  11.1 71.5 %all-gather.2.cloned.1.call-done = bf16[192,8192]{1,0:T(8,128)(2,1)} async-done(((bf16[16,8192]{1,0:T(8,128)(2,1)}), bf16[192,8192]{1,0:T(8,128)(2,1)}) %all-gather.2.cloned.1.call-update) | async-done | bytes 3145744 | tf_op jit(solution)/shard_map/all_gather | solution.py:107
  82.6 2.9 fusion.26
  88.9 3.4 %collective-permute-start.1 = (f32[3,192]{1,0:T(4,128)S(1)}, f32[3,192]{1,0:T(4,128)S(1)}, u32[]{:S(2)}, u32[]{:S(2)}) collective-permute-start(f32[3,192]{1,0:T(4,128)S(1)} %pad_maximum_fusion.2), channel_id=1, source_target_pairs={{0,2},{1,3},{2,0},{3,1},{4,6},{5,7},{6,4},{7,5},{8,10},{9,11},{10,... | collective-permute-start | bytes 6920 | tf_op jit(solution)/shard_map/softmax_stats_exchange/ppermute | solution.py:48
  94.5 2.8 collective-permute-start.2
  100.0 4.3 %collective-permute-start.3 = (f32[3,192]{1,0:T(4,128)S(1)}, f32[3,192]{1,0:T(4,128)S(1)}, u32[]{:S(2)}, u32[]{:S(2)}) collective-permute-start(f32[3,192]{1,0:T(4,128)S(1)} %pad_maximum_fusion.4), channel_id=1, source_target_pairs={{0,4},{1,5},{2,6},{3,7},{4,0},{5,1},{6,2},{7,3},{8,12},{9,13},{10,... | collective-permute-start | bytes 6920 | tf_op jit(solution)/shard_map/softmax_stats_exchange/ppermute | solution.py:48
  106.5 3.4 %collective-permute-start.4 = (f32[3,192]{1,0:T(4,128)S(1)}, f32[3,192]{1,0:T(4,128)S(1)}, u32[]{:S(2)}, u32[]{:S(2)}) collective-permute-start(f32[3,192]{1,0:T(4,128)S(1)} %pad_maximum_fusion.5), channel_id=1, source_target_pairs={{0,32},{1,33},{2,34},{3,35},{4,36},{5,37},{6,38},{7,39},{8,40},{9,... | collective-permute-start | bytes 6920 | tf_op jit(solution)/shard_map/softmax_stats_exchange/ppermute | solution.py:48
  109.9 3.6 %collective-permute-done.4 = f32[3,192]{1,0:T(4,128)S(1)} collective-permute-done((f32[3,192]{1,0:T(4,128)S(1)}, f32[3,192]{1,0:T(4,128)S(1)}, u32[]{:S(2)}, u32[]{:S(2)}) %collective-permute-start.4) | collective-permute-done | bytes 2336 | tf_op jit(solution)/shard_map/softmax_stats_exchange/ppermute | solution.py:48
  113.6 7.4 %collective-permute-start.5 = (f32[3,192]{1,0:T(4,128)S(1)}, f32[3,192]{1,0:T(4,128)S(1)}, u32[]{:S(2)}, u32[]{:S(2)}) collective-permute-start(f32[3,192]{1,0:T(4,128)S(1)} %pad_maximum_fusion.6), channel_id=1, source_target_pairs={{0,8},{1,9},{2,10},{3,11},{4,12},{5,13},{6,14},{7,15},{8,0},{9,1},... | collective-permute-start | bytes 6920 | tf_op jit(solution)/shard_map/softmax_stats_exchange/ppermute | solution.py:48
  125.0 3.5 %collective-permute-done.6 = f32[3,192]{1,0:T(4,128)S(1)} collective-permute-done((f32[3,192]{1,0:T(4,128)S(1)}, f32[3,192]{1,0:T(4,128)S(1)}, u32[]{:S(2)}, u32[]{:S(2)}) %collective-permute-start.6) | collective-permute-done | bytes 2336 | tf_op jit(solution)/shard_map/softmax_stats_exchange/ppermute | solution.py:48
  128.6 3.2 %collective-permute-start.7 = (f32[3,192]{1,0:T(4,128)S(1)}, f32[3,192]{1,0:T(4,128)S(1)}, u32[]{:S(2)}, u32[]{:S(2)}) collective-permute-start(f32[3,192]{1,0:T(4,128)S(1)} %pad_maximum_fusion.8), channel_id=1, source_target_pairs={{0,128},{64,192},{128,0},{192,64},{256,384},{320,448},{384,256},{4... | collective-permute-start | bytes 6920 | tf_op jit(solution)/shard_map/softmax_stats_exchange/ppermute | solution.py:48
  131.8 3.1 %collective-permute-done.7 = f32[3,192]{1,0:T(4,128)S(1)} collective-permute-done((f32[3,192]{1,0:T(4,128)S(1)}, f32[3,192]{1,0:T(4,128)S(1)}, u32[]{:S(2)}, u32[]{:S(2)}) %collective-permute-start.7) | collective-permute-done | bytes 2336 | tf_op jit(solution)/shard_map/softmax_stats_exchange/ppermute | solution.py:48
  135.0 4.9 %collective-permute-start.8 = (f32[3,192]{1,0:T(4,128)S(1)}, f32[3,192]{1,0:T(4,128)S(1)}, u32[]{:S(2)}, u32[]{:S(2)}) collective-permute-start(f32[3,192]{1,0:T(4,128)S(1)} %get-tuple-element.67), channel_id=1, source_target_pairs={{0,256},{64,320},{128,384},{192,448},{256,512},{320,576},{384,640}... | collective-permute-start | bytes 6920 | tf_op jit(solution)/shard_map/softmax_stats_exchange/ppermute | solution.py:58
  139.9 4.9 %collective-permute-start.9 = (f32[3,192]{1,0:T(4,128)S(1)}, f32[3,192]{1,0:T(4,128)S(1)}, u32[]{:S(2)}, u32[]{:S(2)}) collective-permute-start(f32[3,192]{1,0:T(4,128)S(1)} %get-tuple-element.67), channel_id=1, source_target_pairs={{0,512},{64,576},{128,640},{192,704},{256,0},{320,64},{384,128},{4... | collective-permute-start | bytes 6920 | tf_op jit(solution)/shard_map/softmax_stats_exchange/ppermute | solution.py:58
  144.8 4.5 %collective-permute-done.9 = f32[3,192]{1,0:T(4,128)S(1)} collective-permute-done((f32[3,192]{1,0:T(4,128)S(1)}, f32[3,192]{1,0:T(4,128)S(1)}, u32[]{:S(2)}, u32[]{:S(2)}) %collective-permute-start.9) | collective-permute-done | bytes 2336 | tf_op jit(solution)/shard_map/softmax_stats_exchange/ppermute | solution.py:58
  152.3 4.4 %copy.23 = f32[12,16,64,128]{3,1,2,0:T(8,128)S(1)} copy(f32[12,16,64,128]{3,2,1,0:T(8,128)S(1)} %bitcast.78) | data formatting | bytes 12582912 | tf_op jit(solution)/shard_map/reshape | solution.py:130
  162.2 5.9 %collective-permute-done.10 = f32[3,2,2,2,2,2,2,2,16,128]{9,8,7,6,5,4,3,2,1,0:T(8,128)} collective-permute-done((f32[3,2,2,2,2,2,2,2,16,128]{9,8,7,6,5,4,3,2,1,0:T(8,128)}, f32[3,2,2,2,2,2,2,2,16,128]{9,8,7,6,5,4,3,2,1,0:T(8,128)}, u32[]{:S(2)}, u32[]{:S(2)}) %collective-permute-start.10) | collective-permute-done | bytes 3145760 | tf_op jit(solution)/shard_map/grad_rows_reduce_scatter/ppermute | solution.py:80
  168.1 4.0 %bitcast_add_fusion = f32[3,2,2,2,2,2,2,2,16,128]{9,8,7,6,5,4,3,2,1,0:T(8,128)S(1)} fusion(f32[3,2,2,2,2,2,2,2,16,128]{9,8,7,6,5,4,3,2,1,0:T(8,128)} %collective-permute-done.10, f32[3,2,2,2,2,2,2,2,2,16,128]{10,9,8,7,6,5,4,3,2,1,0:T(8,128)} %bitcast.77, s32[]{:T(128)S(6)} %select_n.254), kind=kLoop, calls=%fused_computation.2 | loop fusion | flops 786432 | bytes 9437188 | tf_op jit(solution)/shard_map/grad_rows_reduce_scatter/add | solution.py:83
  174.2 3.6 %collective-permute-start.11 = (f32[3,2,2,2,2,2,2,16,128]{8,7,6,5,4,3,2,1,0:T(8,128)}, f32[3,2,2,2,2,2,2,16,128]{8,7,6,5,4,3,2,1,0:T(8,128)}, u32[]{:S(2)}, u32[]{:S(2)}) collective-permute-start(f32[3,2,2,2,2,2,2,16,128]{8,7,6,5,4,3,2,1,0:T(8,128)} %get-tuple-element.32), channel_id=1, source_target_pairs={{0,2},{1,3},{2,0},{3,1},{4,6},{5,7},{6,4},{7,5},{8,10},{9,11},{10,... | collective-permute-start | bytes 4718600 | tf_op jit(solution)/shard_map/grad_rows_reduce_scatter/ppermute | solution.py:80
  179.6 4.7 %convolution_convert_fusion = bf16[8192,128]{1,0:T(8,128)(2,1)} fusion(bf16[192,8192]{1,0:T(8,128)(2,1)} %all-gather.2.cloned.1.call-done, f32[192,128]{1,0:T(8,128)S(1)} %get-tuple-element.69, f32[192]{0:T(256)S(1)} %fusion.15, f32[192]{0:T(256)S(1)} %get-tuple-element.15), kind=kOutput, calls=%fused_computation.1 | convolution fusion | flops 403775488 | bytes 5342720 | tf_op jit(solution)/shard_map/dot_general | solution.py:124
  184.4 28.4 %collective-permute-done.11 = f32[3,2,2,2,2,2,2,16,128]{8,7,6,5,4,3,2,1,0:T(8,128)} collective-permute-done((f32[3,2,2,2,2,2,2,16,128]{8,7,6,5,4,3,2,1,0:T(8,128)}, f32[3,2,2,2,2,2,2,16,128]{8,7,6,5,4,3,2,1,0:T(8,128)}, u32[]{:S(2)}, u32[]{:S(2)}) %collective-permute-start.11) | collective-permute-done | bytes 1572896 | tf_op jit(solution)/shard_map/grad_rows_reduce_scatter/ppermute | solution.py:80
  218.4 18.0 %collective-permute-done.12 = f32[3,2,2,2,2,2,16,128]{7,6,5,4,3,1,0,2:T(8,128)} collective-permute-done((f32[3,2,2,2,2,2,16,128]{7,6,5,4,3,1,0,2:T(8,128)S(1)}, f32[3,2,2,2,2,2,16,128]{7,6,5,4,3,1,0,2:T(8,128)}, u32[]{:S(2)}, u32[]{:S(2)}) %collective-permute-start.12) | collective-permute-done | bytes 786464 | tf_op jit(solution)/shard_map/grad_rows_reduce_scatter/ppermute | solution.py:80
  240.2 9.2 %collective-permute-done.13 = f32[3,2,2,2,2,16,128]{6,5,4,3,2,1,0:T(8,128)} collective-permute-done((f32[3,2,2,2,2,16,128]{6,5,4,3,2,1,0:T(8,128)S(1)}, f32[3,2,2,2,2,16,128]{6,5,4,3,2,1,0:T(8,128)}, u32[]{:S(2)}, u32[]{:S(2)}) %collective-permute-start.13) | collective-permute-done | bytes 393248 | tf_op jit(solution)/shard_map/grad_rows_reduce_scatter/ppermute | solution.py:80
  250.5 4.3 %collective-permute-start.14 = (f32[3,2,2,2,16,128]{5,4,3,2,1,0:T(8,128)S(1)}, f32[3,2,2,2,16,128]{5,4,3,2,1,0:T(8,128)S(1)}, u32[]{:S(2)}, u32[]{:S(2)}) collective-permute-start(f32[3,2,2,2,16,128]{5,4,3,2,1,0:T(8,128)S(1)} %dynamic-slice_bitcast_fusion.4), channel_id=1, source_target_pairs={{0,4},{1,5},{2,6},{3,7},{4,0},{5,1},{6,2},{7,3},{8,12},{9,13},{10,... | collective-permute-start | bytes 589832 | tf_op jit(solution)/shard_map/grad_rows_reduce_scatter/ppermute | solution.py:80
  254.8 6.9 %collective-permute-done.14 = f32[3,2,2,2,16,128]{5,4,3,2,1,0:T(8,128)S(1)} collective-permute-done((f32[3,2,2,2,16,128]{5,4,3,2,1,0:T(8,128)S(1)}, f32[3,2,2,2,16,128]{5,4,3,2,1,0:T(8,128)S(1)}, u32[]{:S(2)}, u32[]{:S(2)}) %collective-permute-start.14) | collective-permute-done | bytes 196640 | tf_op jit(solution)/shard_map/grad_rows_reduce_scatter/ppermute | solution.py:80
  261.8 3.4 %collective-permute-start.15 = (f32[3,2,2,16,128]{4,3,2,0,1:T(8,128)S(1)}, f32[3,2,2,16,128]{4,3,2,0,1:T(8,128)S(1)}, u32[]{:S(2)}, u32[]{:S(2)}) collective-permute-start(f32[3,2,2,16,128]{4,3,2,0,1:T(8,128)S(1)} %bitcast.80), channel_id=1, source_target_pairs={{0,32},{1,33},{2,34},{3,35},{4,36},{5,37},{6,38},{7,39},{8,40},{9,... | collective-permute-start | bytes 294920 | tf_op jit(solution)/shard_map/grad_rows_reduce_scatter/ppermute | solution.py:80
  265.2 4.6 %collective-permute-done.15 = f32[3,2,2,16,128]{4,3,2,0,1:T(8,128)S(1)} collective-permute-done((f32[3,2,2,16,128]{4,3,2,0,1:T(8,128)S(1)}, f32[3,2,2,16,128]{4,3,2,0,1:T(8,128)S(1)}, u32[]{:S(2)}, u32[]{:S(2)}) %collective-permute-start.15) | collective-permute-done | bytes 98336 | tf_op jit(solution)/shard_map/grad_rows_reduce_scatter/ppermute | solution.py:80
  269.9 3.3 %collective-permute-start.16 = (f32[3,2,16,128]{3,2,1,0:T(8,128)S(1)}, f32[3,2,16,128]{3,2,1,0:T(8,128)S(1)}, u32[]{:S(2)}, u32[]{:S(2)}) collective-permute-start(f32[3,2,16,128]{3,2,1,0:T(8,128)S(1)} %dynamic-slice_bitcast_fusion.5), channel_id=1, source_target_pairs={{0,128},{64,192},{128,0},{192,64},{256,384},{320,448},{384,256},{4... | collective-permute-start | bytes 147464 | tf_op jit(solution)/shard_map/grad_rows_reduce_scatter/ppermute | solution.py:80
  273.3 3.8 %collective-permute-done.16 = f32[3,2,16,128]{3,2,1,0:T(8,128)S(1)} collective-permute-done((f32[3,2,16,128]{3,2,1,0:T(8,128)S(1)}, f32[3,2,16,128]{3,2,1,0:T(8,128)S(1)}, u32[]{:S(2)}, u32[]{:S(2)}) %collective-permute-start.16) | collective-permute-done | bytes 49184 | tf_op jit(solution)/shard_map/grad_rows_reduce_scatter/ppermute | solution.py:80
  277.1 7.4 %collective-permute-start.17 = (f32[3,16,128]{2,1,0:T(8,128)S(1)}, f32[3,16,128]{2,1,0:T(8,128)S(1)}, u32[]{:S(2)}, u32[]{:S(2)}) collective-permute-start(f32[3,16,128]{2,1,0:T(8,128)S(1)} %dynamic-slice_bitcast_fusion.6), channel_id=1, source_target_pairs={{0,8},{1,9},{2,10},{3,11},{4,12},{5,13},{6,14},{7,15},{8,0},{9,1},... | collective-permute-start | bytes 73736 | tf_op jit(solution)/shard_map/grad_rows_reduce_scatter/ppermute | solution.py:80
  286.7 4.5 %collective-permute-start.18 = (f32[16,128]{1,0:T(8,128)S(1)}, f32[16,128]{1,0:T(8,128)S(1)}, u32[]{:S(2)}, u32[]{:S(2)}) collective-permute-start(f32[16,128]{1,0:T(8,128)S(1)} %get-tuple-element.38), channel_id=1, source_target_pairs={{0,256},{64,320},{128,384},{192,448},{256,512},{320,576},{384,640}... | collective-permute-start | bytes 24584 | tf_op jit(solution)/shard_map/grad_rows_reduce_scatter/ppermute | solution.py:90
  291.2 5.3 %collective-permute-start.19 = (f32[16,128]{1,0:T(8,128)S(1)}, f32[16,128]{1,0:T(8,128)S(1)}, u32[]{:S(2)}, u32[]{:S(2)}) collective-permute-start(f32[16,128]{1,0:T(8,128)S(1)} %get-tuple-element.39), channel_id=1, source_target_pairs={{0,512},{64,576},{128,640},{192,704},{256,0},{320,64},{384,128},{4... | collective-permute-start | bytes 24584 | tf_op jit(solution)/shard_map/grad_rows_reduce_scatter/ppermute | solution.py:90
  296.5 4.2 %collective-permute-done.19 = f32[16,128]{1,0:T(8,128)S(1)} collective-permute-done((f32[16,128]{1,0:T(8,128)S(1)}, f32[16,128]{1,0:T(8,128)S(1)}, u32[]{:S(2)}, u32[]{:S(2)}) %collective-permute-start.19) | collective-permute-done | bytes 8224 | tf_op jit(solution)/shard_map/grad_rows_reduce_scatter/ppermute | solution.py:90
  (85 shorter events, 44.0 us)
Async XLA Ops:
  7.2 75.4 %copy-start = (bf16[8192,128]{1,0:T(8,128)(2,1)S(1)}, bf16[8192,128]{1,0:T(8,128)(2,1)}, u32[]{:S(2)}) copy-start(bf16[8192,128]{1,0:T(8,128)(2,1)} %param.7) | copy-start | bytes 6291460
  7.2 75.4 %all-gather.2.cloned.1.call-start = ((), (), s32[]{:S(2)}) async-start(), calls=%async_computation | async-start | bytes 3407872 | tf_op jit(solution)/shard_map/all_gather | solution.py:107
  11.1 74.5 %copy-start.3 = (s32[192]{0:T(256)S(1)}, s32[192]{0:T(256)}, u32[]{:S(2)}) copy-start(s32[192]{0:T(256)} %param.6) | copy-start | bytes 2308
  85.8 3.1 collective-permute-start
  88.9 5.5 %collective-permute-start.1 = (f32[3,192]{1,0:T(4,128)S(1)}, f32[3,192]{1,0:T(4,128)S(1)}, u32[]{:S(2)}, u32[]{:S(2)}) collective-permute-start(f32[3,192]{1,0:T(4,128)S(1)} %pad_maximum_fusion.2), channel_id=1, source_target_pairs={{0,2},{1,3},{2,0},{3,1},{4,6},{5,7},{6,4},{7,5},{8,10},{9,11},{10,... | collective-permute-start | bytes 6920 | tf_op jit(solution)/shard_map/softmax_stats_exchange/ppermute | solution.py:48
  94.5 5.5 %collective-permute-start.2 = (f32[3,192]{1,0:T(4,128)S(1)}, f32[3,192]{1,0:T(4,128)S(1)}, u32[]{:S(2)}, u32[]{:S(2)}) collective-permute-start(f32[3,192]{1,0:T(4,128)S(1)} %pad_maximum_fusion.3), channel_id=1, source_target_pairs={{0,16},{1,17},{2,18},{3,19},{4,20},{5,21},{6,22},{7,23},{8,24},{9,... | collective-permute-start | bytes 6920 | tf_op jit(solution)/shard_map/softmax_stats_exchange/ppermute | solution.py:48
  100.0 6.4 %collective-permute-start.3 = (f32[3,192]{1,0:T(4,128)S(1)}, f32[3,192]{1,0:T(4,128)S(1)}, u32[]{:S(2)}, u32[]{:S(2)}) collective-permute-start(f32[3,192]{1,0:T(4,128)S(1)} %pad_maximum_fusion.4), channel_id=1, source_target_pairs={{0,4},{1,5},{2,6},{3,7},{4,0},{5,1},{6,2},{7,3},{8,12},{9,13},{10,... | collective-permute-start | bytes 6920 | tf_op jit(solution)/shard_map/softmax_stats_exchange/ppermute | solution.py:48
  106.5 7.0 %collective-permute-start.4 = (f32[3,192]{1,0:T(4,128)S(1)}, f32[3,192]{1,0:T(4,128)S(1)}, u32[]{:S(2)}, u32[]{:S(2)}) collective-permute-start(f32[3,192]{1,0:T(4,128)S(1)} %pad_maximum_fusion.5), channel_id=1, source_target_pairs={{0,32},{1,33},{2,34},{3,35},{4,36},{5,37},{6,38},{7,39},{8,40},{9,... | collective-permute-start | bytes 6920 | tf_op jit(solution)/shard_map/softmax_stats_exchange/ppermute | solution.py:48
  113.6 9.4 %collective-permute-start.5 = (f32[3,192]{1,0:T(4,128)S(1)}, f32[3,192]{1,0:T(4,128)S(1)}, u32[]{:S(2)}, u32[]{:S(2)}) collective-permute-start(f32[3,192]{1,0:T(4,128)S(1)} %pad_maximum_fusion.6), channel_id=1, source_target_pairs={{0,8},{1,9},{2,10},{3,11},{4,12},{5,13},{6,14},{7,15},{8,0},{9,1},... | collective-permute-start | bytes 6920 | tf_op jit(solution)/shard_map/softmax_stats_exchange/ppermute | solution.py:48
  123.0 5.5 %collective-permute-start.6 = (f32[3,192]{1,0:T(4,128)S(1)}, f32[3,192]{1,0:T(4,128)S(1)}, u32[]{:S(2)}, u32[]{:S(2)}) collective-permute-start(f32[3,192]{1,0:T(4,128)S(1)} %pad_maximum_fusion.7), channel_id=1, source_target_pairs={{0,64},{64,0},{128,192},{192,128},{256,320},{320,256},{384,448},{4... | collective-permute-start | bytes 6920 | tf_op jit(solution)/shard_map/softmax_stats_exchange/ppermute | solution.py:48
  128.6 6.4 %collective-permute-start.7 = (f32[3,192]{1,0:T(4,128)S(1)}, f32[3,192]{1,0:T(4,128)S(1)}, u32[]{:S(2)}, u32[]{:S(2)}) collective-permute-start(f32[3,192]{1,0:T(4,128)S(1)} %pad_maximum_fusion.8), channel_id=1, source_target_pairs={{0,128},{64,192},{128,0},{192,64},{256,384},{320,448},{384,256},{4... | collective-permute-start | bytes 6920 | tf_op jit(solution)/shard_map/softmax_stats_exchange/ppermute | solution.py:48
  135.0 9.8 %collective-permute-start.8 = (f32[3,192]{1,0:T(4,128)S(1)}, f32[3,192]{1,0:T(4,128)S(1)}, u32[]{:S(2)}, u32[]{:S(2)}) collective-permute-start(f32[3,192]{1,0:T(4,128)S(1)} %get-tuple-element.67), channel_id=1, source_target_pairs={{0,256},{64,320},{128,384},{192,448},{256,512},{320,576},{384,640}... | collective-permute-start | bytes 6920 | tf_op jit(solution)/shard_map/softmax_stats_exchange/ppermute | solution.py:58
  139.9 9.4 %collective-permute-start.9 = (f32[3,192]{1,0:T(4,128)S(1)}, f32[3,192]{1,0:T(4,128)S(1)}, u32[]{:S(2)}, u32[]{:S(2)}) collective-permute-start(f32[3,192]{1,0:T(4,128)S(1)} %get-tuple-element.67), channel_id=1, source_target_pairs={{0,512},{64,576},{128,640},{192,704},{256,0},{320,64},{384,128},{4... | collective-permute-start | bytes 6920 | tf_op jit(solution)/shard_map/softmax_stats_exchange/ppermute | solution.py:58
  156.6 3.6 %copy-start.1 = (f32[12,16,64,128]{3,1,2,0:T(8,128)}, f32[12,16,64,128]{3,1,2,0:T(8,128)S(1)}, u32[]{:S(2)}) copy-start(f32[12,16,64,128]{3,1,2,0:T(8,128)S(1)} %copy.23) | copy-start | bytes 18874372
  160.2 7.9 %collective-permute-start.10 = (f32[3,2,2,2,2,2,2,2,16,128]{9,8,7,6,5,4,3,2,1,0:T(8,128)}, f32[3,2,2,2,2,2,2,2,16,128]{9,8,7,6,5,4,3,2,1,0:T(8,128)}, u32[]{:S(2)}, u32[]{:S(2)}) collective-permute-start(f32[3,2,2,2,2,2,2,2,16,128]{9,8,7,6,5,4,3,2,1,0:T(8,128)} %dynamic-slice_bitcast_fusion), channel_id=1, source_target_pairs={{0,1},{1,0},{2,3},{3,2},{4,5},{5,4},{6,7},{7,6},{8,9},{9,8},{10,11... | collective-permute-start | bytes 9437192 | tf_op jit(solution)/shard_map/grad_rows_reduce_scatter/ppermute | solution.py:80
  174.2 38.6 %collective-permute-start.11 = (f32[3,2,2,2,2,2,2,16,128]{8,7,6,5,4,3,2,1,0:T(8,128)}, f32[3,2,2,2,2,2,2,16,128]{8,7,6,5,4,3,2,1,0:T(8,128)}, u32[]{:S(2)}, u32[]{:S(2)}) collective-permute-start(f32[3,2,2,2,2,2,2,16,128]{8,7,6,5,4,3,2,1,0:T(8,128)} %get-tuple-element.32), channel_id=1, source_target_pairs={{0,2},{1,3},{2,0},{3,1},{4,6},{5,7},{6,4},{7,5},{8,10},{9,11},{10,... | collective-permute-start | bytes 4718600 | tf_op jit(solution)/shard_map/grad_rows_reduce_scatter/ppermute | solution.py:80
  179.6 33.2 %copy-start.2 = (f32[3,2,2,2,2,2,2,16,128]{8,7,6,5,4,3,2,1,0:T(8,128)S(1)}, f32[3,2,2,2,2,2,2,16,128]{8,7,6,5,4,3,2,1,0:T(8,128)}, u32[]{:S(2)}) copy-start(f32[3,2,2,2,2,2,2,16,128]{8,7,6,5,4,3,2,1,0:T(8,128)} %get-tuple-element.9) | copy-start | bytes 4718596
  215.7 20.8 %collective-permute-start.12 = (f32[3,2,2,2,2,2,16,128]{7,6,5,4,3,1,0,2:T(8,128)S(1)}, f32[3,2,2,2,2,2,16,128]{7,6,5,4,3,1,0,2:T(8,128)}, u32[]{:S(2)}, u32[]{:S(2)}) collective-permute-start(f32[3,2,2,2,2,2,16,128]{7,6,5,4,3,1,0,2:T(8,128)S(1)} %bitcast.79), channel_id=1, source_target_pairs={{0,16},{1,17},{2,18},{3,19},{4,20},{5,21},{6,22},{7,23},{8,24},{9,... | collective-permute-start | bytes 2359304 | tf_op jit(solution)/shard_map/grad_rows_reduce_scatter/ppermute | solution.py:80
  238.0 11.4 %collective-permute-start.13 = (f32[3,2,2,2,2,16,128]{6,5,4,3,2,1,0:T(8,128)S(1)}, f32[3,2,2,2,2,16,128]{6,5,4,3,2,1,0:T(8,128)}, u32[]{:S(2)}, u32[]{:S(2)}) collective-permute-start(f32[3,2,2,2,2,16,128]{6,5,4,3,2,1,0:T(8,128)S(1)} %dynamic-slice_bitcast_fusion.3), channel_id=1, source_target_pairs={{0,64},{64,0},{128,192},{192,128},{256,320},{320,256},{384,448},{4... | collective-permute-start | bytes 1179656 | tf_op jit(solution)/shard_map/grad_rows_reduce_scatter/ppermute | solution.py:80
  250.5 11.3 %collective-permute-start.14 = (f32[3,2,2,2,16,128]{5,4,3,2,1,0:T(8,128)S(1)}, f32[3,2,2,2,16,128]{5,4,3,2,1,0:T(8,128)S(1)}, u32[]{:S(2)}, u32[]{:S(2)}) collective-permute-start(f32[3,2,2,2,16,128]{5,4,3,2,1,0:T(8,128)S(1)} %dynamic-slice_bitcast_fusion.4), channel_id=1, source_target_pairs={{0,4},{1,5},{2,6},{3,7},{4,0},{5,1},{6,2},{7,3},{8,12},{9,13},{10,... | collective-permute-start | bytes 589832 | tf_op jit(solution)/shard_map/grad_rows_reduce_scatter/ppermute | solution.py:80
  261.8 8.0 %collective-permute-start.15 = (f32[3,2,2,16,128]{4,3,2,0,1:T(8,128)S(1)}, f32[3,2,2,16,128]{4,3,2,0,1:T(8,128)S(1)}, u32[]{:S(2)}, u32[]{:S(2)}) collective-permute-start(f32[3,2,2,16,128]{4,3,2,0,1:T(8,128)S(1)} %bitcast.80), channel_id=1, source_target_pairs={{0,32},{1,33},{2,34},{3,35},{4,36},{5,37},{6,38},{7,39},{8,40},{9,... | collective-permute-start | bytes 294920 | tf_op jit(solution)/shard_map/grad_rows_reduce_scatter/ppermute | solution.py:80
  269.9 7.2 %collective-permute-start.16 = (f32[3,2,16,128]{3,2,1,0:T(8,128)S(1)}, f32[3,2,16,128]{3,2,1,0:T(8,128)S(1)}, u32[]{:S(2)}, u32[]{:S(2)}) collective-permute-start(f32[3,2,16,128]{3,2,1,0:T(8,128)S(1)} %dynamic-slice_bitcast_fusion.5), channel_id=1, source_target_pairs={{0,128},{64,192},{128,0},{192,64},{256,384},{320,448},{384,256},{4... | collective-permute-start | bytes 147464 | tf_op jit(solution)/shard_map/grad_rows_reduce_scatter/ppermute | solution.py:80
  277.1 9.6 %collective-permute-start.17 = (f32[3,16,128]{2,1,0:T(8,128)S(1)}, f32[3,16,128]{2,1,0:T(8,128)S(1)}, u32[]{:S(2)}, u32[]{:S(2)}) collective-permute-start(f32[3,16,128]{2,1,0:T(8,128)S(1)} %dynamic-slice_bitcast_fusion.6), channel_id=1, source_target_pairs={{0,8},{1,9},{2,10},{3,11},{4,12},{5,13},{6,14},{7,15},{8,0},{9,1},... | collective-permute-start | bytes 73736 | tf_op jit(solution)/shard_map/grad_rows_reduce_scatter/ppermute | solution.py:80
  286.7 9.8 %collective-permute-start.18 = (f32[16,128]{1,0:T(8,128)S(1)}, f32[16,128]{1,0:T(8,128)S(1)}, u32[]{:S(2)}, u32[]{:S(2)}) collective-permute-start(f32[16,128]{1,0:T(8,128)S(1)} %get-tuple-element.38), channel_id=1, source_target_pairs={{0,256},{64,320},{128,384},{192,448},{256,512},{320,576},{384,640}... | collective-permute-start | bytes 24584 | tf_op jit(solution)/shard_map/grad_rows_reduce_scatter/ppermute | solution.py:90
  291.2 9.5 %collective-permute-start.19 = (f32[16,128]{1,0:T(8,128)S(1)}, f32[16,128]{1,0:T(8,128)S(1)}, u32[]{:S(2)}, u32[]{:S(2)}) collective-permute-start(f32[16,128]{1,0:T(8,128)S(1)} %get-tuple-element.39), channel_id=1, source_target_pairs={{0,512},{64,576},{128,640},{192,704},{256,0},{320,64},{384,128},{4... | collective-permute-start | bytes 24584 | tf_op jit(solution)/shard_map/grad_rows_reduce_scatter/ppermute | solution.py:90
Sparse Core Ops, SparseCore 0:
  11.2 71.3 all-gather.1
